TPU v7x, 32 devices: a whole 2x2x4 slice. The times are simulated.
32 devices in a mesh: face: 2 (over y), row: 4 (over z), col: 4 (over x, core).
Axes of the slice: x: 2, y: 2, z: 4, core: 2. Of those that a mesh axis runs over, the one named last changes fastest.
Arguments:
- state: bfloat16 [6, 256, 256, 256], P('face', 'row', 'col'), may hold values from -5 to 5
- offsets: int32 [64, 2], replicated, may hold values from -4 to 4, as said below
- links: int32 [6, 4, 3], replicated, may hold values from 0 to 5, as said below
- stencil: bfloat16 [64, 256], replicated, may hold values from -5 to 5
- gain: bfloat16 [256], replicated, may hold values from 0.25 to 1.75
- w_in: bfloat16 [256, 1024], replicated, may hold values from -0.375 to 0.375
- w_out: bfloat16 [1024, 256], replicated, may hold values from -0.1875 to 0.1875
- cotangent: bfloat16 [6, 256, 256, 256], P('face', 'row', 'col'), may hold values from -0.125 to 0.125
Outputs:
- increment: bfloat16 [6, 256, 256, 256], P('face', 'row', 'col')
- stencil_grad: float32 [64, 256], replicated
- gain_grad: float32 [256], replicated
- w_in_grad: float32 [256, 1024], replicated
- w_out_grad: float32 [1024, 256], replicated
Inputs may be any that keep to these rules, and one draw needn't show every extreme that they name: The 64 rows are distinct (row, column) offsets; (4, 0), (-4, 0), (0, 4) and (0, -4) are always among them. links[g, s] = (f, t, r): side s of face g (0: row 0, 1: the last row, 2: column 0, 3: the last column) meets side t of face f, and r is 1 where positions along the shared edge run in opposite directions on the two faces, else 0. The table is that of a cube whose 6 faces are each stored in one of their eight orientations: every side meets one side of another face, and the pairing is mutual.
All inputs are finite; a program needn't handle non-finite values.
Results may differ from a plain program's by a relative error of at most 0.0058.
Values may be sent and summed in bfloat16 or wider, within the bound.
No kernel may reach another device: no remote copies, remote signals or barrier semaphores. Data moves between devices by JAX's collectives and lax.ppermute only.
A program may use at most 320 MiB of HBM per device.

v0:
```python
import jax
import jax.numpy as jnp
from jax import lax
from jax.sharding import PartitionSpec as P

RADIUS = 4


def with_halo(cells, sides, width):
    for axis, dim in sides:
        count = lax.axis_size(axis)
        ends = count - 1
        head = lax.slice_in_dim(cells, 0, width, axis=dim)
        tail = lax.slice_in_dim(cells, cells.shape[dim] - width, cells.shape[dim], axis=dim)
        cells = jnp.concatenate(
            [
                lax.ppermute(tail, axis, [(i, (i + 1) % count) for i in range(ends)]),
                cells,
                lax.ppermute(head, axis, [((i + 1) % count, i) for i in range(ends)]),
            ],
            axis=dim,
        )
    return cells


def cut_segment(padded_edges, face_local, side_index, flip_flag, start_cell, length):
    padded_len = padded_edges.shape[3]
    begin_cell = jnp.where(flip_flag == 1, padded_len - start_cell - length, start_cell)
    zero_index = jnp.zeros((), jnp.int32)
    segment = lax.dynamic_slice(
        padded_edges,
        (face_local, side_index, zero_index, begin_cell, zero_index),
        (1, 1, padded_edges.shape[2], length, padded_edges.shape[4]),
    )[0, 0]
    return jnp.where(flip_flag == 1, jnp.flip(segment, axis=1), segment)


def shards(state, offsets, links, stencil, gain, w_in, w_out, cotangent):
    local_count, rows_dev, cols_dev, channels = state.shape
    row_count = lax.axis_size("row")
    col_count = lax.axis_size("col")
    face_count = lax.axis_size("face")
    face_side = rows_dev * row_count
    piece_cells = face_side // (row_count * col_count)
    row_index = lax.axis_index("row")
    col_index = lax.axis_index("col")
    face_index = lax.axis_index("face")
    radius_cells = RADIUS
    extended = with_halo(state, (("row", 1), ("col", 2)), RADIUS)
    top_strip = state[:, :radius_cells]
    bottom_strip = jnp.flip(state[:, rows_dev - radius_cells :], axis=1)
    left_strip = jnp.swapaxes(state[:, :, :radius_cells], 1, 2)
    right_strip = jnp.swapaxes(jnp.flip(state[:, :, cols_dev - radius_cells :], axis=2), 1, 2)
    across = jnp.where(row_index == 0, top_strip, bottom_strip)
    downward = jnp.where(col_index == 0, left_strip, right_strip)
    across_pieces = jnp.moveaxis(
        across.reshape(local_count, radius_cells, row_count, piece_cells, channels), 2, 0
    )
    down_pieces = jnp.moveaxis(
        downward.reshape(local_count, radius_cells, col_count, piece_cells, channels), 2, 0
    )
    empty_slots = jnp.zeros(
        (row_count * col_count, local_count, radius_cells, piece_cells, channels), state.dtype
    )
    across_slots = lax.dynamic_update_slice_in_dim(
        empty_slots, across_pieces, col_index * row_count, 0
    )
    down_slots = lax.dynamic_update_slice_in_dim(empty_slots, down_pieces, row_index * col_count, 0)
    outgoing = jnp.stack([across_slots, down_slots], axis=2).reshape(
        row_count, col_count, local_count, 2, radius_cells, piece_cells, channels
    )
    arrived = lax.all_to_all(
        lax.all_to_all(outgoing, "row", split_axis=0, concat_axis=0, tiled=True),
        "col",
        split_axis=1,
        concat_axis=1,
        tiled=True,
    )
    own_pieces = jnp.stack(
        [
            jnp.sum(arrived[0, :, :, 0], axis=0),
            jnp.sum(arrived[row_count - 1, :, :, 0], axis=0),
            jnp.sum(arrived[:, 0, :, 1], axis=0),
            jnp.sum(arrived[:, col_count - 1, :, 1], axis=0),
        ],
        axis=1,
    )
    across_side = jnp.where(row_index == 0, 0, 1).astype(jnp.int32)
    down_side = jnp.where(col_index == 0, 2, 3).astype(jnp.int32)
    across_len = cols_dev + 2 * radius_cells
    down_len = rows_dev + 2 * radius_cells
    edge_pad = ((0, 0), (0, 0), (0, 0), (radius_cells, radius_cells), (0, 0))
    side_edges = lax.all_gather(own_pieces, ("row", "col"), axis=3, tiled=True)
    padded_edges = jnp.pad(side_edges, edge_pad)
    across_list = []
    down_list = []
    for dest_face in range(local_count * face_count):
        link_across = lax.dynamic_index_in_dim(links[dest_face], across_side, 0, keepdims=False)
        link_down = lax.dynamic_index_in_dim(links[dest_face], down_side, 0, keepdims=False)
        segment_across = cut_segment(
            padded_edges,
            link_across[0] % local_count,
            link_across[1],
            link_across[2],
            col_index * cols_dev,
            across_len,
        )
        segment_down = cut_segment(
            padded_edges,
            link_down[0] % local_count,
            link_down[1],
            link_down[2],
            row_index * rows_dev,
            down_len,
        )
        across_list.append(
            jnp.where(
                link_across[0] // local_count == face_index,
                segment_across,
                jnp.zeros_like(segment_across),
            )
        )
        down_list.append(
            jnp.where(
                link_down[0] // local_count == face_index,
                segment_down,
                jnp.zeros_like(segment_down),
            )
        )
    got_across, got_down = (
        lax.all_to_all(jnp.stack(across_list), "face", split_axis=0, concat_axis=0, tiled=True),
        lax.all_to_all(jnp.stack(down_list), "face", split_axis=0, concat_axis=0, tiled=True),
    )
    halo_across = jnp.sum(
        got_across.reshape(face_count, local_count, radius_cells, across_len, channels), axis=0
    )
    halo_down = jnp.sum(
        got_down.reshape(face_count, local_count, radius_cells, down_len, channels), axis=0
    )
    top_part = jnp.where(row_index == 0, jnp.flip(halo_across, axis=1), jnp.zeros_like(halo_across))
    bottom_part = jnp.where(row_index == row_count - 1, halo_across, jnp.zeros_like(halo_across))
    left_block = jnp.swapaxes(jnp.flip(halo_down, axis=1), 1, 2)
    right_block = jnp.swapaxes(halo_down, 1, 2)
    left_part = jnp.where(col_index == 0, left_block, jnp.zeros_like(left_block))
    right_part = jnp.where(col_index == col_count - 1, right_block, jnp.zeros_like(right_block))
    extended = extended.at[:, :radius_cells].add(top_part)
    extended = extended.at[:, radius_cells + rows_dev :].add(bottom_part)
    extended = extended.at[:, :, :radius_cells].add(left_part)
    extended = extended.at[:, :, radius_cells + cols_dev :].add(right_part)
    box_side = 2 * radius_cells + 1
    box_index = (offsets[:, 0] + radius_cells) * box_side + offsets[:, 1] + radius_cells
    onehot = (
        box_index[:, None] == jnp.arange(box_side * box_side, dtype=jnp.int32)[None, :]
    ).astype(jnp.float32)
    box_weights = jnp.dot(onehot.T, stencil.astype(jnp.float32), precision=lax.Precision.HIGHEST)
    aggregated = jnp.zeros((local_count, rows_dev, cols_dev, channels), jnp.float32)
    for row_shift in range(box_side):
        for col_shift in range(box_side):
            window = extended[
                :, row_shift : row_shift + rows_dev, col_shift : col_shift + cols_dev
            ].astype(jnp.float32)
            aggregated = aggregated + box_weights[row_shift * box_side + col_shift] * window
    cell_count = local_count * rows_dev * cols_dev
    aggregated = aggregated.reshape(cell_count, channels)
    mean_square = jnp.mean(aggregated * aggregated, axis=-1, keepdims=True)
    inverse_rms = lax.rsqrt(mean_square + 1e-05)
    normalized = aggregated * inverse_rms
    gain_float = gain.astype(jnp.float32)
    hidden_in = (normalized * gain_float).astype(jnp.bfloat16)
    pre_act = jnp.dot(hidden_in, w_in, preferred_element_type=jnp.float32)
    sigmoid_pre = jax.nn.sigmoid(pre_act)
    activated = (pre_act * sigmoid_pre).astype(jnp.bfloat16)
    increment = jnp.dot(activated, w_out, preferred_element_type=jnp.float32).astype(jnp.bfloat16)
    target_rows = cotangent.reshape(cell_count, channels)
    contract_rows = (((0,), (0,)), ((), ()))
    contract_cols = (((1,), (1,)), ((), ()))
    w_out_grad = lax.dot_general(
        activated, target_rows, contract_rows, preferred_element_type=jnp.float32
    )
    act_grad = lax.dot_general(
        target_rows, w_out, contract_cols, preferred_element_type=jnp.float32
    )
    pre_grad = (act_grad * sigmoid_pre * (1.0 + pre_act * (1.0 - sigmoid_pre))).astype(jnp.bfloat16)
    w_in_grad = lax.dot_general(
        hidden_in, pre_grad, contract_rows, preferred_element_type=jnp.float32
    )
    hidden_grad = lax.dot_general(pre_grad, w_in, contract_cols, preferred_element_type=jnp.float32)
    gain_grad = jnp.sum(hidden_grad * normalized, axis=0)
    scaled_grad = hidden_grad * gain_float
    aggregated_grad = inverse_rms * (
        scaled_grad - normalized * jnp.mean(scaled_grad * normalized, axis=-1, keepdims=True)
    )
    aggregated_grad = aggregated_grad.reshape(local_count, rows_dev, cols_dev, channels)
    tap_grads = []
    for row_shift in range(box_side):
        for col_shift in range(box_side):
            window = extended[
                :, row_shift : row_shift + rows_dev, col_shift : col_shift + cols_dev
            ].astype(jnp.float32)
            tap_grads.append(jnp.sum(aggregated_grad * window, axis=(0, 1, 2)))
    box_grads = jnp.stack(tap_grads)
    stencil_grad = jnp.dot(onehot, box_grads, precision=lax.Precision.HIGHEST)
    summed = lax.psum((stencil_grad, gain_grad, w_in_grad, w_out_grad), ("face", "row", "col"))
    return (increment.reshape(state.shape), summed[0], summed[1], summed[2], summed[3])


def solution(mesh):
    in_specs = (
        P("face", "row", "col", None),
        P(),
        P(),
        P(),
        P(),
        P(),
        P(),
        P("face", "row", "col", None),
    )
    out_specs = (P("face", "row", "col", None), P(), P(), P(), P())
    return jax.shard_map(shards, mesh=mesh, in_specs=in_specs, out_specs=out_specs, check_vma=False)
```

profile of v0, /device:TPU:0, one launch (start us, length us, event | category | flops | bytes accessed | tf_op | source)
XLA Modules:
  0.0 1136.1 jit_solution(4897836279082226139)
XLA Ops:
  7.2 6.4 copy.485
  21.9 76.9 %all_to_all.20 = bf16[4,4,3,2,4,16,256]{6,5,1,4,2,3,0:T(8,128)(2,1)S(1)} all-to-all(bf16[4,4,3,2,4,16,256]{6,5,1,4,2,3,0:T(8,128)(2,1)S(1)} %copy.493), channel_id=1, replica_groups=mesh['face'=2,'row'=4,'col'=4] {'row'}, dimensions={0} | all-to-all | bytes 6291456 | tf_op jit(solution)/shard_map/all_to_all | solution.py:73
  99.3 39.5 %all_to_all.21 = bf16[4,4,3,2,4,16,256]{6,5,0,4,2,3,1:T(8,128)(2,1)S(1)} all-to-all(bf16[4,4,3,2,4,16,256]{6,5,0,4,2,3,1:T(8,128)(2,1)S(1)} %copy.494), channel_id=1, replica_groups=mesh['face'=2,'row'=4,'col'=4] {'col'}, dimensions={1} | all-to-all | bytes 6291456 | tf_op jit(solution)/shard_map/all_to_all | solution.py:72
  202.0 2.6 pad_maximum_fusion.4
  209.2 2.5 rev.64
  212.0 2.5 rev.61
  215.7 2.5 rev.65
  222.2 2.5 rev.66
  224.8 2.5 rev.55
  231.0 2.5 rev.63
  236.0 2.5 rev.54
  243.7 3.6 all-to-all-start.2
  253.3 7.0 all-to-all-done.2
  260.3 3.6 all-to-all-start.3
  264.1 10.9 pad_maximum_fusion
  275.4 8.0 copy.496
  297.3 367.0 %multiply_reduce_fusion.2 = (f32[3,64,64]{2,1,0:T(8,128)S(1)}, f32[3,64,64,256]{3,2,1,0:T(8,128)}) fusion(bf16[3,72,72,256]{3,2,1,0:T(8,128)(2,1)} %fusion.161, f32[256]{0:T(256)S(1)} %bitcast.482, f32[256]{0:T(256)S(1)} %bitcast.483, f32[256]{0:T(256)S(1)} %bitcast.484, f32[256]{0:T(256)S(1)} %bitcast.485, f32[256]{0:T(256)S(1)} %bitcast.486, ...), kind=kLoop, calls=%fused_computation.332 | loop fusion | flops 767545344 | bytes 522322944 | tf_op jit(solution)/shard_map/reduce_sum | solution.py:165
  664.6 8.6 multiply_convert_fusion.2
  673.2 29.6 %multiply_convert_fusion.1 = (bf16[12288,1024]{1,0:T(8,128)(2,1)}, f32[12288,1024]{1,0:T(8,128)}) fusion(bf16[12288,256]{1,0:T(8,128)(2,1)} %multiply_convert_fusion.2, bf16[256,1024]{1,0:T(8,128)(2,1)S(1)} %copy-done), kind=kOutput, calls=%fused_computation.1 | convolution fusion | flops 6505365504 | bytes 82313216 | tf_op jit(solution)/shard_map/dot_general | solution.py:170
  702.9 33.1 %multiply_convert_fusion = bf16[12288,1024]{1,0:T(8,128)(2,1)} fusion(f32[12288,1024]{1,0:T(8,128)} %get-tuple-element.285, bf16[12288,256]{1,0:T(8,128)(2,1)} %bitcast.500, bf16[1024,256]{1,0:T(8,128)(2,1)S(1)} %copy-done.49), kind=kOutput, calls=%fused_computation | convolution fusion | flops 6555697152 | bytes 82313216 | tf_op jit(solution)/shard_map/dot_general | solution.py:180
  736.0 14.2 %fusion.175 = f32[256,1024]{1,0:T(8,128)} fusion(bf16[12288,256]{1,0:T(8,128)(2,1)} %multiply_convert_fusion.2, bf16[12288,1024]{1,0:T(8,128)(2,1)} %multiply_convert_fusion), kind=kOutput, calls=%fused_computation.429 | convolution fusion | flops 6442450944 | bytes 32505856 | tf_op jit(solution)/shard_map/dot_general | solution.py:184
  750.2 19.5 %multiply_reduce_fusion = (f32[256]{0:T(256)}, f32[12288]{0:T(1024)S(1)}, f32[12288,256]{1,0:T(8,128)}) fusion(f32[3,64,64,256]{3,2,1,0:T(8,128)} %get-tuple-element.144, f32[12288]{0:T(1024)S(1)} %copy-done.3, f32[256]{0:T(256)S(1)} %copy-done.7, bf16[12288,1024]{1,0:T(8,128)(2,1)} %multiply_convert_fusion, bf16[256,1024]{1,0:T(8,128)(2,1)S(1)} %copy-done), kind=kOutput, calls=%fused_computation.328 | convolution fusion | flops 6461313024 | bytes 50956288 | tf_op jit(solution)/shard_map/dot_general | solution.py:187
  769.7 17.9 %subtract_multiply_fusion = f32[12288,256]{1,0:T(8,128)} fusion(f32[12288,256]{1,0:T(8,128)} %get-tuple-element.286, f32[3,64,64,256]{3,2,1,0:T(8,128)} %get-tuple-element.144, f32[12288]{0:T(1024)S(1)} %broadcast_multiply_fusion, f32[256]{0:T(256)S(1)} %copy-done.7, f32[12288]{0:T(1024)S(1)} %copy-done.3), kind=kLoop, calls=%fused_computation.329 | loop fusion | flops 15728640 | bytes 37848064 | tf_op jit(solution)/shard_map/mul | solution.py:190
  787.6 15.9 %fusion.33 = (f32[256]{0:T(256)S(1)}, f32[256]{0:T(256)S(1)}, f32[256]{0:T(256)S(1)}, f32[256]{0:T(256)S(1)}, f32[256]{0:T(256)S(1)}, /*index=5*/f32[256]{0:T(25...) fusion(f32[3,64,64,256]{3,2,1,0:T(8,128)} %bitcast.324, bf16[3,72,72,256]{3,2,1,0:T(8,128)(2,1)S(1)} %bitcast.323), kind=kLoop, calls=%fused_computation.199 | loop fusion | flops 84932352 | bytes 69215232 | tf_op jit(solution)/shard_map/reduce_sum | solution.py:200
  803.6 31.3 %fusion.94 = (f32[256]{0:T(256)S(1)}, f32[256]{0:T(256)S(1)}, f32[256]{0:T(256)S(1)}, f32[256]{0:T(256)S(1)}, f32[256]{0:T(256)S(1)}, /*index=5*/f32[256]{0:T(25...) fusion(f32[3,64,64,256]{3,2,1,0:T(8,128)} %bitcast.325, ...), kind=kLoop, calls=%fused_computation.260 | loop fusion | flops 169864704 | bytes 125847552 | tf_op jit(solution)/shard_map/reduce_sum | solution.py:200
  834.9 31.3 %fusion.137 = (f32[256]{0:T(256)S(1)}, f32[256]{0:T(256)S(1)}, f32[256]{0:T(256)S(1)}, f32[256]{0:T(256)S(1)}, f32[256]{0:T(256)S(1)}, /*index=5*/f32[256]{0:T(2...) fusion(f32[3,64,64,256]{3,2,1,0:T(8,128)} %bitcast.326, ...), kind=kLoop, calls=%fused_computation.303 | loop fusion | flops 169864704 | bytes 125847552 | tf_op jit(solution)/shard_map/reduce_sum | solution.py:200
  866.2 31.3 %fusion.160 = (f32[256]{0:T(256)S(1)}, f32[256]{0:T(256)S(1)}, f32[256]{0:T(256)S(1)}, f32[256]{0:T(256)S(1)}, f32[256]{0:T(256)S(1)}, /*index=5*/f32[256]{0:T(2...) fusion(f32[3,64,64,256]{3,2,1,0:T(8,128)} %bitcast.327, ...), kind=kLoop, calls=%fused_computation.326 | loop fusion | flops 169864704 | bytes 125847552 | tf_op jit(solution)/shard_map/reduce_sum | solution.py:200
  897.5 31.3 %fusion.76 = (f32[256]{0:T(256)S(1)}, f32[256]{0:T(256)S(1)}, f32[256]{0:T(256)S(1)}, f32[256]{0:T(256)S(1)}, f32[256]{0:T(256)S(1)}, /*index=5*/f32[256]{0:T(25...) fusion(f32[3,64,64,256]{3,2,1,0:T(8,128)} %bitcast.328, ...), kind=kLoop, calls=%fused_computation.242 | loop fusion | flops 169864704 | bytes 125847552 | tf_op jit(solution)/shard_map/reduce_sum | solution.py:200
  928.9 42.7 %psum.29 = f32[256]{0:T(256)} all-reduce(f32[256]{0:T(256)S(1)} %copy-done.48), channel_id=1, replica_groups=mesh['face'=2,'row'=4,'col'=4] {'face','row','col'}, use_global_device_ids=true, to_apply=%region_91.92 | all-reduce | flops 256 | bytes 2048 | tf_op jit(solution)/shard_map/psum | solution.py:203
  972.7 14.2 %fusion.176 = f32[1024,256]{1,0:T(8,128)} fusion(bf16[12288,1024]{1,0:T(8,128)(2,1)} %get-tuple-element.284, bf16[12288,256]{1,0:T(8,128)(2,1)} %bitcast.501), kind=kOutput, calls=%fused_computation.430 | convolution fusion | flops 6442450944 | bytes 32505856 | tf_op jit(solution)/shard_map/dot_general | solution.py:177
  987.0 13.6 %convolution_convert_fusion = bf16[12288,256]{1,0:T(8,128)(2,1)} fusion(bf16[12288,1024]{1,0:T(8,128)(2,1)} %get-tuple-element.284, bf16[1024,256]{1,0:T(8,128)(2,1)S(1)} %copy-done.50), kind=kOutput, calls=%fused_computation.165 | convolution fusion | flops 6445596672 | bytes 31981568 | tf_op jit(solution)/shard_map/dot_general | solution.py:173
  1000.6 122.2 %all-reduce.4.cloned.1.call-done = (f32[64,256]{1,0:T(8,128)}, f32[256,1024]{1,0:T(8,128)}, f32[1024,256]{1,0:T(8,128)}) async-done(((f32[64,256]{1,0:T(8,128)}, f32[256,1024]{1,0:T(8,128)}, f32[1024,256]{1,0:T(8,128)}), (f32[64,256]{1,0:T(8,128)}, f32[256,1024]{1,0:T(8,128)}, f32[1024,256]{1,0:T(8,128)})) %all-reduce.4.cloned.1.call-update) | async-done | bytes 2162704 | tf_op jit(solution)/shard_map/psum | solution.py:203
  (195 shorter events, 67.5 us)
Async XLA Ops:
  7.2 666.1 %copy-start = (bf16[256,1024]{1,0:T(8,128)(2,1)S(1)}, bf16[256,1024]{1,0:T(8,128)(2,1)}, u32[]{:S(2)}) copy-start(bf16[256,1024]{1,0:T(8,128)(2,1)} %param.21) | copy-start | bytes 1572868
  7.2 200.8 %all-gather.2.cloned.1.call-start = ((), (), s32[]{:S(2)}) async-start(), calls=%async_computation.4 | async-start | bytes 6684672 | tf_op jit(solution)/shard_map/all_gather | solution.py:93
  21.8 121.5 %copy-start.4 = (s32[6,4,3]{0,1,2:T(4,128)S(1)}, s32[6,4,3]{0,1,2:T(4,128)}, u32[]{:S(2)}) copy-start(s32[6,4,3]{0,1,2:T(4,128)} %param.18) | copy-start | bytes 868
  21.9 169.2 %copy-start.52 = (bf16[256]{0:T(256)(128)(2,1)S(1)}, bf16[256]{0:T(256)(128)(2,1)}, u32[]{:S(2)}) copy-start(bf16[256]{0:T(256)(128)(2,1)} %param.20) | copy-start | bytes 1540
  21.9 177.2 %copy-start.51 = (s32[64,2]{0,1:T(2,128)S(1)}, s32[64,2]{0,1:T(2,128)}, u32[]{:S(2)}) copy-start(s32[64,2]{0,1:T(2,128)} %param.17) | copy-start | bytes 1540
  21.9 177.2 %copy-start.5 = (bf16[64,256]{1,0:T(8,128)(2,1)S(1)}, bf16[64,256]{1,0:T(8,128)(2,1)}, u32[]{:S(2)}) copy-start(bf16[64,256]{1,0:T(8,128)(2,1)} %param.19) | copy-start | bytes 98308
  139.9 62.1 %collective-permute-start = (bf16[3,4,64,256]{3,1,2,0:T(4,128)(2,1)S(1)}, bf16[3,4,64,256]{3,1,2,0:T(4,128)(2,1)S(1)}, u32[]{:S(2)}, u32[]{:S(2)}) collective-permute-start(bf16[3,4,64,256]{3,1,2,0:T(4,128)(2,1)S(1)} %slice.1122), channel_id=1, source_target_pairs={{0,4},{4,8},{8,12},{1,5},{5,9},{9,13},{2,6},{6,10},{10,14},{3,7},{... | collective-permute-start | bytes 1179656 | tf_op jit(solution)/shard_map/ppermute | solution.py:17
  142.0 60.0 %collective-permute-start.1 = (bf16[3,4,64,256]{3,1,2,0:T(4,128)(2,1)S(1)}, bf16[3,4,64,256]{3,1,2,0:T(4,128)(2,1)S(1)}, u32[]{:S(2)}, u32[]{:S(2)}) collective-permute-start(bf16[3,4,64,256]{3,1,2,0:T(4,128)(2,1)S(1)} %get-tuple-element.160), channel_id=1, source_target_pairs={{4,0},{8,4},{12,8},{5,1},{9,5},{13,9},{6,2},{10,6},{14,10},{7,3},{... | collective-permute-start | bytes 1179656 | tf_op jit(solution)/shard_map/ppermute | solution.py:19
  204.6 59.5 %collective-permute-start.2 = (bf16[3,72,4,256]{3,1,2,0:T(8,128)(2,1)}, bf16[3,72,4,256]{3,1,2,0:T(8,128)(2,1)}, u32[]{:S(2)}, u32[]{:S(2)}) collective-permute-start(bf16[3,72,4,256]{3,1,2,0:T(8,128)(2,1)} %get-tuple-element.145), channel_id=1, source_target_pairs={{0,1},{1,2},{2,3},{4,5},{5,6},{6,7},{8,9},{9,10},{10,11},{12,13},{... | collective-permute-start | bytes 1327112 | tf_op jit(solution)/shard_map/ppermute | solution.py:17
  206.7 57.4 %collective-permute-start.3 = (bf16[3,72,4,256]{3,1,2,0:T(8,128)(2,1)}, bf16[3,72,4,256]{3,1,2,0:T(8,128)(2,1)}, u32[]{:S(2)}, u32[]{:S(2)}) collective-permute-start(bf16[3,72,4,256]{3,1,2,0:T(8,128)(2,1)} %get-tuple-element.146), channel_id=1, source_target_pairs={{1,0},{2,1},{3,2},{5,4},{6,5},{7,6},{9,8},{10,9},{11,10},{13,12},{... | collective-permute-start | bytes 1327112 | tf_op jit(solution)/shard_map/ppermute | solution.py:19
  243.7 16.6 %all-to-all-start.2 = ((bf16[6,4,72,256]{3,2,1,0:T(8,128)(2,1)}), bf16[6,4,72,256]{3,2,1,0:T(8,128)(2,1)S(1)}, u32[]{:S(2)}, u32[]{:S(2)}) async-start(bf16[6,4,72,256]{3,2,1,0:T(8,128)(2,1)} %bitcast_dynamic-update-slice_fusion.6), calls=%async_computation.2 | async-start | bytes 1769472 | tf_op jit(solution)/shard_map/all_to_all | solution.py:131
  260.3 25.4 %all-to-all-start.3 = ((bf16[6,4,72,256]{3,2,1,0:T(8,128)(2,1)}), bf16[6,4,72,256]{3,2,1,0:T(8,128)(2,1)S(1)}, u32[]{:S(2)}, u32[]{:S(2)}) async-start(bf16[6,4,72,256]{3,2,1,0:T(8,128)(2,1)} %bitcast_dynamic-update-slice_fusion), calls=%async_computation.3 | async-start | bytes 1769472 | tf_op jit(solution)/shard_map/all_to_all | solution.py:132
  263.8 859.0 %all-reduce.4.cloned.1.call-start = ((), (), s32[]{:S(2)}) async-start(), calls=%async_computation.5 | async-start | bytes 4325376 | tf_op jit(solution)/shard_map/psum | solution.py:203
  275.0 21.9 %copy-start.11 = (f32[1,256]{1,0:T(1,128)S(1)}, f32[1,256]{1,0:T(1,128)}, u32[]{:S(2)}) copy-start(f32[1,256]{1,0:T(1,128)} %get-tuple-element.215) | copy-start | bytes 3076
  275.0 21.9 %copy-start.12 = (f32[1,256]{1,0:T(1,128)S(1)}, f32[1,256]{1,0:T(1,128)}, u32[]{:S(2)}) copy-start(f32[1,256]{1,0:T(1,128)} %get-tuple-element.216) | copy-start | bytes 3076
  275.0 21.9 %copy-start.13 = (f32[1,256]{1,0:T(1,128)S(1)}, f32[1,256]{1,0:T(1,128)}, u32[]{:S(2)}) copy-start(f32[1,256]{1,0:T(1,128)} %get-tuple-element.217) | copy-start | bytes 3076
  275.0 21.9 %copy-start.14 = (f32[1,256]{1,0:T(1,128)S(1)}, f32[1,256]{1,0:T(1,128)}, u32[]{:S(2)}) copy-start(f32[1,256]{1,0:T(1,128)} %get-tuple-element.180) | copy-start | bytes 3076
  275.1 21.9 %copy-start.15 = (f32[1,256]{1,0:T(1,128)S(1)}, f32[1,256]{1,0:T(1,128)}, u32[]{:S(2)}) copy-start(f32[1,256]{1,0:T(1,128)} %get-tuple-element.181) | copy-start | bytes 3076
  275.1 21.9 %copy-start.16 = (f32[1,256]{1,0:T(1,128)S(1)}, f32[1,256]{1,0:T(1,128)}, u32[]{:S(2)}) copy-start(f32[1,256]{1,0:T(1,128)} %get-tuple-element.182) | copy-start | bytes 3076
  275.1 21.9 %copy-start.17 = (f32[1,256]{1,0:T(1,128)S(1)}, f32[1,256]{1,0:T(1,128)}, u32[]{:S(2)}) copy-start(f32[1,256]{1,0:T(1,128)} %get-tuple-element.183) | copy-start | bytes 3076
  275.1 21.9 %copy-start.18 = (f32[1,256]{1,0:T(1,128)S(1)}, f32[1,256]{1,0:T(1,128)}, u32[]{:S(2)}) copy-start(f32[1,256]{1,0:T(1,128)} %get-tuple-element.184) | copy-start | bytes 3076
  275.1 21.9 %copy-start.19 = (f32[1,256]{1,0:T(1,128)S(1)}, f32[1,256]{1,0:T(1,128)}, u32[]{:S(2)}) copy-start(f32[1,256]{1,0:T(1,128)} %get-tuple-element.185) | copy-start | bytes 3076
  275.1 21.9 %copy-start.20 = (f32[1,256]{1,0:T(1,128)S(1)}, f32[1,256]{1,0:T(1,128)}, u32[]{:S(2)}) copy-start(f32[1,256]{1,0:T(1,128)} %get-tuple-element.186) | copy-start | bytes 3076
  275.1 21.9 %copy-start.21 = (f32[1,256]{1,0:T(1,128)S(1)}, f32[1,256]{1,0:T(1,128)}, u32[]{:S(2)}) copy-start(f32[1,256]{1,0:T(1,128)} %get-tuple-element.187) | copy-start | bytes 3076
  275.1 21.9 %copy-start.22 = (f32[1,256]{1,0:T(1,128)S(1)}, f32[1,256]{1,0:T(1,128)}, u32[]{:S(2)}) copy-start(f32[1,256]{1,0:T(1,128)} %get-tuple-element.188) | copy-start | bytes 3076
  275.1 21.9 %copy-start.23 = (f32[1,256]{1,0:T(1,128)S(1)}, f32[1,256]{1,0:T(1,128)}, u32[]{:S(2)}) copy-start(f32[1,256]{1,0:T(1,128)} %get-tuple-element.189) | copy-start | bytes 3076
  275.1 21.9 %copy-start.24 = (f32[1,256]{1,0:T(1,128)S(1)}, f32[1,256]{1,0:T(1,128)}, u32[]{:S(2)}) copy-start(f32[1,256]{1,0:T(1,128)} %get-tuple-element.190) | copy-start | bytes 3076
  297.3 367.3 %copy-start.6 = (f32[256]{0:T(256)S(1)}, f32[256]{0:T(256)}, u32[]{:S(2)}) copy-start(f32[256]{0:T(256)} %convert_element_type.436) | copy-start | bytes 3076
  664.6 38.3 %copy-start.2 = (f32[12288]{0:T(1024)}, f32[12288]{0:T(1024)S(1)}, u32[]{:S(2)}) copy-start(f32[12288]{0:T(1024)S(1)} %rsqrt.12) | copy-start | bytes 147460
  673.2 29.6 %copy-start.49 = (bf16[1024,256]{1,0:T(8,128)(2,1)S(1)}, bf16[1024,256]{1,0:T(8,128)(2,1)}, u32[]{:S(2)}) copy-start(bf16[1024,256]{1,0:T(8,128)(2,1)} %param.22) | copy-start | bytes 1572868
  897.5 31.3 %copy-start.48 = (f32[256]{0:T(256)S(1)}, f32[256]{0:T(256)}, u32[]{:S(2)}) copy-start(f32[256]{0:T(256)} %get-tuple-element.53) | copy-start | bytes 3076
  897.5 74.3 %copy-start.47 = (s32[64]{0:T(128)S(1)}, s32[64]{0:T(128)}, u32[]{:S(2)}) copy-start(s32[64]{0:T(128)} %copy-done.46) | copy-start | bytes 772
  (31 other events, 620.2 us)
Sparse Core Ops, SparseCore 0:
  140.0 66.0 all-gather.1
  987.1 135.6 all-reduce.3
where the time goes:
time: 1150 us; the launch traced here: 1140 us
  other arithmetic  572 us (50%)
  blocking collectives  159 us (14%)
  waiting for transfers between devices  129 us (11%)
  matrix products  125 us (11%)
  between operations  68.8 us (6%)
  local copies, waits for them, and re-layouts  66.8 us (6%)
  starting transfers between devices  14.2 us (1%)
    reduce_sum x1, other arithmetic, shards(): mean_square = jnp.mean(aggregated * aggregated, axis=-1, keepdims=True)  367 us
    reduce_sum x5, other arithmetic, shards(): tap_grads.append(jnp.sum(aggregated_grad * window, axis=(0, 1, 2)))  141 us
    psum x1, waiting for transfers between devices, shards(): lax.psum((stencil_grad, gain_grad, w_in_grad, w_out_grad), ('face', 'row'...  122 us
    all_to_all x1, blocking collectives, shards(): lax.all_to_all(outgoing, 'row', split_axis=0, concat_axis=0, tiled=True)  76.9 us
    psum x1, blocking collectives, shards(): lax.psum((stencil_grad, gain_grad, w_in_grad, w_out_grad), ('face', 'row'...  42.7 us
    all_to_all x1, blocking collectives, shards(): lax.all_to_all(lax.all_to_all(outgoing, 'row', split_axis=0, concat_axis=...  39.5 us
    dot_general x1, matrix products, shards(): lax.dot_general(target_rows, w_out, contract_cols, preferred_element_type...  33.1 us
    dot_general x1, matrix products, shards(): pre_act = jnp.dot(hidden_in, w_in, preferred_element_type=jnp.float32)  29.6 us
  transfers between devices with their start and end apart: 8, of which 2 were waited for; matrix products, arithmetic and copies ran while one was open for 7% of the time, Pallas kernels for 0%

commit v1 on v0

--- a/solution.py
+++ b/solution.py
@@ -1,9 +1,110 @@
 import jax
 import jax.numpy as jnp
 from jax import lax
+from jax.experimental import pallas as pl
+from jax.experimental.pallas import tpu as pltpu
 from jax.sharding import PartitionSpec as P
 
 RADIUS = 4
+BOX = 2 * RADIUS + 1
+
+
+def _fwd_kernel(ext_ref, w_ref, out_ref, shift_ref):
+    rows = out_ref.shape[1]
+    cols = out_ref.shape[2]
+    ext_rows = ext_ref.shape[1]
+    for dj in range(BOX):
+        def shift_row(r, carry):
+            shift_ref[r] = ext_ref[0, r, pl.ds(dj, cols), :].astype(jnp.float32)
+            return carry
+
+        lax.fori_loop(0, ext_rows, shift_row, 0)
+        weights = [w_ref[pl.ds(di * BOX + dj, 1), :] for di in range(BOX)]
+
+        def out_row(i, carry):
+            if dj == 0:
+                acc = jnp.zeros((cols, out_ref.shape[3]), jnp.float32)
+            else:
+                acc = out_ref[0, i]
+            for di in range(BOX):
+                acc = acc + weights[di] * shift_ref[i + di]
+            out_ref[0, i] = acc
+            return carry
+
+        lax.fori_loop(0, rows, out_row, 0)
+
+
+def _bwd_kernel(ext_ref, g_ref, out_ref, shift_ref):
+    rows = g_ref.shape[1]
+    cols = g_ref.shape[2]
+    chans = g_ref.shape[3]
+    ext_rows = ext_ref.shape[1]
+
+    @pl.when(pl.program_id(0) == 0)
+    def _():
+        out_ref[...] = jnp.zeros_like(out_ref)
+
+    for dj in range(BOX):
+        def shift_row(r, carry):
+            shift_ref[r] = ext_ref[0, r, pl.ds(dj, cols), :].astype(jnp.float32)
+            return carry
+
+        lax.fori_loop(0, ext_rows, shift_row, 0)
+
+        def grad_row(i, accs):
+            g = g_ref[0, i]
+            new = []
+            for di in range(BOX):
+                p = g * shift_ref[i + di]
+                p = p.reshape(cols // 8, 8, chans).sum(axis=0)
+                new.append(accs[di] + p)
+            return tuple(new)
+
+        init = tuple(jnp.zeros((8, chans), jnp.float32) for _ in range(BOX))
+        accs = lax.fori_loop(0, rows, grad_row, init)
+        for di in range(BOX):
+            out_ref[di * BOX + dj] = out_ref[di * BOX + dj] + accs[di]
+
+
+def stencil_forward(ext, box_weights):
+    faces, ext_rows, ext_cols, chans = ext.shape
+    rows = ext_rows - 2 * RADIUS
+    cols = ext_cols - 2 * RADIUS
+    return pl.pallas_call(
+        _fwd_kernel,
+        grid=(faces,),
+        in_specs=[
+            pl.BlockSpec((1, ext_rows, ext_cols, chans), lambda f: (f, 0, 0, 0)),
+            pl.BlockSpec((BOX * BOX, chans), lambda f: (0, 0)),
+        ],
+        out_specs=pl.BlockSpec((1, rows, cols, chans), lambda f: (f, 0, 0, 0)),
+        out_shape=jax.ShapeDtypeStruct((faces, rows, cols, chans), jnp.float32),
+        scratch_shapes=[pltpu.VMEM((ext_rows, cols, chans), jnp.float32)],
+        compiler_params=pltpu.CompilerParams(
+            dimension_semantics=("arbitrary",), vmem_limit_bytes=48 * 1024 * 1024
+        ),
+    )(ext, box_weights)
+
+
+def stencil_backward(ext, agg_grad):
+    faces, ext_rows, ext_cols, chans = ext.shape
+    rows = ext_rows - 2 * RADIUS
+    cols = ext_cols - 2 * RADIUS
+    partial = pl.pallas_call(
+        _bwd_kernel,
+        grid=(faces,),
+        in_specs=[
+            pl.BlockSpec((1, ext_rows, ext_cols, chans), lambda f: (f, 0, 0, 0)),
+            pl.BlockSpec((1, rows, cols, chans), lambda f: (f, 0, 0, 0)),
+        ],
+        out_specs=pl.BlockSpec((BOX * BOX, 8, chans), lambda f: (0, 0, 0)),
+        out_shape=jax.ShapeDtypeStruct((BOX * BOX, 8, chans), jnp.float32),
+        scratch_shapes=[pltpu.VMEM((ext_rows, cols, chans), jnp.float32)],
+        compiler_params=pltpu.CompilerParams(
+            dimension_semantics=("arbitrary",), vmem_limit_bytes=48 * 1024 * 1024
+        ),
+    )(ext, agg_grad)
+    return jnp.sum(partial, axis=1)
 
 
 def with_halo(cells, sides, width):
@@ -153,13 +254,7 @@
         box_index[:, None] == jnp.arange(box_side * box_side, dtype=jnp.int32)[None, :]
     ).astype(jnp.float32)
     box_weights = jnp.dot(onehot.T, stencil.astype(jnp.float32), precision=lax.Precision.HIGHEST)
-    aggregated = jnp.zeros((local_count, rows_dev, cols_dev, channels), jnp.float32)
-    for row_shift in range(box_side):
-        for col_shift in range(box_side):
-            window = extended[
-                :, row_shift : row_shift + rows_dev, col_shift : col_shift + cols_dev
-            ].astype(jnp.float32)
-            aggregated = aggregated + box_weights[row_shift * box_side + col_shift] * window
+    aggregated = stencil_forward(extended, box_weights)
     cell_count = local_count * rows_dev * cols_dev
     aggregated = aggregated.reshape(cell_count, channels)
     mean_square = jnp.mean(aggregated * aggregated, axis=-1, keepdims=True)
@@ -177,6 +272,7 @@
     w_out_grad = lax.dot_general(
         activated, target_rows, contract_rows, preferred_element_type=jnp.float32
     )
+    w_out_grad = lax.psum(w_out_grad, ("face", "row", "col"))
     act_grad = lax.dot_general(
         target_rows, w_out, contract_cols, preferred_element_type=jnp.float32
     )
@@ -184,6 +280,7 @@
     w_in_grad = lax.dot_general(
         hidden_in, pre_grad, contract_rows, preferred_element_type=jnp.float32
     )
+    w_in_grad = lax.psum(w_in_grad, ("face", "row", "col"))
     hidden_grad = lax.dot_general(pre_grad, w_in, contract_cols, preferred_element_type=jnp.float32)
     gain_grad = jnp.sum(hidden_grad * normalized, axis=0)
     scaled_grad = hidden_grad * gain_float
@@ -191,17 +288,13 @@
         scaled_grad - normalized * jnp.mean(scaled_grad * normalized, axis=-1, keepdims=True)
     )
     aggregated_grad = aggregated_grad.reshape(local_count, rows_dev, cols_dev, channels)
-    tap_grads = []
-    for row_shift in range(box_side):
-        for col_shift in range(box_side):
-            window = extended[
-                :, row_shift : row_shift + rows_dev, col_shift : col_shift + cols_dev
-            ].astype(jnp.float32)
-            tap_grads.append(jnp.sum(aggregated_grad * window, axis=(0, 1, 2)))
-    box_grads = jnp.stack(tap_grads)
+    box_grads = stencil_backward(extended, aggregated_grad)
     stencil_grad = jnp.dot(onehot, box_grads, precision=lax.Precision.HIGHEST)
-    summed = lax.psum((stencil_grad, gain_grad, w_in_grad, w_out_grad), ("face", "row", "col"))
-    return (increment.reshape(state.shape), summed[0], summed[1], summed[2], summed[3])
+    stencil_grad, gain_grad, w_in_grad, w_out_grad = lax.optimization_barrier(
+        (stencil_grad, gain_grad, w_in_grad, w_out_grad)
+    )
+    summed = lax.psum((stencil_grad, gain_grad), ("face", "row", "col"))
+    return (increment.reshape(state.shape), summed[0], summed[1], w_in_grad, w_out_grad)
 
 
 def solution(mesh):

time: 1150 us -> 775 us (0.67)
  other arithmetic: 572 us -> 58.9 us
  Pallas kernels: 0 us -> 216 us
  waiting for transfers between devices: 129 us -> 89.8 us
  local copies, waits for them, and re-layouts: 66.8 us -> 39.6 us
    reduce_sum x1, other arithmetic: 367 us -> 6.27 us  [shards(): mean_square = jnp.mean(aggregated * aggregated, axis=-1, keepdims=True)]
    pallas_call x0 -> x2, Pallas kernels: none -> 216 us  [the longest x1 109 us: stencil_backward(): pl.pallas_call(_bwd_kernel, grid=(faces,), in_specs=[pl.BlockSpec((1, ext...]
    reduce_sum x5 -> x1, other arithmetic: 141 us -> 0.16 us  [stencil_backward(): return jnp.sum(partial, axis=1)]
    psum x1 -> x2, waiting for transfers between devices: 122 us -> 78.9 us  [the longest x1 70.9 us: shards(): summed = lax.psum((stencil_grad, gain_grad), ('face', 'row', 'col'))]
  transfers between devices with their start and end apart: 8 -> 9, of which waited for: 2 -> 4; matrix products, arithmetic and copies ran while one was open for 7% -> 10% of each run, Pallas kernels for 0% -> 14%
where the time goes in v1:
time: 775 us; the launch traced here: 766 us
  Pallas kernels  216 us (28%)
  blocking collectives  155 us (20%)
  matrix products  125 us (16%)
  waiting for transfers between devices  89.8 us (12%)
  between operations  67.1 us (9%)
  other arithmetic  58.9 us (8%)
  local copies, waits for them, and re-layouts  39.6 us (5%)
  starting transfers between devices  14.2 us (2%)
    pallas_call x1, Pallas kernels, stencil_backward(): pl.pallas_call(_bwd_kernel, grid=(faces,), in_specs=[pl.BlockSpec((1, ext...  109 us
    pallas_call x1, Pallas kernels, stencil_forward(): pl.pallas_call(_fwd_kernel, grid=(faces,), in_specs=[pl.BlockSpec((1, ext...  107 us
    all_to_all x1, blocking collectives, shards(): lax.all_to_all(outgoing, 'row', split_axis=0, concat_axis=0, tiled=True)  76.8 us
    psum x1, waiting for transfers between devices, shards(): summed = lax.psum((stencil_grad, gain_grad), ('face', 'row', 'col'))  70.9 us
    all_to_all x1, blocking collectives, shards(): lax.all_to_all(lax.all_to_all(outgoing, 'row', split_axis=0, concat_axis=...  39.5 us
    psum x1, blocking collectives, shards(): summed = lax.psum((stencil_grad, gain_grad), ('face', 'row', 'col'))  39.2 us
    dot_general x1, matrix products, shards(): lax.dot_general(target_rows, w_out, contract_cols, preferred_element_type...  33.3 us
    dot_general x1, matrix products, shards(): pre_act = jnp.dot(hidden_in, w_in, preferred_element_type=jnp.float32)  29.7 us
  transfers between devices with their start and end apart: 9, of which 4 were waited for; matrix products, arithmetic and copies ran while one was open for 10% of the time, Pallas kernels for 14%

profile of v1, /device:TPU:0, one launch (start us, length us, event | category | flops | bytes accessed | tf_op | source)
XLA Modules:
  0.0 766.5 jit_solution(16941680926776449394)
XLA Ops:
  12.6 76.8 %all_to_all.20 = bf16[4,4,3,2,4,16,256]{6,5,1,4,2,3,0:T(8,128)(2,1)S(1)} all-to-all(bf16[4,4,3,2,4,16,256]{6,5,1,4,2,3,0:T(8,128)(2,1)S(1)} %copy.37), channel_id=1, replica_groups=mesh['face'=2,'row'=4,'col'=4] {'row'}, dimensions={0} | all-to-all | bytes 6291456 | tf_op jit(solution)/shard_map/all_to_all | solution.py:174
  89.8 39.5 %all_to_all.21 = bf16[4,4,3,2,4,16,256]{6,5,0,4,2,3,1:T(8,128)(2,1)S(1)} all-to-all(bf16[4,4,3,2,4,16,256]{6,5,0,4,2,3,1:T(8,128)(2,1)S(1)} %copy.38), channel_id=1, replica_groups=mesh['face'=2,'row'=4,'col'=4] {'col'}, dimensions={1} | all-to-all | bytes 6291456 | tf_op jit(solution)/shard_map/all_to_all | solution.py:173
  130.4 2.1 collective-permute-start
  188.7 3.4 constant_dynamic-update-slice_fusion.1
  192.1 2.9 copy-done.1
  196.3 2.1 collective-permute-start.2
  203.3 2.5 rev.57
  205.8 2.5 rev.58
  209.8 2.5 rev.55
  212.4 2.5 rev.56
  216.6 2.5 rev.54
  223.4 3.6 all-to-all-start.3
  230.1 9.9 %all-to-all-done.3 = bf16[6,4,72,256]{3,2,1,0:T(8,128)(2,1)S(1)} async-done(((bf16[6,4,72,256]{3,2,1,0:T(8,128)(2,1)}), bf16[6,4,72,256]{3,2,1,0:T(8,128)(2,1)S(1)}, u32[]{:S(2)}, u32[]{:S(2)}) %all-to-all-start.3) | async-done | bytes 884768 | tf_op jit(solution)/shard_map/all_to_all | solution.py:233
  240.0 3.6 all-to-all-start.2
  243.8 8.9 %pad_maximum_fusion = bf16[3,72,72,256]{3,2,1,0:T(8,128)(2,1)} fusion(bf16[3,72,4,256]{3,2,1,0:T(4,128)(2,1)} %collective-permute-done.3, bf16[3,72,64,256]{3,2,1,0:T(8,128)(2,1)} %copy-done.1, bf16[3,72,4,256]{3,2,1,0:T(4,128)(2,1)} %collective-permute-done.2), kind=kLoop, calls=%fused_computation.10 | loop fusion | flops 23887872 | bytes 15925248 | tf_op jit(solution)/shard_map/concatenate | solution.py:116
  256.3 1.9 fusion.3
  260.2 2.3 fusion.1
  262.5 2.4 fusion.ext_ref
  264.8 107.0 %shard_map.119 = f32[3,64,64,256]{3,2,1,0:T(8,128)} custom-call(bf16[3,72,72,256]{3,2,1,0:T(8,128)(2,1)} %fusion.ext_ref, f32[81,256]{1,0:T(8,128)S(1)} %fusion.5.w_ref), custom_call_target="tpu_custom_call" | custom-call | tf_op jit(solution)/shard_map/pallas_call | solution.py:73
  371.9 6.3 multiply_reduce_fusion.2
  378.3 8.6 %multiply_convert_fusion.2 = bf16[12288,256]{1,0:T(8,128)(2,1)} fusion(f32[3,64,64,256]{3,2,1,0:T(8,128)} %shard_map.119, f32[256]{0:T(256)S(1)} %convert_element_type.12, f32[12288]{0:T(1024)S(1)} %rsqrt.12), kind=kLoop, calls=%fused_computation.8 | loop fusion | flops 9437184 | bytes 18924544 | tf_op jit(solution)/shard_map/convert_element_type | solution.py:264
  386.9 29.7 %multiply_convert_fusion.1 = (bf16[12288,1024]{1,0:T(8,128)(2,1)}, f32[12288,1024]{1,0:T(8,128)}) fusion(bf16[12288,256]{1,0:T(8,128)(2,1)} %multiply_convert_fusion.2, bf16[256,1024]{1,0:T(8,128)(2,1)S(1)} %copy-done), kind=kOutput, calls=%fused_computation.1 | convolution fusion | flops 6505365504 | bytes 82313216 | tf_op jit(solution)/shard_map/dot_general | solution.py:265
  416.6 33.3 %multiply_convert_fusion = bf16[12288,1024]{1,0:T(8,128)(2,1)} fusion(f32[12288,1024]{1,0:T(8,128)} %get-tuple-element.130, bf16[12288,256]{1,0:T(8,128)(2,1)} %bitcast.170, bf16[1024,256]{1,0:T(8,128)(2,1)S(1)} %copy-done.13), kind=kOutput, calls=%fused_computation | convolution fusion | flops 6555697152 | bytes 82313216 | tf_op jit(solution)/shard_map/dot_general | solution.py:276
  449.9 14.2 %fusion.11 = f32[256,1024]{1,0:T(8,128)} fusion(bf16[12288,256]{1,0:T(8,128)(2,1)} %multiply_convert_fusion.2, bf16[12288,1024]{1,0:T(8,128)(2,1)} %multiply_convert_fusion), kind=kOutput, calls=%fused_computation.103 | convolution fusion | flops 6442450944 | bytes 32505856 | tf_op jit(solution)/shard_map/dot_general | solution.py:280
  464.1 18.8 %multiply_reduce_fusion = (f32[256]{0:T(256)S(1)}, f32[12288]{0:T(1024)S(1)}, f32[12288,256]{1,0:T(8,128)}) fusion(f32[3,64,64,256]{3,2,1,0:T(8,128)} %shard_map.119, f32[12288]{0:T(1024)S(1)} %copy-done.6, f32[256]{0:T(256)S(1)} %copy-done.10, bf16[12288,1024]{1,0:T(8,128)(2,1)} %multiply_convert_fusion, bf16[256,1024]{1,0:T(8,128)(2,1)S(1)} %copy-done), kind=kOutput, calls=%fused_computation.5 | convolution fusion | flops 6461313024 | bytes 50956288 | tf_op jit(solution)/shard_map/dot_general | solution.py:284
  482.9 14.4 %fusion.12 = f32[1024,256]{1,0:T(8,128)} fusion(bf16[12288,1024]{1,0:T(8,128)(2,1)} %get-tuple-element.129, bf16[12288,256]{1,0:T(8,128)(2,1)} %bitcast.171), kind=kOutput, calls=%fused_computation.104 | convolution fusion | flops 6442450944 | bytes 32505856 | tf_op jit(solution)/shard_map/dot_general | solution.py:272
  497.4 16.6 %subtract_multiply_fusion = f32[12288,256]{1,0:T(8,128)} fusion(f32[12288,256]{1,0:T(8,128)} %get-tuple-element.131, f32[3,64,64,256]{3,2,1,0:T(8,128)} %shard_map.119, f32[12288]{0:T(1024)S(1)} %broadcast_multiply_fusion, f32[256]{0:T(256)S(1)} %copy-done.10, f32[12288]{0:T(1024)S(1)} %copy-done.6), kind=kLoop, calls=%fused_computation.6 | loop fusion | flops 15728640 | bytes 37848064 | tf_op jit(solution)/shard_map/mul | solution.py:287
  514.0 109.5 %shard_map.120 = f32[81,8,256]{2,1,0:T(8,128)S(1)} custom-call(bf16[3,72,72,256]{3,2,1,0:T(8,128)(2,1)} %fusion.ext_ref, f32[3,64,64,256]{3,2,1,0:T(8,128)} %bitcast.160), custom_call_target="tpu_custom_call" | custom-call | tf_op jit(solution)/shard_map/pallas_call | solution.py:93
  624.5 8.0 %all-reduce.7.cloned.1.call-done = (f32[256,1024]{1,0:T(8,128)}, f32[1024,256]{1,0:T(8,128)}) async-done(((f32[256,1024]{1,0:T(8,128)}, f32[1024,256]{1,0:T(8,128)}), (f32[256,1024]{1,0:T(8,128)}, f32[1024,256]{1,0:T(8,128)})) %all-reduce.7.cloned.1.call-update) | async-done | bytes 2097168 | tf_op jit(solution)/shard_map/psum | solution.py:283
  632.6 13.4 %convolution_convert_fusion = bf16[12288,256]{1,0:T(8,128)(2,1)} fusion(bf16[12288,1024]{1,0:T(8,128)(2,1)} %get-tuple-element.129, bf16[1024,256]{1,0:T(8,128)(2,1)S(1)} %copy-done.13), kind=kOutput, calls=%fused_computation.3 | convolution fusion | flops 6445596672 | bytes 31981568 | tf_op jit(solution)/shard_map/dot_general | solution.py:268
  646.0 39.2 %psum.31 = f32[256]{0:T(256)} all-reduce(f32[256]{0:T(256)S(1)} %get-tuple-element.58), channel_id=1, replica_groups=mesh['face'=2,'row'=4,'col'=4] {'face','row','col'}, use_global_device_ids=true, to_apply=%region_13.14 | all-reduce | flops 256 | bytes 2048 | tf_op jit(solution)/shard_map/psum | solution.py:296
  685.2 70.9 %all-reduce.5.cloned.1.call-done = f32[64,256]{1,0:T(8,128)} async-done(((f32[64,256]{1,0:T(8,128)}), f32[64,256]{1,0:T(8,128)}) %all-reduce.5.cloned.1.call-update) | async-done | bytes 65552 | tf_op jit(solution)/shard_map/psum | solution.py:296
  (106 shorter events, 37.6 us)
Async XLA Ops:
  7.2 379.7 %copy-start = (bf16[256,1024]{1,0:T(8,128)(2,1)S(1)}, bf16[256,1024]{1,0:T(8,128)(2,1)}, u32[]{:S(2)}) copy-start(bf16[256,1024]{1,0:T(8,128)(2,1)} %param.21) | copy-start | bytes 1572868
  7.2 192.5 %all-gather.2.cloned.1.call-start = ((), (), s32[]{:S(2)}) async-start(), calls=%async_computation.4 | async-start | bytes 6684672 | tf_op jit(solution)/shard_map/all_gather | solution.py:194
  89.4 44.6 %copy-start.7 = (s32[6,4,3]{0,1,2:T(4,128)S(1)}, s32[6,4,3]{0,1,2:T(4,128)}, u32[]{:S(2)}) copy-start(s32[6,4,3]{0,1,2:T(4,128)} %param.18) | copy-start | bytes 868
  89.4 91.5 %copy-start.15 = (bf16[256]{0:T(256)(128)(2,1)S(1)}, bf16[256]{0:T(256)(128)(2,1)}, u32[]{:S(2)}) copy-start(bf16[256]{0:T(256)(128)(2,1)} %param.20) | copy-start | bytes 1540
  89.4 98.9 %copy-start.14 = (s32[64,2]{0,1:T(2,128)S(1)}, s32[64,2]{0,1:T(2,128)}, u32[]{:S(2)}) copy-start(s32[64,2]{0,1:T(2,128)} %param.17) | copy-start | bytes 1540
  89.4 98.9 %copy-start.8 = (bf16[64,256]{1,0:T(8,128)(2,1)S(1)}, bf16[64,256]{1,0:T(8,128)(2,1)}, u32[]{:S(2)}) copy-start(bf16[64,256]{1,0:T(8,128)(2,1)} %param.19) | copy-start | bytes 98308
  130.4 58.2 %collective-permute-start = (bf16[3,4,64,256]{3,2,1,0:T(8,128)(2,1)S(1)}, bf16[3,4,64,256]{3,2,1,0:T(8,128)(2,1)S(1)}, u32[]{:S(2)}, u32[]{:S(2)}) collective-permute-start(bf16[3,4,64,256]{3,2,1,0:T(8,128)(2,1)S(1)} %slice.334), channel_id=1, source_target_pairs={{0,4},{4,8},{8,12},{1,5},{5,9},{9,13},{2,6},{6,10},{10,14},{3,7},{... | collective-permute-start | bytes 1179656 | tf_op jit(solution)/shard_map/ppermute | solution.py:118
  132.6 59.5 %collective-permute-start.1 = (bf16[3,4,64,256]{3,2,1,0:T(8,128)(2,1)S(1)}, bf16[3,4,64,256]{3,2,1,0:T(8,128)(2,1)S(1)}, u32[]{:S(2)}, u32[]{:S(2)}) collective-permute-start(bf16[3,4,64,256]{3,2,1,0:T(8,128)(2,1)S(1)} %get-tuple-element.84), channel_id=1, source_target_pairs={{4,0},{8,4},{12,8},{5,1},{9,5},{13,9},{6,2},{10,6},{14,10},{7,3},{... | collective-permute-start | bytes 1179656 | tf_op jit(solution)/shard_map/ppermute | solution.py:120
  180.9 197.4 %copy-start.9 = (f32[256]{0:T(256)}, f32[256]{0:T(256)S(1)}, u32[]{:S(2)}) copy-start(f32[256]{0:T(256)S(1)} %convert_element_type.12) | copy-start | bytes 3076
  188.3 8.0 %copy-start.11 = (s32[64]{0:T(128)}, s32[64]{0:T(128)S(1)}, u32[]{:S(2)}) copy-start(s32[64]{0:T(128)S(1)} %add_bitcast_fusion) | copy-start | bytes 772
  192.1 2.9 copy-start.1
  196.3 47.5 %collective-permute-start.2 = (bf16[3,72,4,256]{3,2,1,0:T(4,128)(2,1)}, bf16[3,72,4,256]{3,2,1,0:T(4,128)(2,1)}, u32[]{:S(2)}, u32[]{:S(2)}) collective-permute-start(bf16[3,72,4,256]{3,2,1,0:T(4,128)(2,1)} %get-tuple-element.69), channel_id=1, source_target_pairs={{0,1},{1,2},{2,3},{4,5},{5,6},{6,7},{8,9},{9,10},{10,11},{12,13},{... | collective-permute-start | bytes 1327112 | tf_op jit(solution)/shard_map/ppermute | solution.py:118
  198.4 45.4 %collective-permute-start.3 = (bf16[3,72,4,256]{3,2,1,0:T(4,128)(2,1)}, bf16[3,72,4,256]{3,2,1,0:T(4,128)(2,1)}, u32[]{:S(2)}, u32[]{:S(2)}) collective-permute-start(bf16[3,72,4,256]{3,2,1,0:T(4,128)(2,1)} %get-tuple-element.70), channel_id=1, source_target_pairs={{1,0},{2,1},{3,2},{5,4},{6,5},{7,6},{9,8},{10,9},{11,10},{13,12},{... | collective-permute-start | bytes 1327112 | tf_op jit(solution)/shard_map/ppermute | solution.py:120
  223.4 16.6 %all-to-all-start.3 = ((bf16[6,4,72,256]{3,2,1,0:T(8,128)(2,1)}), bf16[6,4,72,256]{3,2,1,0:T(8,128)(2,1)S(1)}, u32[]{:S(2)}, u32[]{:S(2)}) async-start(bf16[6,4,72,256]{3,2,1,0:T(8,128)(2,1)} %bitcast_dynamic-update-slice_fusion.1), calls=%async_computation.3 | async-start | bytes 1769472 | tf_op jit(solution)/shard_map/all_to_all | solution.py:233
  229.2 0.9 copy-start.2
  240.0 15.9 %all-to-all-start.2 = ((bf16[6,4,72,256]{3,2,1,0:T(8,128)(2,1)}), bf16[6,4,72,256]{3,2,1,0:T(8,128)(2,1)S(1)}, u32[]{:S(2)}, u32[]{:S(2)}) async-start(bf16[6,4,72,256]{3,2,1,0:T(8,128)(2,1)} %copy-done.2), calls=%async_computation.2 | async-start | bytes 1769472 | tf_op jit(solution)/shard_map/all_to_all | solution.py:232
  243.6 389.0 %all-reduce.7.cloned.1.call-start = ((), (), s32[]{:S(2)}) async-start(), calls=%async_computation.6 | async-start | bytes 4194304 | tf_op jit(solution)/shard_map/psum | solution.py:283
  378.3 8.6 %copy-start.5 = (f32[12288]{0:T(1024)}, f32[12288]{0:T(1024)S(1)}, u32[]{:S(2)}) copy-start(f32[12288]{0:T(1024)S(1)} %rsqrt.12) | copy-start | bytes 147460
  386.9 29.7 %copy-start.13 = (bf16[1024,256]{1,0:T(8,128)(2,1)S(1)}, bf16[1024,256]{1,0:T(8,128)(2,1)}, u32[]{:S(2)}) copy-start(bf16[1024,256]{1,0:T(8,128)(2,1)} %param.22) | copy-start | bytes 1572868
  449.9 14.2 %copy-start.6 = (f32[12288]{0:T(1024)S(1)}, f32[12288]{0:T(1024)}, u32[]{:S(2)}) copy-start(f32[12288]{0:T(1024)} %copy-done.5) | copy-start | bytes 147460
  449.9 14.2 %copy-start.10 = (f32[256]{0:T(256)S(1)}, f32[256]{0:T(256)}, u32[]{:S(2)}) copy-start(f32[256]{0:T(256)} %copy-done.9) | copy-start | bytes 3076
  497.4 258.7 %all-reduce.5.cloned.1.call-start = ((), (), s32[]{:S(2)}) async-start(), calls=%async_computation.5 | async-start | bytes 131072 | tf_op jit(solution)/shard_map/psum | solution.py:296
  514.0 109.6 %copy-start.12 = (s32[64]{0:T(128)S(1)}, s32[64]{0:T(128)}, u32[]{:S(2)}) copy-start(s32[64]{0:T(128)} %copy-done.11) | copy-start | bytes 772
  632.6 125.0 %copy-start.4 = (f32[256,1024]{1,0:T(8,128)S(1)}, f32[256,1024]{1,0:T(8,128)}, u32[]{:S(2)}) copy-start(f32[256,1024]{1,0:T(8,128)} %get-tuple-element.153) | copy-start | bytes 3145732
  632.6 126.0 %copy-start.3 = (f32[1024,256]{1,0:T(8,128)S(1)}, f32[1024,256]{1,0:T(8,128)}, u32[]{:S(2)}) copy-start(f32[1024,256]{1,0:T(8,128)} %get-tuple-element.154) | copy-start | bytes 3145732
Sparse Core Ops, SparseCore 0:
  130.6 66.0 all-gather.1
  497.5 135.0 all-reduce.6
  639.6 116.4 all-reduce.4

commit v2 on v1

--- a/solution.py
+++ b/solution.py
@@ -154,44 +154,42 @@
     right_strip = jnp.swapaxes(jnp.flip(state[:, :, cols_dev - radius_cells :], axis=2), 1, 2)
     across = jnp.where(row_index == 0, top_strip, bottom_strip)
     downward = jnp.where(col_index == 0, left_strip, right_strip)
-    across_pieces = jnp.moveaxis(
-        across.reshape(local_count, radius_cells, row_count, piece_cells, channels), 2, 0
-    )
-    down_pieces = jnp.moveaxis(
-        downward.reshape(local_count, radius_cells, col_count, piece_cells, channels), 2, 0
-    )
-    empty_slots = jnp.zeros(
-        (row_count * col_count, local_count, radius_cells, piece_cells, channels), state.dtype
-    )
-    across_slots = lax.dynamic_update_slice_in_dim(
-        empty_slots, across_pieces, col_index * row_count, 0
-    )
-    down_slots = lax.dynamic_update_slice_in_dim(empty_slots, down_pieces, row_index * col_count, 0)
-    outgoing = jnp.stack([across_slots, down_slots], axis=2).reshape(
-        row_count, col_count, local_count, 2, radius_cells, piece_cells, channels
-    )
-    arrived = lax.all_to_all(
-        lax.all_to_all(outgoing, "row", split_axis=0, concat_axis=0, tiled=True),
+    sub_across = cols_dev // row_count
+    sub_down = rows_dev // col_count
+    across_sub = lax.all_to_all(
+        across.reshape(local_count, radius_cells, row_count, sub_across, channels),
+        "row",
+        split_axis=2,
+        concat_axis=2,
+        tiled=True,
+    )
+    down_sub = lax.all_to_all(
+        downward.reshape(local_count, radius_cells, col_count, sub_down, channels),
         "col",
-        split_axis=1,
-        concat_axis=1,
+        split_axis=2,
+        concat_axis=2,
         tiled=True,
     )
-    own_pieces = jnp.stack(
-        [
-            jnp.sum(arrived[0, :, :, 0], axis=0),
-            jnp.sum(arrived[row_count - 1, :, :, 0], axis=0),
-            jnp.sum(arrived[:, 0, :, 1], axis=0),
-            jnp.sum(arrived[:, col_count - 1, :, 1], axis=0),
-        ],
-        axis=1,
-    )
+    own_across = jnp.stack([across_sub[:, :, 0], across_sub[:, :, row_count - 1]], axis=1)
+    own_down = jnp.stack([down_sub[:, :, 0], down_sub[:, :, col_count - 1]], axis=1)
+    across_all = lax.all_gather(own_across, ("row", "col")).reshape(
+        row_count, col_count, local_count, 2, radius_cells, sub_across, channels
+    )
+    down_all = lax.all_gather(own_down, ("row", "col")).reshape(
+        row_count, col_count, local_count, 2, radius_cells, sub_down, channels
+    )
+    across_full = jnp.transpose(across_all, (2, 3, 4, 1, 0, 5, 6)).reshape(
+        local_count, 2, radius_cells, face_side, channels
+    )
+    down_full = jnp.transpose(down_all, (2, 3, 4, 0, 1, 5, 6)).reshape(
+        local_count, 2, radius_cells, face_side, channels
+    )
+    side_edges = jnp.concatenate([across_full, down_full], axis=1)
     across_side = jnp.where(row_index == 0, 0, 1).astype(jnp.int32)
     down_side = jnp.where(col_index == 0, 2, 3).astype(jnp.int32)
     across_len = cols_dev + 2 * radius_cells
     down_len = rows_dev + 2 * radius_cells
     edge_pad = ((0, 0), (0, 0), (0, 0), (radius_cells, radius_cells), (0, 0))
-    side_edges = lax.all_gather(own_pieces, ("row", "col"), axis=3, tiled=True)
     padded_edges = jnp.pad(side_edges, edge_pad)
     across_list = []
     down_list = []
@@ -272,7 +270,6 @@
     w_out_grad = lax.dot_general(
         activated, target_rows, contract_rows, preferred_element_type=jnp.float32
     )
-    w_out_grad = lax.psum(w_out_grad, ("face", "row", "col"))
     act_grad = lax.dot_general(
         target_rows, w_out, contract_cols, preferred_element_type=jnp.float32
     )
@@ -280,9 +277,15 @@
     w_in_grad = lax.dot_general(
         hidden_in, pre_grad, contract_rows, preferred_element_type=jnp.float32
     )
-    w_in_grad = lax.psum(w_in_grad, ("face", "row", "col"))
     hidden_grad = lax.dot_general(pre_grad, w_in, contract_cols, preferred_element_type=jnp.float32)
     gain_grad = jnp.sum(hidden_grad * normalized, axis=0)
+    out_rows = w_out_grad.shape[0]
+    w_in_grad, out_and_gain = lax.psum(
+        (w_in_grad, jnp.concatenate([w_out_grad, gain_grad[None, :]], axis=0)),
+        ("face", "row", "col"),
+    )
+    w_out_grad = out_and_gain[:out_rows]
+    gain_grad = out_and_gain[out_rows]
     scaled_grad = hidden_grad * gain_float
     aggregated_grad = inverse_rms * (
         scaled_grad - normalized * jnp.mean(scaled_grad * normalized, axis=-1, keepdims=True)
@@ -290,11 +293,26 @@
     aggregated_grad = aggregated_grad.reshape(local_count, rows_dev, cols_dev, channels)
     box_grads = stencil_backward(extended, aggregated_grad)
     stencil_grad = jnp.dot(onehot, box_grads, precision=lax.Precision.HIGHEST)
-    stencil_grad, gain_grad, w_in_grad, w_out_grad = lax.optimization_barrier(
-        (stencil_grad, gain_grad, w_in_grad, w_out_grad)
-    )
-    summed = lax.psum((stencil_grad, gain_grad), ("face", "row", "col"))
-    return (increment.reshape(state.shape), summed[0], summed[1], w_in_grad, w_out_grad)
+    stencil_grad, w_in_grad, out_and_gain = lax.optimization_barrier(
+        (stencil_grad, w_in_grad, out_and_gain)
+    )
+    w_out_grad = out_and_gain[:out_rows]
+    gain_grad = out_and_gain[out_rows]
+    stencil_grad = butterfly_sum(stencil_grad, ("face", "row", "col"))
+    return (increment.reshape(state.shape), stencil_grad, gain_grad, w_in_grad, w_out_grad)
+
+
+def butterfly_sum(value, axes):
+    for axis in axes:
+        count = lax.axis_size(axis)
+        if count & (count - 1):
+            value = lax.psum(value, axis)
+            continue
+        step = 1
+        while step < count:
+            value = value + lax.ppermute(value, axis, [(i, i ^ step) for i in range(count)])
+            step *= 2
+    return value
 
 
 def solution(mesh):

time: 775 us -> 609 us (0.79)
  blocking collectives: 155 us -> 33.8 us
  waiting for transfers between devices: 89.8 us -> 28.1 us
    all_to_all x2, blocking collectives: 116 us -> 33.8 us  [the longest x1 22.3 us: shards(): lax.all_to_all(across.reshape(local_count, radius_cells, row_count, sub_a...]
    psum x2 -> x1, waiting for transfers between devices: 78.9 us -> 8.18 us  [shards(): lax.psum((w_in_grad, jnp.concatenate([w_out_grad, gain_grad[None, :]], ax...]
    psum x1 -> x0, blocking collectives: 39.2 us -> none  [shards(): summed = lax.psum((stencil_grad, gain_grad), ('face', 'row', 'col'))]
    ppermute x0 -> x5, waiting for transfers between devices: none -> 9.03 us  [butterfly_sum(): lax.ppermute(value, axis, [(i, i ^ step) for i in range(count)])]
    ppermute x0 -> x5, starting transfers between devices: none -> 8 us  [butterfly_sum(): lax.ppermute(value, axis, [(i, i ^ step) for i in range(count)])]
  transfers between devices with their start and end apart: 9 -> 14, of which waited for: 4 -> 7; matrix products, arithmetic and copies ran while one was open for 10% -> 15% of each run, Pallas kernels for 14% -> 18%
where the time goes in v2:
time: 609 us; the launch traced here: 602 us
  Pallas kernels  216 us (35%)
  matrix products  124 us (20%)
  between operations  67.5 us (11%)
  other arithmetic  65.3 us (11%)
  local copies, waits for them, and re-layouts  44.8 us (7%)
  blocking collectives  33.8 us (6%)
  waiting for transfers between devices  28.1 us (5%)
  starting transfers between devices  21.9 us (4%)
    pallas_call x1, Pallas kernels, stencil_backward(): pl.pallas_call(_bwd_kernel, grid=(faces,), in_specs=[pl.BlockSpec((1, ext...  109 us
    pallas_call x1, Pallas kernels, stencil_forward(): pl.pallas_call(_fwd_kernel, grid=(faces,), in_specs=[pl.BlockSpec((1, ext...  107 us
    dot_general x1, matrix products, shards(): lax.dot_general(target_rows, w_out, contract_cols, preferred_element_type...  33.4 us
    dot_general x1, matrix products, shards(): pre_act = jnp.dot(hidden_in, w_in, preferred_element_type=jnp.float32)  29.7 us
    all_to_all x1, blocking collectives, shards(): lax.all_to_all(across.reshape(local_count, radius_cells, row_count, sub_a...  22.3 us
    dot_general x1, matrix products, shards(): lax.dot_general(pre_grad, w_in, contract_cols, preferred_element_type=jnp...  18.7 us
    mul x1, other arithmetic, shards(): inverse_rms * (scaled_grad - normalized * jnp.mean(scaled_grad * normaliz...  16.6 us
    rev x12, local copies, waits for them, and re-layouts, cut_segment(): return jnp.where(flip_flag == 1, jnp.flip(segment, axis=1), segment)  14.5 us
  transfers between devices with their start and end apart: 14, of which 7 were waited for; matrix products, arithmetic and copies ran while one was open for 15% of the time, Pallas kernels for 18%

profile of v2, /device:TPU:0, one launch (start us, length us, event | category | flops | bytes accessed | tf_op | source)
XLA Modules:
  0.0 602.1 jit_solution(3254558388955425121)
XLA Ops:
  9.2 11.5 %all_to_all.20 = bf16[3,4,4,16,256]{4,3,1,0,2:T(8,128)(2,1)S(1)} all-to-all(bf16[3,4,4,16,256]{4,3,1,0,2:T(8,128)(2,1)S(1)} %copy.54), channel_id=1, replica_groups=mesh['face'=2,'row'=4,'col'=4] {'col'}, dimensions={2} | all-to-all | bytes 786432 | tf_op jit(solution)/shard_map/all_to_all | solution.py:166
  23.7 22.3 %all_to_all.21 = bf16[3,4,4,16,256]{4,3,1,0,2:T(8,128)(2,1)S(1)} all-to-all(bf16[3,4,4,16,256]{4,3,1,0,2:T(8,128)(2,1)S(1)} %copy.49), channel_id=1, replica_groups=mesh['face'=2,'row'=4,'col'=4] {'row'}, dimensions={2} | all-to-all | bytes 786432 | tf_op jit(solution)/shard_map/all_to_all | solution.py:159
  108.2 3.4 constant_dynamic-update-slice_fusion.1
  111.7 2.9 copy-done.2
  119.2 4.1 copy.56
  125.7 3.9 fusion.3
  129.6 2.8 copy-done.1
  132.8 2.5 rev.58
  135.3 2.5 rev.57
  137.8 2.5 rev.56
  140.3 2.5 rev.55
  142.8 2.5 rev.54
  152.6 3.6 all-to-all-start.3
  159.3 9.9 %all-to-all-done.3 = bf16[6,4,72,256]{3,2,1,0:T(8,128)(2,1)S(1)} async-done(((bf16[6,4,72,256]{3,2,1,0:T(8,128)(2,1)}), bf16[6,4,72,256]{3,2,1,0:T(8,128)(2,1)S(1)}, u32[]{:S(2)}, u32[]{:S(2)}) %all-to-all-start.3) | async-done | bytes 884768 | tf_op jit(solution)/shard_map/all_to_all | solution.py:231
  169.2 3.6 all-to-all-start.2
  173.0 8.8 %pad_maximum_fusion = bf16[3,72,72,256]{3,2,1,0:T(8,128)(2,1)} fusion(bf16[3,72,4,256]{3,2,1,0:T(4,128)(2,1)} %collective-permute-done.3, bf16[3,72,64,256]{3,2,1,0:T(8,128)(2,1)} %copy-done.2, bf16[3,72,4,256]{3,2,1,0:T(4,128)(2,1)} %collective-permute-done.2), kind=kLoop, calls=%fused_computation.15 | loop fusion | flops 23887872 | bytes 15925248 | tf_op jit(solution)/shard_map/concatenate | solution.py:116
  194.1 107.0 %shard_map.119 = f32[3,64,64,256]{3,2,1,0:T(8,128)} custom-call(bf16[3,72,72,256]{3,2,1,0:T(8,128)(2,1)} %fusion.4.ext_ref, f32[81,256]{1,0:T(8,128)S(1)} %fusion.9.w_ref), custom_call_target="tpu_custom_call" | custom-call | tf_op jit(solution)/shard_map/pallas_call | solution.py:73
  301.1 6.3 %multiply_reduce_fusion.2 = f32[3,64,64]{2,1,0:T(8,128)S(1)} fusion(f32[3,64,64,256]{3,2,1,0:T(8,128)} %shard_map.119), kind=kLoop, calls=%fused_computation.12 | loop fusion | flops 6279168 | bytes 12632064 | tf_op jit(solution)/shard_map/reduce_sum | solution.py:258
  307.5 8.6 %multiply_convert_fusion.2 = bf16[12288,256]{1,0:T(8,128)(2,1)} fusion(f32[3,64,64,256]{3,2,1,0:T(8,128)} %shard_map.119, f32[256]{0:T(256)S(1)} %convert_element_type.12, f32[12288]{0:T(1024)S(1)} %rsqrt.12), kind=kLoop, calls=%fused_computation.11 | loop fusion | flops 9437184 | bytes 18924544 | tf_op jit(solution)/shard_map/convert_element_type | solution.py:262
  316.1 29.7 %multiply_convert_fusion.1 = (bf16[12288,1024]{1,0:T(8,128)(2,1)}, f32[12288,1024]{1,0:T(8,128)}) fusion(bf16[12288,256]{1,0:T(8,128)(2,1)} %multiply_convert_fusion.2, bf16[256,1024]{1,0:T(8,128)(2,1)S(1)} %copy-done), kind=kOutput, calls=%fused_computation.1 | convolution fusion | flops 6505365504 | bytes 82313216 | tf_op jit(solution)/shard_map/dot_general | solution.py:263
  345.8 33.4 %multiply_convert_fusion = bf16[12288,1024]{1,0:T(8,128)(2,1)} fusion(f32[12288,1024]{1,0:T(8,128)} %get-tuple-element.128, bf16[12288,256]{1,0:T(8,128)(2,1)} %bitcast.178, bf16[1024,256]{1,0:T(8,128)(2,1)S(1)} %copy-done.12), kind=kOutput, calls=%fused_computation | convolution fusion | flops 6555697152 | bytes 82313216 | tf_op jit(solution)/shard_map/dot_general | solution.py:273
  379.2 14.2 %fusion.15 = f32[256,1024]{1,0:T(8,128)} fusion(bf16[12288,256]{1,0:T(8,128)(2,1)} %multiply_convert_fusion.2, bf16[12288,1024]{1,0:T(8,128)(2,1)} %multiply_convert_fusion), kind=kOutput, calls=%fused_computation.108 | convolution fusion | flops 6442450944 | bytes 32505856 | tf_op jit(solution)/shard_map/dot_general | solution.py:277
  393.4 18.7 %multiply_reduce_fusion = (f32[256]{0:T(256)S(1)}, f32[12288]{0:T(1024)S(1)}, f32[12288,256]{1,0:T(8,128)}) fusion(f32[3,64,64,256]{3,2,1,0:T(8,128)} %shard_map.119, f32[12288]{0:T(1024)S(1)} %copy-done.7, f32[256]{0:T(256)S(1)} %copy-done.9, bf16[12288,1024]{1,0:T(8,128)(2,1)} %multiply_convert_fusion, bf16[256,1024]{1,0:T(8,128)(2,1)S(1)} %copy-done), kind=kOutput, calls=%fused_computation.8 | convolution fusion | flops 6461313024 | bytes 50956288 | tf_op jit(solution)/shard_map/dot_general | solution.py:280
  412.1 13.7 %fusion.16 = f32[1024,256]{1,0:T(8,128)S(1)} fusion(bf16[12288,1024]{1,0:T(8,128)(2,1)} %get-tuple-element.127, bf16[12288,256]{1,0:T(8,128)(2,1)} %bitcast.179), kind=kOutput, calls=%fused_computation.109 | convolution fusion | flops 6442450944 | bytes 32505856 | tf_op jit(solution)/shard_map/dot_general | solution.py:270
  426.8 16.6 %subtract_multiply_fusion = f32[12288,256]{1,0:T(8,128)} fusion(f32[12288,256]{1,0:T(8,128)} %get-tuple-element.129, f32[3,64,64,256]{3,2,1,0:T(8,128)} %shard_map.119, f32[12288]{0:T(1024)S(1)} %broadcast_multiply_fusion, f32[256]{0:T(256)S(1)} %copy-done.9, f32[12288]{0:T(1024)S(1)} %copy-done.7), kind=kLoop, calls=%fused_computation.9 | loop fusion | flops 15728640 | bytes 37848064 | tf_op jit(solution)/shard_map/mul | solution.py:290
  443.5 109.5 %shard_map.120 = f32[81,8,256]{2,1,0:T(8,128)S(1)} custom-call(bf16[3,72,72,256]{3,2,1,0:T(8,128)(2,1)} %fusion.4.ext_ref, f32[3,64,64,256]{3,2,1,0:T(8,128)} %bitcast.167), custom_call_target="tpu_custom_call" | custom-call | tf_op jit(solution)/shard_map/pallas_call | solution.py:93
  553.3 8.2 %all-reduce.4.cloned.1.call-done = (f32[256,1024]{1,0:T(8,128)}, f32[1025,256]{1,0:T(8,128)}) async-done(((f32[256,1024]{1,0:T(8,128)}, f32[1025,256]{1,0:T(8,128)}), (f32[256,1024]{1,0:T(8,128)}, f32[1025,256]{1,0:T(8,128)})) %all-reduce.4.cloned.1.call-update) | async-done | bytes 2098192 | tf_op jit(solution)/shard_map/psum | solution.py:283
  563.0 2.8 collective-permute-done.4
  565.8 2.4 collective-permute-start.5
  570.5 2.5 collective-permute-start.6
  573.1 2.7 collective-permute-done.6
  578.6 13.3 %convolution_convert_fusion = bf16[12288,256]{1,0:T(8,128)(2,1)} fusion(bf16[12288,1024]{1,0:T(8,128)(2,1)} %get-tuple-element.127, bf16[1024,256]{1,0:T(8,128)(2,1)S(1)} %copy-done.12), kind=kOutput, calls=%fused_computation.5 | convolution fusion | flops 6445596672 | bytes 31981568 | tf_op jit(solution)/shard_map/dot_general | solution.py:266
  (113 shorter events, 55.8 us)
Async XLA Ops:
  7.2 309.0 %copy-start = (bf16[256,1024]{1,0:T(8,128)(2,1)S(1)}, bf16[256,1024]{1,0:T(8,128)(2,1)}, u32[]{:S(2)}) copy-start(bf16[256,1024]{1,0:T(8,128)(2,1)} %param.21) | copy-start | bytes 1572868
  7.2 112.0 %all-gather.7.cloned.1.call-start = ((), (), s32[]{:S(2)}) async-start(), calls=%async_computation.5 | async-start | bytes 3342336 | tf_op jit(solution)/shard_map/all_gather | solution.py:178
  21.4 101.9 %all-gather.5.cloned.1.call-start = ((), (), s32[]{:S(2)}) async-start(), calls=%async_computation.4 | async-start | bytes 3342336 | tf_op jit(solution)/shard_map/all_gather | solution.py:175
  46.7 61.5 %collective-permute-start = (bf16[3,4,64,256]{3,2,1,0:T(8,128)(2,1)S(1)}, bf16[3,4,64,256]{3,2,1,0:T(8,128)(2,1)S(1)}, u32[]{:S(2)}, u32[]{:S(2)}) collective-permute-start(bf16[3,4,64,256]{3,2,1,0:T(8,128)(2,1)S(1)} %slice.340), channel_id=1, source_target_pairs={{0,4},{4,8},{8,12},{1,5},{5,9},{9,13},{2,6},{6,10},{10,14},{3,7},{... | collective-permute-start | bytes 1179656 | tf_op jit(solution)/shard_map/ppermute | solution.py:118
  48.6 63.0 %collective-permute-start.1 = (bf16[3,4,64,256]{3,2,1,0:T(8,128)(2,1)S(1)}, bf16[3,4,64,256]{3,2,1,0:T(8,128)(2,1)S(1)}, u32[]{:S(2)}, u32[]{:S(2)}) collective-permute-start(bf16[3,4,64,256]{3,2,1,0:T(8,128)(2,1)S(1)} %get-tuple-element.78), channel_id=1, source_target_pairs={{4,0},{8,4},{12,8},{5,1},{9,5},{13,9},{6,2},{10,6},{14,10},{7,3},{... | collective-permute-start | bytes 1179656 | tf_op jit(solution)/shard_map/ppermute | solution.py:120
  98.9 208.6 %copy-start.8 = (f32[256]{0:T(256)}, f32[256]{0:T(256)S(1)}, u32[]{:S(2)}) copy-start(f32[256]{0:T(256)S(1)} %convert_element_type.12) | copy-start | bytes 3076
  107.1 18.5 %copy-start.10 = (s32[64]{0:T(128)}, s32[64]{0:T(128)S(1)}, u32[]{:S(2)}) copy-start(s32[64]{0:T(128)S(1)} %add_bitcast_fusion) | copy-start | bytes 772
  111.7 2.9 copy-start.2
  115.8 57.2 %collective-permute-start.2 = (bf16[3,72,4,256]{3,2,1,0:T(4,128)(2,1)}, bf16[3,72,4,256]{3,2,1,0:T(4,128)(2,1)}, u32[]{:S(2)}, u32[]{:S(2)}) collective-permute-start(bf16[3,72,4,256]{3,2,1,0:T(4,128)(2,1)} %get-tuple-element.63), channel_id=1, source_target_pairs={{0,1},{1,2},{2,3},{4,5},{5,6},{6,7},{8,9},{9,10},{10,11},{12,13},{... | collective-permute-start | bytes 1327112 | tf_op jit(solution)/shard_map/ppermute | solution.py:118
  117.8 55.1 %collective-permute-start.3 = (bf16[3,72,4,256]{3,2,1,0:T(4,128)(2,1)}, bf16[3,72,4,256]{3,2,1,0:T(4,128)(2,1)}, u32[]{:S(2)}, u32[]{:S(2)}) collective-permute-start(bf16[3,72,4,256]{3,2,1,0:T(4,128)(2,1)} %get-tuple-element.64), channel_id=1, source_target_pairs={{1,0},{2,1},{3,2},{5,4},{6,5},{7,6},{9,8},{10,9},{11,10},{13,12},{... | collective-permute-start | bytes 1327112 | tf_op jit(solution)/shard_map/ppermute | solution.py:120
  129.6 2.8 copy-start.1
  152.6 16.6 %all-to-all-start.3 = ((bf16[6,4,72,256]{3,2,1,0:T(8,128)(2,1)}), bf16[6,4,72,256]{3,2,1,0:T(8,128)(2,1)S(1)}, u32[]{:S(2)}, u32[]{:S(2)}) async-start(bf16[6,4,72,256]{3,2,1,0:T(8,128)(2,1)} %bitcast_dynamic-update-slice_fusion), calls=%async_computation.3 | async-start | bytes 1769472 | tf_op jit(solution)/shard_map/all_to_all | solution.py:231
  158.4 0.9 copy-start.3
  169.2 15.9 %all-to-all-start.2 = ((bf16[6,4,72,256]{3,2,1,0:T(8,128)(2,1)}), bf16[6,4,72,256]{3,2,1,0:T(8,128)(2,1)S(1)}, u32[]{:S(2)}, u32[]{:S(2)}) async-start(bf16[6,4,72,256]{3,2,1,0:T(8,128)(2,1)} %copy-done.3), calls=%async_computation.2 | async-start | bytes 1769472 | tf_op jit(solution)/shard_map/all_to_all | solution.py:230
  172.7 388.8 %all-reduce.4.cloned.1.call-start = ((), (), s32[]{:S(2)}) async-start(), calls=%async_computation.6 | async-start | bytes 4210688 | tf_op jit(solution)/shard_map/psum | solution.py:283
  307.5 38.3 %copy-start.6 = (f32[12288]{0:T(1024)}, f32[12288]{0:T(1024)S(1)}, u32[]{:S(2)}) copy-start(f32[12288]{0:T(1024)S(1)} %rsqrt.12) | copy-start | bytes 147460
  316.1 29.7 %copy-start.12 = (bf16[1024,256]{1,0:T(8,128)(2,1)S(1)}, bf16[1024,256]{1,0:T(8,128)(2,1)}, u32[]{:S(2)}) copy-start(bf16[1024,256]{1,0:T(8,128)(2,1)} %param.22) | copy-start | bytes 1572868
  379.2 14.2 %copy-start.7 = (f32[12288]{0:T(1024)S(1)}, f32[12288]{0:T(1024)}, u32[]{:S(2)}) copy-start(f32[12288]{0:T(1024)} %copy-done.6) | copy-start | bytes 147460
  379.2 14.2 %copy-start.9 = (f32[256]{0:T(256)S(1)}, f32[256]{0:T(256)}, u32[]{:S(2)}) copy-start(f32[256]{0:T(256)} %copy-done.8) | copy-start | bytes 3076
  443.5 109.6 %copy-start.11 = (s32[64]{0:T(128)S(1)}, s32[64]{0:T(128)}, u32[]{:S(2)}) copy-start(s32[64]{0:T(128)} %copy-done.10) | copy-start | bytes 772
  561.5 4.3 collective-permute-start.4
  565.8 4.7 collective-permute-start.5
  570.5 5.2 collective-permute-start.6
  575.8 1.3 collective-permute-start.7
  577.1 14.8 %copy-start.5 = (f32[1025,256]{1,0:T(8,128)S(1)}, f32[1025,256]{1,0:T(8,128)}, u32[]{:S(2)}) copy-start(f32[1025,256]{1,0:T(8,128)} %get-tuple-element.57) | copy-start | bytes 3148804
  577.1 17.0 %copy-start.4 = (f32[256,1024]{1,0:T(8,128)S(1)}, f32[256,1024]{1,0:T(8,128)}, u32[]{:S(2)}) copy-start(f32[256,1024]{1,0:T(8,128)} %get-tuple-element.151) | copy-start | bytes 3145732
  577.1 16.4 %collective-permute-start.8 = (f32[64,256]{1,0:T(8,128)S(1)}, f32[64,256]{1,0:T(8,128)S(1)}, u32[]{:S(2)}, u32[]{:S(2)}) collective-permute-start(f32[64,256]{1,0:T(8,128)S(1)} %add.315), channel_id=1, source_target_pairs={{0,2},{1,3},{2,0},{3,1},{4,6},{5,7},{6,4},{7,5},{8,10},{9,11},{10,... | collective-permute-start | bytes 196616 | tf_op jit(solution)/shard_map/ppermute | solution.py:313
Sparse Core Ops, SparseCore 0:
  21.5 52.5 all-gather.6
  77.0 43.7 all-gather.4
  427.0 134.5 all-reduce.3

commit v3 on v2

--- a/solution.py
+++ b/solution.py
@@ -13,6 +13,7 @@
     rows = out_ref.shape[1]
     cols = out_ref.shape[2]
     ext_rows = ext_ref.shape[1]
+    row_block = 4 if rows % 4 == 0 else 1
     for dj in range(BOX):
         def shift_row(r, carry):
             shift_ref[r] = ext_ref[0, r, pl.ds(dj, cols), :].astype(jnp.float32)
@@ -21,49 +22,22 @@
         lax.fori_loop(0, ext_rows, shift_row, 0)
         weights = [w_ref[pl.ds(di * BOX + dj, 1), :] for di in range(BOX)]
 
-        def out_row(i, carry):
+        def out_rows(block_index, carry):
+            first = block_index * row_block
             if dj == 0:
-                acc = jnp.zeros((cols, out_ref.shape[3]), jnp.float32)
+                accs = [jnp.zeros((cols, out_ref.shape[3]), jnp.float32) for _ in range(row_block)]
             else:
-                acc = out_ref[0, i]
-            for di in range(BOX):
-                acc = acc + weights[di] * shift_ref[i + di]
-            out_ref[0, i] = acc
+                accs = [out_ref[0, first + q] for q in range(row_block)]
+            for t in range(BOX + row_block - 1):
+                window = shift_ref[first + t]
+                for q in range(row_block):
+                    if 0 <= t - q < BOX:
+                        accs[q] = accs[q] + weights[t - q] * window
+            for q in range(row_block):
+                out_ref[0, first + q] = accs[q]
             return carry
 
-        lax.fori_loop(0, rows, out_row, 0)
-
-
-def _bwd_kernel(ext_ref, g_ref, out_ref, shift_ref):
-    rows = g_ref.shape[1]
-    cols = g_ref.shape[2]
-    chans = g_ref.shape[3]
-    ext_rows = ext_ref.shape[1]
-
-    @pl.when(pl.program_id(0) == 0)
-    def _():
-        out_ref[...] = jnp.zeros_like(out_ref)
-
-    for dj in range(BOX):
-        def shift_row(r, carry):
-            shift_ref[r] = ext_ref[0, r, pl.ds(dj, cols), :].astype(jnp.float32)
-            return carry
-
-        lax.fori_loop(0, ext_rows, shift_row, 0)
-
-        def grad_row(i, accs):
-            g = g_ref[0, i]
-            new = []
-            for di in range(BOX):
-                p = g * shift_ref[i + di]
-                p = p.reshape(cols // 8, 8, chans).sum(axis=0)
-                new.append(accs[di] + p)
-            return tuple(new)
-
-        init = tuple(jnp.zeros((8, chans), jnp.float32) for _ in range(BOX))
-        accs = lax.fori_loop(0, rows, grad_row, init)
-        for di in range(BOX):
-            out_ref[di * BOX + dj] = out_ref[di * BOX + dj] + accs[di]
+        lax.fori_loop(0, rows // row_block, out_rows, 0)
 
 
 def stencil_forward(ext, box_weights):
@@ -86,24 +60,69 @@
     )(ext, box_weights)
 
 
-def stencil_backward(ext, agg_grad):
+def _fill_slabs(ext_ref, slab_ref, first_row):
+    cols = slab_ref.shape[2]
+    for dj in range(BOX):
+        def shift_row(r, carry):
+            slab_ref[dj, r] = ext_ref[0, first_row + r, pl.ds(dj, cols), :].astype(jnp.float32)
+            return carry
+
+        lax.fori_loop(0, slab_ref.shape[1], shift_row, 0)
+
+
+def _bwd_kernel(off_ref, ext_ref, g_ref, out_ref, slab_ref):
+    rows, cols, chans = g_ref.shape[1], g_ref.shape[2], g_ref.shape[3]
+    block = slab_ref.shape[1] - 2 * RADIUS
+
+    @pl.when(pl.program_id(0) == 0)
+    def _():
+        out_ref[...] = jnp.zeros_like(out_ref)
+
+    for first_row in range(0, rows, block):
+        _fill_slabs(ext_ref, slab_ref, first_row)
+
+        def grad_row(i, carry):
+            g = g_ref[0, first_row + i]
+            for tap in range(out_ref.shape[0]):
+                di = off_ref[2 * tap] + RADIUS
+                dj = off_ref[2 * tap + 1] + RADIUS
+                p = (g * slab_ref[dj, i + di]).reshape(cols // 8, 8, chans).sum(axis=0)
+                out_ref[tap] = out_ref[tap] + p
+            return carry
+
+        lax.fori_loop(0, block, grad_row, 0)
+
+
+def _slab_block(rows):
+    block = min(rows, 32)
+    while rows % block:
+        block -= 1
+    return block
+
+
+def stencil_backward(offsets, ext, agg_grad):
     faces, ext_rows, ext_cols, chans = ext.shape
     rows = ext_rows - 2 * RADIUS
     cols = ext_cols - 2 * RADIUS
+    taps = offsets.shape[0]
+    block = _slab_block(rows)
     partial = pl.pallas_call(
         _bwd_kernel,
-        grid=(faces,),
-        in_specs=[
-            pl.BlockSpec((1, ext_rows, ext_cols, chans), lambda f: (f, 0, 0, 0)),
-            pl.BlockSpec((1, rows, cols, chans), lambda f: (f, 0, 0, 0)),
-        ],
-        out_specs=pl.BlockSpec((BOX * BOX, 8, chans), lambda f: (0, 0, 0)),
-        out_shape=jax.ShapeDtypeStruct((BOX * BOX, 8, chans), jnp.float32),
-        scratch_shapes=[pltpu.VMEM((ext_rows, cols, chans), jnp.float32)],
+        grid_spec=pltpu.PrefetchScalarGridSpec(
+            num_scalar_prefetch=1,
+            grid=(faces,),
+            in_specs=[
+                pl.BlockSpec((1, ext_rows, ext_cols, chans), lambda f, o: (f, 0, 0, 0)),
+                pl.BlockSpec((1, rows, cols, chans), lambda f, o: (f, 0, 0, 0)),
+            ],
+            out_specs=pl.BlockSpec((taps, 8, chans), lambda f, o: (0, 0, 0)),
+            scratch_shapes=[pltpu.VMEM((BOX, block + 2 * RADIUS, cols, chans), jnp.float32)],
+        ),
+        out_shape=jax.ShapeDtypeStruct((taps, 8, chans), jnp.float32),
         compiler_params=pltpu.CompilerParams(
-            dimension_semantics=("arbitrary",), vmem_limit_bytes=48 * 1024 * 1024
+            dimension_semantics=("arbitrary",), vmem_limit_bytes=56 * 1024 * 1024
         ),
-    )(ext, agg_grad)
+    )(offsets.reshape(-1), ext, agg_grad)
     return jnp.sum(partial, axis=1)
 
 
@@ -291,8 +310,7 @@
         scaled_grad - normalized * jnp.mean(scaled_grad * normalized, axis=-1, keepdims=True)
     )
     aggregated_grad = aggregated_grad.reshape(local_count, rows_dev, cols_dev, channels)
-    box_grads = stencil_backward(extended, aggregated_grad)
-    stencil_grad = jnp.dot(onehot, box_grads, precision=lax.Precision.HIGHEST)
+    stencil_grad = stencil_backward(offsets, extended, aggregated_grad)
     stencil_grad, w_in_grad, out_and_gain = lax.optimization_barrier(
         (stencil_grad, w_in_grad, out_and_gain)
     )

time: 609 us -> 590 us (0.969)
  Pallas kernels: 216 us -> 176 us
  waiting for transfers between devices: 28.1 us -> 45.7 us
    pallas_call x1, Pallas kernels: 109 us -> 81.7 us  [stencil_backward(): pl.pallas_call(_bwd_kernel, grid_spec=pltpu.PrefetchScalarGridSpec(num_sc...]
    psum x1, waiting for transfers between devices: 8.18 us -> 35.1 us  [shards(): lax.psum((w_in_grad, jnp.concatenate([w_out_grad, gain_grad[None, :]], ax...]
    pallas_call x1, Pallas kernels: 107 us -> 94.5 us  [stencil_forward(): pl.pallas_call(_fwd_kernel, grid=(faces,), in_specs=[pl.BlockSpec((1, ext...]
    all_to_all x1, waiting for transfers between devices: 9.9 us -> 0.01 us  [shards(): lax.all_to_all(jnp.stack(down_list), 'face', split_axis=0, concat_axis=0,...]
  transfers between devices with their start and end apart: 14 -> 14, of which waited for: 7 -> 6; matrix products, arithmetic and copies ran while one was open for 15% -> 16% of each run, Pallas kernels for 18% -> 14%
where the time goes in v3:
time: 590 us; the launch traced here: 583 us
  Pallas kernels  176 us (30%)
  matrix products  122 us (21%)
  other arithmetic  69.1 us (12%)
  between operations  67.7 us (11%)
  local copies, waits for them, and re-layouts  46.2 us (8%)
  waiting for transfers between devices  45.7 us (8%)
  blocking collectives  33.8 us (6%)
  starting transfers between devices  21.9 us (4%)
    pallas_call x1, Pallas kernels, stencil_forward(): pl.pallas_call(_fwd_kernel, grid=(faces,), in_specs=[pl.BlockSpec((1, ext...  94.5 us
    pallas_call x1, Pallas kernels, stencil_backward(): pl.pallas_call(_bwd_kernel, grid_spec=pltpu.PrefetchScalarGridSpec(num_sc...  81.7 us
    psum x1, waiting for transfers between devices, shards(): lax.psum((w_in_grad, jnp.concatenate([w_out_grad, gain_grad[None, :]], ax...  35.1 us
    dot_general x1, matrix products, shards(): lax.dot_general(target_rows, w_out, contract_cols, preferred_element_type...  33.4 us
    dot_general x1, matrix products, shards(): pre_act = jnp.dot(hidden_in, w_in, preferred_element_type=jnp.float32)  29.7 us
    all_to_all x1, blocking collectives, shards(): lax.all_to_all(across.reshape(local_count, radius_cells, row_count, sub_a...  22.3 us
    dot_general x1, matrix products, shards(): lax.dot_general(pre_grad, w_in, contract_cols, preferred_element_type=jnp...  18.7 us
    mul x1, other arithmetic, shards(): inverse_rms * (scaled_grad - normalized * jnp.mean(scaled_grad * normaliz...  16.6 us
  transfers between devices with their start and end apart: 14, of which 6 were waited for; matrix products, arithmetic and copies ran while one was open for 16% of the time, Pallas kernels for 14%

profile of v3, /device:TPU:0, one launch (start us, length us, event | category | flops | bytes accessed | tf_op | source)
XLA Modules:
  0.0 582.8 jit_solution(1155379250215240078)
XLA Ops:
  9.2 11.5 %all_to_all.20 = bf16[3,4,4,16,256]{4,3,1,0,2:T(8,128)(2,1)S(1)} all-to-all(bf16[3,4,4,16,256]{4,3,1,0,2:T(8,128)(2,1)S(1)} %copy.59), channel_id=1, replica_groups=mesh['face'=2,'row'=4,'col'=4] {'col'}, dimensions={2} | all-to-all | bytes 786432 | tf_op jit(solution)/shard_map/all_to_all | solution.py:185
  23.7 22.3 %all_to_all.21 = bf16[3,4,4,16,256]{4,3,1,0,2:T(8,128)(2,1)S(1)} all-to-all(bf16[3,4,4,16,256]{4,3,1,0,2:T(8,128)(2,1)S(1)} %copy.54), channel_id=1, replica_groups=mesh['face'=2,'row'=4,'col'=4] {'row'}, dimensions={2} | all-to-all | bytes 786432 | tf_op jit(solution)/shard_map/all_to_all | solution.py:178
  109.9 3.4 constant_dynamic-update-slice_fusion.1
  113.3 2.9 copy-done.2
  120.8 4.0 copy.61
  127.2 3.9 fusion.3
  131.2 2.8 copy-done.1
  140.0 3.6 all-to-all-start.3
  145.0 2.5 rev.54
  147.5 2.5 rev.55
  150.0 2.5 rev.56
  152.5 2.5 rev.57
  155.0 2.5 rev.58
  163.6 3.6 all-to-all-start.2
  167.4 8.8 %pad_maximum_fusion = bf16[3,72,72,256]{3,2,1,0:T(8,128)(2,1)} fusion(bf16[3,72,4,256]{3,2,1,0:T(4,128)(2,1)} %collective-permute-done.3, bf16[3,72,64,256]{3,2,1,0:T(8,128)(2,1)} %copy-done.2, bf16[3,72,4,256]{3,2,1,0:T(4,128)(2,1)} %collective-permute-done.2), kind=kLoop, calls=%fused_computation.15 | loop fusion | flops 23887872 | bytes 15925248 | tf_op jit(solution)/shard_map/concatenate | solution.py:135
  186.7 2.4 fusion.4.ext_ref
  189.1 94.5 %shard_map.119 = f32[3,64,64,256]{3,2,1,0:T(8,128)} custom-call(bf16[3,72,72,256]{3,2,1,0:T(8,128)(2,1)} %fusion.4.ext_ref, f32[81,256]{1,0:T(8,128)S(1)} %fusion.8.w_ref), custom_call_target="tpu_custom_call" | custom-call | tf_op jit(solution)/shard_map/pallas_call | solution.py:47
  283.5 6.3 %multiply_reduce_fusion.2 = f32[3,64,64]{2,1,0:T(8,128)S(1)} fusion(f32[3,64,64,256]{3,2,1,0:T(8,128)} %shard_map.119), kind=kLoop, calls=%fused_computation.12 | loop fusion | flops 6279168 | bytes 12632064 | tf_op jit(solution)/shard_map/reduce_sum | solution.py:277
  289.9 8.6 %multiply_convert_fusion.2 = bf16[12288,256]{1,0:T(8,128)(2,1)} fusion(f32[3,64,64,256]{3,2,1,0:T(8,128)} %shard_map.119, f32[256]{0:T(256)S(1)} %convert_element_type.12, f32[12288]{0:T(1024)S(1)} %rsqrt.12), kind=kLoop, calls=%fused_computation.11 | loop fusion | flops 9437184 | bytes 18924544 | tf_op jit(solution)/shard_map/convert_element_type | solution.py:281
  298.6 29.7 %multiply_convert_fusion.1 = (bf16[12288,1024]{1,0:T(8,128)(2,1)}, f32[12288,1024]{1,0:T(8,128)}) fusion(bf16[12288,256]{1,0:T(8,128)(2,1)} %multiply_convert_fusion.2, bf16[256,1024]{1,0:T(8,128)(2,1)S(1)} %copy-done), kind=kOutput, calls=%fused_computation.1 | convolution fusion | flops 6505365504 | bytes 82313216 | tf_op jit(solution)/shard_map/dot_general | solution.py:282
  328.3 33.4 %multiply_convert_fusion = bf16[12288,1024]{1,0:T(8,128)(2,1)} fusion(f32[12288,1024]{1,0:T(8,128)} %get-tuple-element.128, bf16[12288,256]{1,0:T(8,128)(2,1)} %bitcast.177, bf16[1024,256]{1,0:T(8,128)(2,1)S(1)} %copy-done.11), kind=kOutput, calls=%fused_computation | convolution fusion | flops 6555697152 | bytes 82313216 | tf_op jit(solution)/shard_map/dot_general | solution.py:292
  361.7 18.7 %multiply_reduce_fusion = (f32[256]{0:T(256)S(1)}, f32[12288]{0:T(1024)S(1)}, f32[12288,256]{1,0:T(8,128)}) fusion(f32[3,64,64,256]{3,2,1,0:T(8,128)} %shard_map.119, f32[12288]{0:T(1024)S(1)} %copy-done.7, f32[256]{0:T(256)S(1)} %copy-done.9, bf16[12288,1024]{1,0:T(8,128)(2,1)} %multiply_convert_fusion, bf16[256,1024]{1,0:T(8,128)(2,1)S(1)} %copy-done), kind=kOutput, calls=%fused_computation.8 | convolution fusion | flops 6461313024 | bytes 50956288 | tf_op jit(solution)/shard_map/dot_general | solution.py:299
  380.4 14.3 %fusion.13 = f32[256,1024]{1,0:T(8,128)} fusion(bf16[12288,256]{1,0:T(8,128)(2,1)} %multiply_convert_fusion.2, bf16[12288,1024]{1,0:T(8,128)(2,1)} %multiply_convert_fusion), kind=kOutput, calls=%fused_computation.106 | convolution fusion | flops 6442450944 | bytes 32505856 | tf_op jit(solution)/shard_map/dot_general | solution.py:296
  394.7 11.8 %fusion.14 = f32[1024,256]{1,0:T(8,128)S(1)} fusion(bf16[12288,1024]{1,0:T(8,128)(2,1)} %get-tuple-element.127, bf16[12288,256]{1,0:T(8,128)(2,1)S(1)} %bitcast.178), kind=kOutput, calls=%fused_computation.107 | convolution fusion | flops 6442450944 | bytes 32505856 | tf_op jit(solution)/shard_map/dot_general | solution.py:289
  407.7 16.6 %subtract_multiply_fusion = f32[12288,256]{1,0:T(8,128)} fusion(f32[12288,256]{1,0:T(8,128)} %get-tuple-element.129, f32[3,64,64,256]{3,2,1,0:T(8,128)} %shard_map.119, f32[12288]{0:T(1024)S(1)} %broadcast_multiply_fusion, f32[256]{0:T(256)S(1)} %copy-done.9, f32[12288]{0:T(1024)S(1)} %copy-done.7), kind=kLoop, calls=%fused_computation.9 | loop fusion | flops 15728640 | bytes 37848064 | tf_op jit(solution)/shard_map/mul | solution.py:309
  424.3 81.7 %shard_map.120 = f32[64,8,256]{2,1,0:T(8,128)} custom-call(s32[128]{0:T(128)} %reshape.422.off_ref, bf16[3,72,72,256]{3,2,1,0:T(8,128)(2,1)} %fusion.4.ext_ref, f32[3,64,64,256]{3,2,1,0:T(8,128)} %bitcast.166), custom_call_target="tpu_custom_call" | custom-call | tf_op jit(solution)/shard_map/pallas_call | solution.py:109
  507.1 35.1 %all-reduce.4.cloned.1.call-done = (f32[256,1024]{1,0:T(8,128)}, f32[1025,256]{1,0:T(8,128)}) async-done(((f32[256,1024]{1,0:T(8,128)}, f32[1025,256]{1,0:T(8,128)}), (f32[256,1024]{1,0:T(8,128)}, f32[1025,256]{1,0:T(8,128)})) %all-reduce.4.cloned.1.call-update) | async-done | bytes 2098192 | tf_op jit(solution)/shard_map/psum | solution.py:302
  543.7 2.8 collective-permute-done.4
  546.5 2.4 collective-permute-start.5
  551.3 2.5 collective-permute-start.6
  553.8 2.7 collective-permute-done.6
  559.3 13.3 %convolution_convert_fusion = bf16[12288,256]{1,0:T(8,128)(2,1)} fusion(bf16[12288,1024]{1,0:T(8,128)(2,1)} %get-tuple-element.127, bf16[1024,256]{1,0:T(8,128)(2,1)S(1)} %copy-done.11), kind=kOutput, calls=%fused_computation.5 | convolution fusion | flops 6445596672 | bytes 31981568 | tf_op jit(solution)/shard_map/dot_general | solution.py:285
  (112 shorter events, 59.0 us)
Async XLA Ops:
  7.2 291.4 %copy-start = (bf16[256,1024]{1,0:T(8,128)(2,1)S(1)}, bf16[256,1024]{1,0:T(8,128)(2,1)}, u32[]{:S(2)}) copy-start(bf16[256,1024]{1,0:T(8,128)(2,1)} %param.21) | copy-start | bytes 1572868
  7.2 113.7 %all-gather.7.cloned.1.call-start = ((), (), s32[]{:S(2)}) async-start(), calls=%async_computation.5 | async-start | bytes 3342336 | tf_op jit(solution)/shard_map/all_gather | solution.py:197
  21.4 103.5 %all-gather.5.cloned.1.call-start = ((), (), s32[]{:S(2)}) async-start(), calls=%async_computation.4 | async-start | bytes 3342336 | tf_op jit(solution)/shard_map/all_gather | solution.py:194
  46.7 63.1 %collective-permute-start = (bf16[3,4,64,256]{3,2,1,0:T(8,128)(2,1)S(1)}, bf16[3,4,64,256]{3,2,1,0:T(8,128)(2,1)S(1)}, u32[]{:S(2)}, u32[]{:S(2)}) collective-permute-start(bf16[3,4,64,256]{3,2,1,0:T(8,128)(2,1)S(1)} %slice.340), channel_id=1, source_target_pairs={{0,4},{4,8},{8,12},{1,5},{5,9},{9,13},{2,6},{6,10},{10,14},{3,7},{... | collective-permute-start | bytes 1179656 | tf_op jit(solution)/shard_map/ppermute | solution.py:137
  48.6 64.6 %collective-permute-start.1 = (bf16[3,4,64,256]{3,2,1,0:T(8,128)(2,1)S(1)}, bf16[3,4,64,256]{3,2,1,0:T(8,128)(2,1)S(1)}, u32[]{:S(2)}, u32[]{:S(2)}) collective-permute-start(bf16[3,4,64,256]{3,2,1,0:T(8,128)(2,1)S(1)} %get-tuple-element.78), channel_id=1, source_target_pairs={{4,0},{8,4},{12,8},{5,1},{9,5},{13,9},{6,2},{10,6},{14,10},{7,3},{... | collective-permute-start | bytes 1179656 | tf_op jit(solution)/shard_map/ppermute | solution.py:139
  99.1 190.9 %copy-start.8 = (f32[256]{0:T(256)}, f32[256]{0:T(256)S(1)}, u32[]{:S(2)}) copy-start(f32[256]{0:T(256)S(1)} %convert_element_type.12) | copy-start | bytes 3076
  113.3 2.9 copy-start.2
  117.5 49.9 %collective-permute-start.2 = (bf16[3,72,4,256]{3,2,1,0:T(4,128)(2,1)}, bf16[3,72,4,256]{3,2,1,0:T(4,128)(2,1)}, u32[]{:S(2)}, u32[]{:S(2)}) collective-permute-start(bf16[3,72,4,256]{3,2,1,0:T(4,128)(2,1)} %get-tuple-element.63), channel_id=1, source_target_pairs={{0,1},{1,2},{2,3},{4,5},{5,6},{6,7},{8,9},{9,10},{10,11},{12,13},{... | collective-permute-start | bytes 1327112 | tf_op jit(solution)/shard_map/ppermute | solution.py:137
  119.5 47.9 %collective-permute-start.3 = (bf16[3,72,4,256]{3,2,1,0:T(4,128)(2,1)}, bf16[3,72,4,256]{3,2,1,0:T(4,128)(2,1)}, u32[]{:S(2)}, u32[]{:S(2)}) collective-permute-start(bf16[3,72,4,256]{3,2,1,0:T(4,128)(2,1)} %get-tuple-element.64), channel_id=1, source_target_pairs={{1,0},{2,1},{3,2},{5,4},{6,5},{7,6},{9,8},{10,9},{11,10},{13,12},{... | collective-permute-start | bytes 1327112 | tf_op jit(solution)/shard_map/ppermute | solution.py:139
  131.2 2.8 copy-start.1
  140.0 23.6 %all-to-all-start.3 = ((bf16[6,4,72,256]{3,2,1,0:T(8,128)(2,1)}), bf16[6,4,72,256]{3,2,1,0:T(8,128)(2,1)S(1)}, u32[]{:S(2)}, u32[]{:S(2)}) async-start(bf16[6,4,72,256]{3,2,1,0:T(8,128)(2,1)} %bitcast_dynamic-update-slice_fusion), calls=%async_computation.3 | async-start | bytes 1769472 | tf_op jit(solution)/shard_map/all_to_all | solution.py:250
  162.7 0.9 copy-start.3
  163.6 16.5 %all-to-all-start.2 = ((bf16[6,4,72,256]{3,2,1,0:T(8,128)(2,1)}), bf16[6,4,72,256]{3,2,1,0:T(8,128)(2,1)S(1)}, u32[]{:S(2)}, u32[]{:S(2)}) async-start(bf16[6,4,72,256]{3,2,1,0:T(8,128)(2,1)} %copy-done.3), calls=%async_computation.2 | async-start | bytes 1769472 | tf_op jit(solution)/shard_map/all_to_all | solution.py:249
  167.2 375.1 %all-reduce.4.cloned.1.call-start = ((), (), s32[]{:S(2)}) async-start(), calls=%async_computation.6 | async-start | bytes 4210688 | tf_op jit(solution)/shard_map/psum | solution.py:302
  289.9 38.4 %copy-start.6 = (f32[12288]{0:T(1024)}, f32[12288]{0:T(1024)S(1)}, u32[]{:S(2)}) copy-start(f32[12288]{0:T(1024)S(1)} %rsqrt.12) | copy-start | bytes 147460
  298.6 29.7 %copy-start.11 = (bf16[1024,256]{1,0:T(8,128)(2,1)S(1)}, bf16[1024,256]{1,0:T(8,128)(2,1)}, u32[]{:S(2)}) copy-start(bf16[1024,256]{1,0:T(8,128)(2,1)} %param.22) | copy-start | bytes 1572868
  328.3 33.4 %copy-start.7 = (f32[12288]{0:T(1024)S(1)}, f32[12288]{0:T(1024)}, u32[]{:S(2)}) copy-start(f32[12288]{0:T(1024)} %copy-done.6) | copy-start | bytes 147460
  328.3 33.4 %copy-start.9 = (f32[256]{0:T(256)S(1)}, f32[256]{0:T(256)}, u32[]{:S(2)}) copy-start(f32[256]{0:T(256)} %copy-done.8) | copy-start | bytes 3076
  380.4 14.3 %copy-start.10 = (bf16[3,64,64,256]{3,2,1,0:T(8,128)(2,1)S(1)}, bf16[3,64,64,256]{3,2,1,0:T(8,128)(2,1)}, u32[]{:S(2)}) copy-start(bf16[3,64,64,256]{3,2,1,0:T(8,128)(2,1)} %param.23) | copy-start | bytes 18874372
  542.2 4.3 collective-permute-start.4
  546.5 4.7 collective-permute-start.5
  551.3 5.2 collective-permute-start.6
  556.5 1.3 collective-permute-start.7
  557.8 14.8 %copy-start.5 = (f32[1025,256]{1,0:T(8,128)S(1)}, f32[1025,256]{1,0:T(8,128)}, u32[]{:S(2)}) copy-start(f32[1025,256]{1,0:T(8,128)} %get-tuple-element.57) | copy-start | bytes 3148804
  557.8 17.0 %copy-start.4 = (f32[256,1024]{1,0:T(8,128)S(1)}, f32[256,1024]{1,0:T(8,128)}, u32[]{:S(2)}) copy-start(f32[256,1024]{1,0:T(8,128)} %get-tuple-element.151) | copy-start | bytes 3145732
  557.9 16.4 %collective-permute-start.8 = (f32[64,256]{1,0:T(8,128)S(1)}, f32[64,256]{1,0:T(8,128)S(1)}, u32[]{:S(2)}, u32[]{:S(2)}) collective-permute-start(f32[64,256]{1,0:T(8,128)S(1)} %add.315), channel_id=1, source_target_pairs={{0,2},{1,3},{2,0},{3,1},{4,6},{5,7},{6,4},{7,5},{8,10},{9,11},{10,... | collective-permute-start | bytes 196616 | tf_op jit(solution)/shard_map/ppermute | solution.py:331
Sparse Core Ops, SparseCore 0:
  21.5 52.5 all-gather.6
  77.0 43.8 all-gather.4
  407.8 134.4 all-reduce.3

commit v4 on v3

--- a/solution.py
+++ b/solution.py
@@ -166,7 +166,13 @@
     col_index = lax.axis_index("col")
     face_index = lax.axis_index("face")
     radius_cells = RADIUS
-    extended = with_halo(state, (("row", 1), ("col", 2)), RADIUS)
+    intra = with_halo(state, (("row", 1), ("col", 2)), RADIUS)
+    box_side = 2 * radius_cells + 1
+    box_index = (offsets[:, 0] + radius_cells) * box_side + offsets[:, 1] + radius_cells
+    onehot = (
+        box_index[:, None] == jnp.arange(box_side * box_side, dtype=jnp.int32)[None, :]
+    ).astype(jnp.float32)
+    box_weights = jnp.dot(onehot.T, stencil.astype(jnp.float32), precision=lax.Precision.HIGHEST)
     top_strip = state[:, :radius_cells]
     bottom_strip = jnp.flip(state[:, rows_dev - radius_cells :], axis=1)
     left_strip = jnp.swapaxes(state[:, :, :radius_cells], 1, 2)
@@ -191,12 +197,15 @@
     )
     own_across = jnp.stack([across_sub[:, :, 0], across_sub[:, :, row_count - 1]], axis=1)
     own_down = jnp.stack([down_sub[:, :, 0], down_sub[:, :, col_count - 1]], axis=1)
+    own_across, own_down, intra = lax.optimization_barrier((own_across, own_down, intra))
+    aggregated = stencil_forward(intra, box_weights)
     across_all = lax.all_gather(own_across, ("row", "col")).reshape(
         row_count, col_count, local_count, 2, radius_cells, sub_across, channels
     )
     down_all = lax.all_gather(own_down, ("row", "col")).reshape(
         row_count, col_count, local_count, 2, radius_cells, sub_down, channels
     )
+    across_all, down_all, aggregated = lax.optimization_barrier((across_all, down_all, aggregated))
     across_full = jnp.transpose(across_all, (2, 3, 4, 1, 0, 5, 6)).reshape(
         local_count, 2, radius_cells, face_side, channels
     )
@@ -261,17 +270,37 @@
     right_block = jnp.swapaxes(halo_down, 1, 2)
     left_part = jnp.where(col_index == 0, left_block, jnp.zeros_like(left_block))
     right_part = jnp.where(col_index == col_count - 1, right_block, jnp.zeros_like(right_block))
-    extended = extended.at[:, :radius_cells].add(top_part)
+    extended = intra.at[:, :radius_cells].add(top_part)
     extended = extended.at[:, radius_cells + rows_dev :].add(bottom_part)
     extended = extended.at[:, :, :radius_cells].add(left_part)
     extended = extended.at[:, :, radius_cells + cols_dev :].add(right_part)
-    box_side = 2 * radius_cells + 1
-    box_index = (offsets[:, 0] + radius_cells) * box_side + offsets[:, 1] + radius_cells
-    onehot = (
-        box_index[:, None] == jnp.arange(box_side * box_side, dtype=jnp.int32)[None, :]
-    ).astype(jnp.float32)
-    box_weights = jnp.dot(onehot.T, stencil.astype(jnp.float32), precision=lax.Precision.HIGHEST)
-    aggregated = stencil_forward(extended, box_weights)
+    box_flipped = jnp.transpose(box_weights.reshape(box_side, box_side, channels), (1, 0, 2)).reshape(
+        box_side * box_side, channels
+    )
+    pad_rows = jnp.zeros((local_count, 2 * radius_cells, across_len, channels), state.dtype)
+    row_bands = jnp.concatenate(
+        [
+            jnp.concatenate([top_part, pad_rows], axis=1),
+            jnp.concatenate([pad_rows, bottom_part], axis=1),
+        ],
+        axis=0,
+    )
+    row_fix = stencil_forward(row_bands, box_weights)
+    left_rows = jnp.swapaxes(left_part, 1, 2)
+    right_rows = jnp.swapaxes(right_part, 1, 2)
+    pad_cols = jnp.zeros((local_count, 2 * radius_cells, down_len, channels), state.dtype)
+    col_bands = jnp.concatenate(
+        [
+            jnp.concatenate([left_rows, pad_cols], axis=1),
+            jnp.concatenate([pad_cols, right_rows], axis=1),
+        ],
+        axis=0,
+    )
+    col_fix = jnp.swapaxes(stencil_forward(col_bands, box_flipped), 1, 2)
+    aggregated = aggregated.at[:, :radius_cells].add(row_fix[:local_count])
+    aggregated = aggregated.at[:, rows_dev - radius_cells :].add(row_fix[local_count:])
+    aggregated = aggregated.at[:, :, :radius_cells].add(col_fix[:local_count])
+    aggregated = aggregated.at[:, :, cols_dev - radius_cells :].add(col_fix[local_count:])
     cell_count = local_count * rows_dev * cols_dev
     aggregated = aggregated.reshape(cell_count, channels)
     mean_square = jnp.mean(aggregated * aggregated, axis=-1, keepdims=True)

time: 590 us -> 647 us (1.097)
  blocking collectives: 33.8 us -> 0 us
  Pallas kernels: 176 us -> 209 us
  local copies, waits for them, and re-layouts: 46.2 us -> 76 us
  starting transfers between devices: 21.9 us -> 33.9 us
  waiting for transfers between devices: 45.7 us -> 56.5 us
    all_to_all x2 -> x0, blocking collectives: 33.8 us -> none  [the longest x1 22.3 us: shards(): lax.all_to_all(across.reshape(local_count, radius_cells, row_count, sub_a...]
    pallas_call x1 -> x3, Pallas kernels: 94.5 us -> 127 us  [stencil_forward(): pl.pallas_call(_fwd_kernel, grid=(faces,), in_specs=[pl.BlockSpec((1, ext...]
    optimization_barrier x0 -> x2, local copies, waits for them, and re-layouts: none -> 17.1 us  [the longest x1 16.4 us: shards(): lax.optimization_barrier((across_all, down_all, aggregated))]
    scatter-add x0 -> x1, local copies, waits for them, and re-layouts: none -> 16.4 us  [shards(): aggregated.at[:, :, cols_dev - radius_cells:].add(col_fix[local_count:])]
    scatter-add x1 -> x5, other arithmetic: 1.96 us -> 12.2 us  [the longest x1 3.01 us: shards(): aggregated.at[:, rows_dev - radius_cells:].add(row_fix[local_count:])]
    all_to_all x0 -> x2, starting transfers between devices: none -> 10.1 us  [the longest x1 5.94 us: shards(): lax.all_to_all(across.reshape(local_count, radius_cells, row_count, sub_a...]
  transfers between devices with their start and end apart: 14 -> 16, of which waited for: 6 -> 8; matrix products, arithmetic and copies ran while one was open for 16% -> 12% of each run, Pallas kernels for 14% -> 28%
where the time goes in v4:
time: 647 us; the launch traced here: 638 us
  Pallas kernels  209 us (32%)
  matrix products  122 us (19%)
  local copies, waits for them, and re-layouts  76 us (12%)
  other arithmetic  74.6 us (12%)
  between operations  67.1 us (10%)
  waiting for transfers between devices  56.5 us (9%)
  starting transfers between devices  33.9 us (5%)
    pallas_call x3, Pallas kernels, stencil_forward(): pl.pallas_call(_fwd_kernel, grid=(faces,), in_specs=[pl.BlockSpec((1, ext...  127 us
    pallas_call x1, Pallas kernels, stencil_backward(): pl.pallas_call(_bwd_kernel, grid_spec=pltpu.PrefetchScalarGridSpec(num_sc...  81.8 us
    psum x1, waiting for transfers between devices, shards(): lax.psum((w_in_grad, jnp.concatenate([w_out_grad, gain_grad[None, :]], ax...  40.3 us
    dot_general x1, matrix products, shards(): lax.dot_general(target_rows, w_out, contract_cols, preferred_element_type...  33.2 us
    dot_general x1, matrix products, shards(): pre_act = jnp.dot(hidden_in, w_in, preferred_element_type=jnp.float32)  29.9 us
    dot_general x1, matrix products, shards(): lax.dot_general(pre_grad, w_in, contract_cols, preferred_element_type=jnp...  19.2 us
    mul x1, other arithmetic, shards(): inverse_rms * (scaled_grad - normalized * jnp.mean(scaled_grad * normaliz...  16.5 us
    optimization_barrier x1, local copies, waits for them, and re-layouts, shards(): lax.optimization_barrier((across_all, down_all, aggregated))  16.4 us
  transfers between devices with their start and end apart: 16, of which 8 were waited for; matrix products, arithmetic and copies ran while one was open for 12% of the time, Pallas kernels for 28%

profile of v4, /device:TPU:0, one launch (start us, length us, event | category | flops | bytes accessed | tf_op | source)
XLA Modules:
  0.0 638.4 jit_solution(3111798107473554551)
XLA Ops:
  9.9 4.2 all-to-all-start.1
  15.1 4.2 collective-permute-start
  22.6 5.9 all-to-all-start
  28.6 3.4 constant_dynamic-update-slice_fusion.1
  34.4 2.9 copy-done.2
  40.3 2.8 all-to-all-done
  44.9 8.8 %pad_maximum_fusion.ext_ref = bf16[3,72,72,256]{3,2,1,0:T(8,128)(2,1)} fusion(bf16[3,72,4,256]{3,2,1,0:T(4,128)(2,1)S(1)} %collective-permute-done.3, bf16[3,72,64,256]{3,2,1,0:T(8,128)(2,1)} %copy-done.2, bf16[3,72,4,256]{3,2,1,0:T(4,128)(2,1)S(1)} %collective-permute-done.2), kind=kLoop, calls=%fused_computation.15 | loop fusion | flops 23887872 | bytes 15925248 | tf_op jit(solution)/shard_map/concatenate | solution.py:135
  110.1 94.6 %shard_map.119 = f32[3,64,64,256]{3,2,1,0:T(8,128)} custom-call(bf16[3,72,72,256]{3,2,1,0:T(8,128)(2,1)} %pad_maximum_fusion.ext_ref, f32[81,256]{1,0:T(8,128)S(1)} %fusion.17.w_ref), custom_call_target="tpu_custom_call" | custom-call | tf_op jit(solution)/shard_map/pallas_call | solution.py:47
  207.9 2.6 fusion.5
  210.6 2.6 copy-done.1
  219.3 3.6 all-to-all-start.3
  240.2 3.6 all-to-all-start.2
  245.2 16.4 %copy.118 = f32[3,64,64,256]{3,1,2,0:T(8,128)} copy(f32[3,64,64,256]{3,2,1,0:T(8,128)} %shard_map.119) | data formatting | bytes 25165824 | tf_op jit(solution)/shard_map/optimization_barrier | solution.py:208
  274.7 16.0 %shard_map.120 = f32[6,4,64,256]{3,2,1,0:T(8,128)S(1)} custom-call(bf16[6,12,72,256]{3,2,1,0:T(8,128)(2,1)S(1)} %fusion.9.ext_ref, f32[81,256]{1,0:T(8,128)S(1)} %fusion.17.w_ref), custom_call_target="tpu_custom_call" | custom-call | tf_op jit(solution)/shard_map/pallas_call | solution.py:47
  290.8 16.4 %shard_map.121 = f32[6,4,64,256]{3,2,1,0:T(8,128)S(1)} custom-call(bf16[6,12,72,256]{3,2,1,0:T(8,128)(2,1)S(1)} %copy.125.ext_ref, f32[81,256]{1,0:T(8,128)S(1)} %reshape.559.w_ref), custom_call_target="tpu_custom_call" | custom-call | tf_op jit(solution)/shard_map/pallas_call | solution.py:47
  307.2 3.0 fusion.13
  310.2 3.0 fusion.12
  317.5 16.4 %copy.126 = f32[3,64,64,256]{3,2,1,0:T(8,128)} copy(f32[3,64,64,256]{3,1,2,0:T(8,128)} %fusion.10) | data formatting | bytes 25165824 | tf_op jit(solution)/shard_map/scatter-add | solution.py:303
  333.9 6.3 multiply_reduce_fusion.2
  340.4 8.6 %multiply_convert_fusion.2 = bf16[12288,256]{1,0:T(8,128)(2,1)} fusion(f32[3,64,64,256]{3,2,1,0:T(8,128)} %copy.126, f32[256]{0:T(256)S(1)} %convert_element_type.12, f32[12288]{0:T(1024)S(1)} %rsqrt.12), kind=kLoop, calls=%fused_computation.11 | loop fusion | flops 9437184 | bytes 18924544 | tf_op jit(solution)/shard_map/convert_element_type | solution.py:310
  349.0 29.9 %multiply_convert_fusion.1 = (bf16[12288,1024]{1,0:T(8,128)(2,1)}, f32[12288,1024]{1,0:T(8,128)}) fusion(bf16[12288,256]{1,0:T(8,128)(2,1)} %multiply_convert_fusion.2, bf16[256,1024]{1,0:T(8,128)(2,1)S(1)} %copy-done), kind=kOutput, calls=%fused_computation.1 | convolution fusion | flops 6505365504 | bytes 82313216 | tf_op jit(solution)/shard_map/dot_general | solution.py:311
  378.9 33.2 %multiply_convert_fusion = bf16[12288,1024]{1,0:T(8,128)(2,1)} fusion(f32[12288,1024]{1,0:T(8,128)} %get-tuple-element.198, bf16[12288,256]{1,0:T(8,128)(2,1)} %bitcast.182, bf16[1024,256]{1,0:T(8,128)(2,1)S(1)} %copy-done.15), kind=kOutput, calls=%fused_computation | convolution fusion | flops 6555697152 | bytes 82313216 | tf_op jit(solution)/shard_map/dot_general | solution.py:321
  412.0 19.2 %multiply_reduce_fusion = (f32[256]{0:T(256)S(1)}, f32[12288]{0:T(1024)S(1)}, f32[12288,256]{1,0:T(8,128)}) fusion(f32[3,64,64,256]{3,2,1,0:T(8,128)} %copy.126, f32[12288]{0:T(1024)S(1)} %copy-done.8, f32[256]{0:T(256)S(1)} %copy-done.12, bf16[12288,1024]{1,0:T(8,128)(2,1)} %multiply_convert_fusion, bf16[256,1024]{1,0:T(8,128)(2,1)S(1)} %copy-done), kind=kOutput, calls=%fused_computation.8 | convolution fusion | flops 6461313024 | bytes 50956288 | tf_op jit(solution)/shard_map/dot_general | solution.py:328
  431.2 14.3 %fusion.24 = f32[256,1024]{1,0:T(8,128)} fusion(bf16[12288,256]{1,0:T(8,128)(2,1)} %multiply_convert_fusion.2, bf16[12288,1024]{1,0:T(8,128)(2,1)} %multiply_convert_fusion), kind=kOutput, calls=%fused_computation.130 | convolution fusion | flops 6442450944 | bytes 32505856 | tf_op jit(solution)/shard_map/dot_general | solution.py:325
  445.5 11.6 %fusion.25 = f32[1024,256]{1,0:T(8,128)S(1)} fusion(bf16[12288,1024]{1,0:T(8,128)(2,1)} %get-tuple-element.197, bf16[12288,256]{1,0:T(8,128)(2,1)S(1)} %bitcast.183), kind=kOutput, calls=%fused_computation.131 | convolution fusion | flops 6442450944 | bytes 32505856 | tf_op jit(solution)/shard_map/dot_general | solution.py:318
  458.2 16.5 %subtract_multiply_fusion = f32[12288,256]{1,0:T(8,128)} fusion(f32[12288,256]{1,0:T(8,128)} %get-tuple-element.199, f32[3,64,64,256]{3,2,1,0:T(8,128)} %copy.126, f32[12288]{0:T(1024)S(1)} %broadcast_multiply_fusion, f32[256]{0:T(256)S(1)} %copy-done.12, f32[12288]{0:T(1024)S(1)} %copy-done.8), kind=kLoop, calls=%fused_computation.9 | loop fusion | flops 15728640 | bytes 37848064 | tf_op jit(solution)/shard_map/mul | solution.py:338
  474.8 81.8 %shard_map.122 = f32[64,8,256]{2,1,0:T(8,128)} custom-call(s32[128]{0:T(128)} %reshape.562.off_ref, bf16[3,72,72,256]{3,2,1,0:T(8,128)(2,1)} %get-tuple-element.123.ext_ref, f32[3,64,64,256]{3,2,1,0:T(8,128)} %bitcast.170), custom_call_target="tpu_custom_call" | custom-call | tf_op jit(solution)/shard_map/pallas_call | solution.py:109
  557.8 40.3 %all-reduce.8.cloned.1.call-done = (f32[256,1024]{1,0:T(8,128)}, f32[1025,256]{1,0:T(8,128)}) async-done(((f32[256,1024]{1,0:T(8,128)}, f32[1025,256]{1,0:T(8,128)}), (f32[256,1024]{1,0:T(8,128)}, f32[1025,256]{1,0:T(8,128)})) %all-reduce.8.cloned.1.call-update) | async-done | bytes 2098192 | tf_op jit(solution)/shard_map/psum | solution.py:331
  599.5 2.8 collective-permute-done.4
  607.1 2.5 collective-permute-start.6
  609.7 2.7 collective-permute-done.6
  615.2 13.3 %convolution_convert_fusion = bf16[12288,256]{1,0:T(8,128)(2,1)} fusion(bf16[12288,1024]{1,0:T(8,128)(2,1)} %get-tuple-element.197, bf16[1024,256]{1,0:T(8,128)(2,1)S(1)} %copy-done.15), kind=kOutput, calls=%fused_computation.5 | convolution fusion | flops 6445596672 | bytes 31981568 | tf_op jit(solution)/shard_map/dot_general | solution.py:314
  (140 shorter events, 78.1 us)
Async XLA Ops:
  7.2 341.8 %copy-start = (bf16[256,1024]{1,0:T(8,128)(2,1)S(1)}, bf16[256,1024]{1,0:T(8,128)(2,1)}, u32[]{:S(2)}) copy-start(bf16[256,1024]{1,0:T(8,128)(2,1)} %param.29) | copy-start | bytes 1572868
  9.9 12.7 %all-to-all-start.1 = ((bf16[3,4,4,16,256]{4,3,1,0,2:T(8,128)(2,1)}), bf16[3,4,4,16,256]{4,3,1,0,2:T(8,128)(2,1)S(1)}, u32[]{:S(2)}, u32[]{:S(2)}) async-start(bf16[3,4,4,16,256]{4,3,1,0,2:T(8,128)(2,1)} %copy.112), calls=%async_computation.1 | async-start | bytes 786432 | tf_op jit(solution)/shard_map/all_to_all | solution.py:191
  15.1 13.4 %collective-permute-start = (bf16[3,4,64,256]{3,2,1,0:T(8,128)(2,1)S(1)}, bf16[3,4,64,256]{3,2,1,0:T(8,128)(2,1)S(1)}, u32[]{:S(2)}, u32[]{:S(2)}) collective-permute-start(bf16[3,4,64,256]{3,2,1,0:T(8,128)(2,1)S(1)} %slice.469), channel_id=1, source_target_pairs={{0,4},{4,8},{8,12},{1,5},{5,9},{9,13},{2,6},{6,10},{10,14},{3,7},{... | collective-permute-start | bytes 1179656 | tf_op jit(solution)/shard_map/ppermute | solution.py:137
  20.5 13.8 %collective-permute-start.1 = (bf16[3,4,64,256]{3,2,1,0:T(8,128)(2,1)S(1)}, bf16[3,4,64,256]{3,2,1,0:T(8,128)(2,1)S(1)}, u32[]{:S(2)}, u32[]{:S(2)}) collective-permute-start(bf16[3,4,64,256]{3,2,1,0:T(8,128)(2,1)S(1)} %get-tuple-element.145), channel_id=1, source_target_pairs={{4,0},{8,4},{12,8},{5,1},{9,5},{13,9},{6,2},{10,6},{14,10},{7,3},{... | collective-permute-start | bytes 1179656 | tf_op jit(solution)/shard_map/ppermute | solution.py:139
  22.6 20.4 %all-to-all-start = ((bf16[3,4,4,16,256]{4,3,1,0,2:T(8,128)(2,1)}), bf16[3,4,4,16,256]{4,3,1,0,2:T(8,128)(2,1)S(1)}, u32[]{:S(2)}, u32[]{:S(2)}) async-start(bf16[3,4,4,16,256]{4,3,1,0,2:T(8,128)(2,1)} %copy.108), calls=%async_computation | async-start | bytes 786432 | tf_op jit(solution)/shard_map/all_to_all | solution.py:184
  28.5 176.1 %all-gather.7.cloned.1.call-start = ((), (), s32[]{:S(2)}) async-start(), calls=%async_computation.5 | async-start | bytes 3342336 | tf_op jit(solution)/shard_map/all_gather | solution.py:205
  34.4 2.9 copy-start.2
  37.6 6.1 collective-permute-start.2
  38.9 6.0 collective-permute-start.3
  43.7 11.5 %copy-start.9 = (s32[6,4,3]{0,1,2:T(4,128)S(1)}, s32[6,4,3]{0,1,2:T(4,128)}, u32[]{:S(2)}) copy-start(s32[6,4,3]{0,1,2:T(4,128)} %param.26) | copy-start | bytes 868
  43.7 66.0 %copy-start.13 = (s32[64,2]{0,1:T(2,128)S(1)}, s32[64,2]{0,1:T(2,128)}, u32[]{:S(2)}) copy-start(s32[64,2]{0,1:T(2,128)} %param.25) | copy-start | bytes 1540
  43.7 66.1 %copy-start.10 = (bf16[64,256]{1,0:T(8,128)(2,1)S(1)}, bf16[64,256]{1,0:T(8,128)(2,1)}, u32[]{:S(2)}) copy-start(bf16[64,256]{1,0:T(8,128)(2,1)} %param.27) | copy-start | bytes 98308
  54.5 150.1 %all-gather.5.cloned.1.call-start = ((), (), s32[]{:S(2)}) async-start(), calls=%async_computation.4 | async-start | bytes 3342336 | tf_op jit(solution)/shard_map/all_gather | solution.py:202
  204.6 2.8 copy-start.3
  210.6 2.7 copy-start.1
  213.3 31.2 %copy-start.16 = (bf16[256]{0:T(256)(128)(2,1)S(1)}, bf16[256]{0:T(256)(128)(2,1)}, u32[]{:S(2)}) copy-start(bf16[256]{0:T(256)(128)(2,1)} %param.28) | copy-start | bytes 1540
  219.3 20.9 %all-to-all-start.3 = ((bf16[6,4,72,256]{3,2,1,0:T(8,128)(2,1)}), bf16[6,4,72,256]{3,2,1,0:T(8,128)(2,1)S(1)}, u32[]{:S(2)}, u32[]{:S(2)}) async-start(bf16[6,4,72,256]{3,2,1,0:T(8,128)(2,1)} %bitcast_dynamic-update-slice_fusion), calls=%async_computation.3 | async-start | bytes 1769472 | tf_op jit(solution)/shard_map/all_to_all | solution.py:259
  240.2 23.8 %all-to-all-start.2 = ((bf16[6,4,72,256]{3,2,1,0:T(8,128)(2,1)}), bf16[6,4,72,256]{3,2,1,0:T(8,128)(2,1)S(1)}, u32[]{:S(2)}, u32[]{:S(2)}) async-start(bf16[6,4,72,256]{3,2,1,0:T(8,128)(2,1)} %copy-done.4), calls=%async_computation.2 | async-start | bytes 1769472 | tf_op jit(solution)/shard_map/all_to_all | solution.py:258
  243.7 354.4 %all-reduce.8.cloned.1.call-start = ((), (), s32[]{:S(2)}) async-start(), calls=%async_computation.6 | async-start | bytes 4210688 | tf_op jit(solution)/shard_map/psum | solution.py:331
  244.5 95.9 %copy-start.11 = (f32[256]{0:T(256)}, f32[256]{0:T(256)S(1)}, u32[]{:S(2)}) copy-start(f32[256]{0:T(256)S(1)} %convert_element_type.12) | copy-start | bytes 3076
  340.3 8.6 %copy-start.7 = (f32[12288]{0:T(1024)}, f32[12288]{0:T(1024)S(1)}, u32[]{:S(2)}) copy-start(f32[12288]{0:T(1024)S(1)} %rsqrt.12) | copy-start | bytes 147460
  349.0 29.9 %copy-start.15 = (bf16[1024,256]{1,0:T(8,128)(2,1)S(1)}, bf16[1024,256]{1,0:T(8,128)(2,1)}, u32[]{:S(2)}) copy-start(bf16[1024,256]{1,0:T(8,128)(2,1)} %param.30) | copy-start | bytes 1572868
  378.9 33.2 %copy-start.8 = (f32[12288]{0:T(1024)S(1)}, f32[12288]{0:T(1024)}, u32[]{:S(2)}) copy-start(f32[12288]{0:T(1024)} %copy-done.7) | copy-start | bytes 147460
  378.9 33.2 %copy-start.12 = (f32[256]{0:T(256)S(1)}, f32[256]{0:T(256)}, u32[]{:S(2)}) copy-start(f32[256]{0:T(256)} %copy-done.11) | copy-start | bytes 3076
  431.2 14.3 %copy-start.14 = (bf16[3,64,64,256]{3,2,1,0:T(8,128)(2,1)S(1)}, bf16[3,64,64,256]{3,2,1,0:T(8,128)(2,1)}, u32[]{:S(2)}) copy-start(bf16[3,64,64,256]{3,2,1,0:T(8,128)(2,1)} %param.31) | copy-start | bytes 18874372
  598.1 4.3 collective-permute-start.4
  602.4 4.7 collective-permute-start.5
  607.1 5.2 collective-permute-start.6
  612.3 1.3 collective-permute-start.7
  613.7 14.8 %copy-start.6 = (f32[1025,256]{1,0:T(8,128)S(1)}, f32[1025,256]{1,0:T(8,128)}, u32[]{:S(2)}) copy-start(f32[1025,256]{1,0:T(8,128)} %get-tuple-element.117) | copy-start | bytes 3148804
  613.7 17.0 %copy-start.5 = (f32[256,1024]{1,0:T(8,128)S(1)}, f32[256,1024]{1,0:T(8,128)}, u32[]{:S(2)}) copy-start(f32[256,1024]{1,0:T(8,128)} %get-tuple-element.221) | copy-start | bytes 3145732
  613.7 16.4 %collective-permute-start.8 = (f32[64,256]{1,0:T(8,128)S(1)}, f32[64,256]{1,0:T(8,128)S(1)}, u32[]{:S(2)}, u32[]{:S(2)}) collective-permute-start(f32[64,256]{1,0:T(8,128)S(1)} %add.355), channel_id=1, source_target_pairs={{0,2},{1,3},{2,0},{3,1},{4,6},{5,7},{6,4},{7,5},{8,10},{9,11},{10,... | collective-permute-start | bytes 196616 | tf_op jit(solution)/shard_map/ppermute | solution.py:360
  (1 other events, 0.9 us)
Sparse Core Ops, SparseCore 0:
  54.6 50.7 all-gather.6
  108.3 44.2 all-gather.4
  458.4 139.6 all-reduce.7

commit v5 on v3

--- a/solution.py
+++ b/solution.py
@@ -191,10 +191,17 @@
     )
     own_across = jnp.stack([across_sub[:, :, 0], across_sub[:, :, row_count - 1]], axis=1)
     own_down = jnp.stack([down_sub[:, :, 0], down_sub[:, :, col_count - 1]], axis=1)
-    across_all = lax.all_gather(own_across, ("row", "col")).reshape(
+    if own_across.shape == own_down.shape:
+        both_all = lax.all_gather(jnp.concatenate([own_across, own_down], axis=1), ("row", "col"))
+        across_all = both_all[:, :, :2]
+        down_all = both_all[:, :, 2:]
+    else:
+        across_all = lax.all_gather(own_across, ("row", "col"))
+        down_all = lax.all_gather(own_down, ("row", "col"))
+    across_all = across_all.reshape(
         row_count, col_count, local_count, 2, radius_cells, sub_across, channels
     )
-    down_all = lax.all_gather(own_down, ("row", "col")).reshape(
+    down_all = down_all.reshape(
         row_count, col_count, local_count, 2, radius_cells, sub_down, channels
     )
     across_full = jnp.transpose(across_all, (2, 3, 4, 1, 0, 5, 6)).reshape(

time: 590 us -> 580 us (0.983)
  blocking collectives: 33.8 us -> 0 us
  waiting for transfers between devices: 45.7 us -> 64.9 us
  starting transfers between devices: 21.9 us -> 31.2 us
    all_to_all x2 -> x0, blocking collectives: 33.8 us -> none  [the longest x1 22.3 us: shards(): lax.all_to_all(across.reshape(local_count, radius_cells, row_count, sub_a...]
    all_to_all x0 -> x2, waiting for transfers between devices: none -> 15.9 us  [the longest x1 11.5 us: shards(): lax.all_to_all(across.reshape(local_count, radius_cells, row_count, sub_a...]
    all_to_all x0 -> x2, starting transfers between devices: none -> 9.75 us  [the longest x1 5.54 us: shards(): lax.all_to_all(across.reshape(local_count, radius_cells, row_count, sub_a...]
  transfers between devices with their start and end apart: 14 -> 15, of which waited for: 6 -> 8; matrix products, arithmetic and copies ran while one was open for 16% -> 15% of each run, Pallas kernels for 14% -> 14%
where the time goes in v5:
time: 580 us; the launch traced here: 572 us
  Pallas kernels  176 us (30%)
  matrix products  122 us (21%)
  between operations  68.2 us (12%)
  waiting for transfers between devices  64.9 us (11%)
  other arithmetic  63.4 us (11%)
  local copies, waits for them, and re-layouts  45.9 us (8%)
  starting transfers between devices  31.2 us (5%)
    pallas_call x1, Pallas kernels, stencil_forward(): pl.pallas_call(_fwd_kernel, grid=(faces,), in_specs=[pl.BlockSpec((1, ext...  94.4 us
    pallas_call x1, Pallas kernels, stencil_backward(): pl.pallas_call(_bwd_kernel, grid_spec=pltpu.PrefetchScalarGridSpec(num_sc...  81.7 us
    psum x1, waiting for transfers between devices, shards(): lax.psum((w_in_grad, jnp.concatenate([w_out_grad, gain_grad[None, :]], ax...  38.3 us
    dot_general x1, matrix products, shards(): lax.dot_general(target_rows, w_out, contract_cols, preferred_element_type...  33.4 us
    dot_general x1, matrix products, shards(): pre_act = jnp.dot(hidden_in, w_in, preferred_element_type=jnp.float32)  29.7 us
    dot_general x1, matrix products, shards(): lax.dot_general(pre_grad, w_in, contract_cols, preferred_element_type=jnp...  18.7 us
    mul x1, other arithmetic, shards(): inverse_rms * (scaled_grad - normalized * jnp.mean(scaled_grad * normaliz...  16.6 us
    rev x12, local copies, waits for them, and re-layouts, cut_segment(): return jnp.where(flip_flag == 1, jnp.flip(segment, axis=1), segment)  14.5 us
  transfers between devices with their start and end apart: 15, of which 8 were waited for; matrix products, arithmetic and copies ran while one was open for 15% of the time, Pallas kernels for 14%

profile of v5, /device:TPU:0, one launch (start us, length us, event | category | flops | bytes accessed | tf_op | source)
XLA Modules:
  0.0 571.9 jit_solution(16318015643904519377)
XLA Ops:
  9.9 4.2 all-to-all-start.1
  17.1 4.5 all-to-all-done.1
  21.5 5.5 all-to-all-start
  27.1 11.5 %all-to-all-done = bf16[3,4,4,16,256]{4,3,1,0,2:T(8,128)(2,1)S(1)} async-done(((bf16[3,4,4,16,256]{4,3,1,0,2:T(8,128)(2,1)}), bf16[3,4,4,16,256]{4,3,1,0,2:T(8,128)(2,1)S(1)}, u32[]{:S(2)}, u32[]{:S(2)}) %all-to-all-start) | async-done | bytes 393248 | tf_op jit(solution)/shard_map/all_to_all | solution.py:178
  102.3 3.4 constant_dynamic-update-slice_fusion.1
  105.8 2.9 copy-done.2
  113.2 3.6 copy.57
  118.6 2.6 fusion.3
  121.2 2.8 copy-done.1
  130.1 3.6 all-to-all-start.3
  135.0 2.5 rev.54
  137.5 2.5 rev.55
  140.0 2.5 rev.56
  142.5 2.5 rev.57
  145.0 2.5 rev.58
  149.1 3.6 all-to-all-start.2
  152.9 8.8 %pad_maximum_fusion = bf16[3,72,72,256]{3,2,1,0:T(8,128)(2,1)} fusion(bf16[3,72,4,256]{3,2,1,0:T(4,128)(2,1)} %collective-permute-done.3, bf16[3,72,64,256]{3,2,1,0:T(8,128)(2,1)} %copy-done.2, bf16[3,72,4,256]{3,2,1,0:T(4,128)(2,1)} %collective-permute-done.2), kind=kLoop, calls=%fused_computation.15 | loop fusion | flops 23887872 | bytes 15925248 | tf_op jit(solution)/shard_map/concatenate | solution.py:135
  174.7 94.4 %shard_map.119 = f32[3,64,64,256]{3,2,1,0:T(8,128)} custom-call(bf16[3,72,72,256]{3,2,1,0:T(8,128)(2,1)} %fusion.4.ext_ref, f32[81,256]{1,0:T(8,128)S(1)} %fusion.8.w_ref), custom_call_target="tpu_custom_call" | custom-call | tf_op jit(solution)/shard_map/pallas_call | solution.py:47
  269.1 6.3 %multiply_reduce_fusion.2 = f32[3,64,64]{2,1,0:T(8,128)S(1)} fusion(f32[3,64,64,256]{3,2,1,0:T(8,128)} %shard_map.119), kind=kLoop, calls=%fused_computation.12 | loop fusion | flops 6279168 | bytes 12632064 | tf_op jit(solution)/shard_map/reduce_sum | solution.py:284
  275.6 8.6 %multiply_convert_fusion.2 = bf16[12288,256]{1,0:T(8,128)(2,1)} fusion(f32[3,64,64,256]{3,2,1,0:T(8,128)} %shard_map.119, f32[256]{0:T(256)S(1)} %convert_element_type.12, f32[12288]{0:T(1024)S(1)} %rsqrt.12), kind=kLoop, calls=%fused_computation.11 | loop fusion | flops 9437184 | bytes 18924544 | tf_op jit(solution)/shard_map/convert_element_type | solution.py:288
  284.2 29.7 %multiply_convert_fusion.1 = (bf16[12288,1024]{1,0:T(8,128)(2,1)}, f32[12288,1024]{1,0:T(8,128)}) fusion(bf16[12288,256]{1,0:T(8,128)(2,1)} %multiply_convert_fusion.2, bf16[256,1024]{1,0:T(8,128)(2,1)S(1)} %copy-done), kind=kOutput, calls=%fused_computation.1 | convolution fusion | flops 6505365504 | bytes 82313216 | tf_op jit(solution)/shard_map/dot_general | solution.py:289
  313.9 33.4 %multiply_convert_fusion = bf16[12288,1024]{1,0:T(8,128)(2,1)} fusion(f32[12288,1024]{1,0:T(8,128)} %get-tuple-element.130, bf16[12288,256]{1,0:T(8,128)(2,1)} %bitcast.177, bf16[1024,256]{1,0:T(8,128)(2,1)S(1)} %copy-done.11), kind=kOutput, calls=%fused_computation | convolution fusion | flops 6555697152 | bytes 82313216 | tf_op jit(solution)/shard_map/dot_general | solution.py:299
  347.3 18.7 %multiply_reduce_fusion = (f32[256]{0:T(256)S(1)}, f32[12288]{0:T(1024)S(1)}, f32[12288,256]{1,0:T(8,128)}) fusion(f32[3,64,64,256]{3,2,1,0:T(8,128)} %shard_map.119, f32[12288]{0:T(1024)S(1)} %copy-done.7, f32[256]{0:T(256)S(1)} %copy-done.9, bf16[12288,1024]{1,0:T(8,128)(2,1)} %multiply_convert_fusion, bf16[256,1024]{1,0:T(8,128)(2,1)S(1)} %copy-done), kind=kOutput, calls=%fused_computation.8 | convolution fusion | flops 6461313024 | bytes 50956288 | tf_op jit(solution)/shard_map/dot_general | solution.py:306
  366.0 14.3 %fusion.14 = f32[256,1024]{1,0:T(8,128)} fusion(bf16[12288,256]{1,0:T(8,128)(2,1)} %multiply_convert_fusion.2, bf16[12288,1024]{1,0:T(8,128)(2,1)} %multiply_convert_fusion), kind=kOutput, calls=%fused_computation.106 | convolution fusion | flops 6442450944 | bytes 32505856 | tf_op jit(solution)/shard_map/dot_general | solution.py:303
  380.3 11.8 %fusion.15 = f32[1024,256]{1,0:T(8,128)S(1)} fusion(bf16[12288,1024]{1,0:T(8,128)(2,1)} %get-tuple-element.129, bf16[12288,256]{1,0:T(8,128)(2,1)S(1)} %bitcast.178), kind=kOutput, calls=%fused_computation.107 | convolution fusion | flops 6442450944 | bytes 32505856 | tf_op jit(solution)/shard_map/dot_general | solution.py:296
  393.3 16.6 %subtract_multiply_fusion = f32[12288,256]{1,0:T(8,128)} fusion(f32[12288,256]{1,0:T(8,128)} %get-tuple-element.131, f32[3,64,64,256]{3,2,1,0:T(8,128)} %shard_map.119, f32[12288]{0:T(1024)S(1)} %broadcast_multiply_fusion, f32[256]{0:T(256)S(1)} %copy-done.9, f32[12288]{0:T(1024)S(1)} %copy-done.7), kind=kLoop, calls=%fused_computation.9 | loop fusion | flops 15728640 | bytes 37848064 | tf_op jit(solution)/shard_map/mul | solution.py:316
  409.9 81.7 %shard_map.120 = f32[64,8,256]{2,1,0:T(8,128)} custom-call(s32[128]{0:T(128)} %reshape.422.off_ref, bf16[3,72,72,256]{3,2,1,0:T(8,128)(2,1)} %fusion.4.ext_ref, f32[3,64,64,256]{3,2,1,0:T(8,128)} %bitcast.165), custom_call_target="tpu_custom_call" | custom-call | tf_op jit(solution)/shard_map/pallas_call | solution.py:109
  492.7 38.3 %all-reduce.4.cloned.1.call-done = (f32[256,1024]{1,0:T(8,128)}, f32[1025,256]{1,0:T(8,128)}) async-done(((f32[256,1024]{1,0:T(8,128)}, f32[1025,256]{1,0:T(8,128)}), (f32[256,1024]{1,0:T(8,128)}, f32[1025,256]{1,0:T(8,128)})) %all-reduce.4.cloned.1.call-update) | async-done | bytes 2098192 | tf_op jit(solution)/shard_map/psum | solution.py:309
  532.5 2.8 collective-permute-done.4
  540.0 2.5 collective-permute-start.6
  542.6 2.7 collective-permute-done.6
  548.1 13.3 %convolution_convert_fusion = bf16[12288,256]{1,0:T(8,128)(2,1)} fusion(bf16[12288,1024]{1,0:T(8,128)(2,1)} %get-tuple-element.129, bf16[1024,256]{1,0:T(8,128)(2,1)S(1)} %copy-done.11), kind=kOutput, calls=%fused_computation.5 | convolution fusion | flops 6445596672 | bytes 31981568 | tf_op jit(solution)/shard_map/dot_general | solution.py:292
  (111 shorter events, 59.1 us)
Async XLA Ops:
  7.2 277.0 %copy-start = (bf16[256,1024]{1,0:T(8,128)(2,1)S(1)}, bf16[256,1024]{1,0:T(8,128)(2,1)}, u32[]{:S(2)}) copy-start(bf16[256,1024]{1,0:T(8,128)(2,1)} %param.21) | copy-start | bytes 1572868
  9.9 11.7 %all-to-all-start.1 = ((bf16[3,4,4,16,256]{4,3,1,0,2:T(8,128)(2,1)}), bf16[3,4,4,16,256]{4,3,1,0,2:T(8,128)(2,1)S(1)}, u32[]{:S(2)}, u32[]{:S(2)}) async-start(bf16[3,4,4,16,256]{4,3,1,0,2:T(8,128)(2,1)} %copy.56), calls=%async_computation.1 | async-start | bytes 786432 | tf_op jit(solution)/shard_map/all_to_all | solution.py:185
  21.5 17.0 %all-to-all-start = ((bf16[3,4,4,16,256]{4,3,1,0,2:T(8,128)(2,1)}), bf16[3,4,4,16,256]{4,3,1,0,2:T(8,128)(2,1)S(1)}, u32[]{:S(2)}, u32[]{:S(2)}) async-start(bf16[3,4,4,16,256]{4,3,1,0,2:T(8,128)(2,1)} %copy.53), calls=%async_computation | async-start | bytes 786432 | tf_op jit(solution)/shard_map/all_to_all | solution.py:178
  27.1 86.2 %all-gather.3.cloned.1.call-start = ((), (), s32[]{:S(2)}) async-start(), calls=%async_computation.4 | async-start | bytes 6684672 | tf_op jit(solution)/shard_map/all_gather | solution.py:195
  39.4 62.9 %collective-permute-start = (bf16[3,4,64,256]{3,2,1,0:T(8,128)(2,1)S(1)}, bf16[3,4,64,256]{3,2,1,0:T(8,128)(2,1)S(1)}, u32[]{:S(2)}, u32[]{:S(2)}) collective-permute-start(bf16[3,4,64,256]{3,2,1,0:T(8,128)(2,1)S(1)} %slice.346), channel_id=1, source_target_pairs={{0,4},{4,8},{8,12},{1,5},{5,9},{9,13},{2,6},{6,10},{10,14},{3,7},{... | collective-permute-start | bytes 1179656 | tf_op jit(solution)/shard_map/ppermute | solution.py:137
  40.9 64.8 %collective-permute-start.1 = (bf16[3,4,64,256]{3,2,1,0:T(8,128)(2,1)S(1)}, bf16[3,4,64,256]{3,2,1,0:T(8,128)(2,1)S(1)}, u32[]{:S(2)}, u32[]{:S(2)}) collective-permute-start(bf16[3,4,64,256]{3,2,1,0:T(8,128)(2,1)S(1)} %get-tuple-element.80), channel_id=1, source_target_pairs={{4,0},{8,4},{12,8},{5,1},{9,5},{13,9},{6,2},{10,6},{14,10},{7,3},{... | collective-permute-start | bytes 1179656 | tf_op jit(solution)/shard_map/ppermute | solution.py:139
  91.5 184.0 %copy-start.8 = (f32[256]{0:T(256)}, f32[256]{0:T(256)S(1)}, u32[]{:S(2)}) copy-start(f32[256]{0:T(256)S(1)} %convert_element_type.12) | copy-start | bytes 3076
  105.8 2.9 copy-start.2
  109.9 43.0 %collective-permute-start.2 = (bf16[3,72,4,256]{3,2,1,0:T(4,128)(2,1)}, bf16[3,72,4,256]{3,2,1,0:T(4,128)(2,1)}, u32[]{:S(2)}, u32[]{:S(2)}) collective-permute-start(bf16[3,72,4,256]{3,2,1,0:T(4,128)(2,1)} %get-tuple-element.63), channel_id=1, source_target_pairs={{0,1},{1,2},{2,3},{4,5},{5,6},{6,7},{8,9},{9,10},{10,11},{12,13},{... | collective-permute-start | bytes 1327112 | tf_op jit(solution)/shard_map/ppermute | solution.py:137
  111.9 41.0 %collective-permute-start.3 = (bf16[3,72,4,256]{3,2,1,0:T(4,128)(2,1)}, bf16[3,72,4,256]{3,2,1,0:T(4,128)(2,1)}, u32[]{:S(2)}, u32[]{:S(2)}) collective-permute-start(bf16[3,72,4,256]{3,2,1,0:T(4,128)(2,1)} %get-tuple-element.64), channel_id=1, source_target_pairs={{1,0},{2,1},{3,2},{5,4},{6,5},{7,6},{9,8},{10,9},{11,10},{13,12},{... | collective-permute-start | bytes 1327112 | tf_op jit(solution)/shard_map/ppermute | solution.py:139
  121.2 2.8 copy-start.1
  130.1 19.0 %all-to-all-start.3 = ((bf16[6,4,72,256]{3,2,1,0:T(8,128)(2,1)}), bf16[6,4,72,256]{3,2,1,0:T(8,128)(2,1)S(1)}, u32[]{:S(2)}, u32[]{:S(2)}) async-start(bf16[6,4,72,256]{3,2,1,0:T(8,128)(2,1)} %bitcast_dynamic-update-slice_fusion), calls=%async_computation.3 | async-start | bytes 1769472 | tf_op jit(solution)/shard_map/all_to_all | solution.py:257
  148.2 0.9 copy-start.3
  149.1 16.6 %all-to-all-start.2 = ((bf16[6,4,72,256]{3,2,1,0:T(8,128)(2,1)}), bf16[6,4,72,256]{3,2,1,0:T(8,128)(2,1)S(1)}, u32[]{:S(2)}, u32[]{:S(2)}) async-start(bf16[6,4,72,256]{3,2,1,0:T(8,128)(2,1)} %copy-done.3), calls=%async_computation.2 | async-start | bytes 1769472 | tf_op jit(solution)/shard_map/all_to_all | solution.py:256
  152.7 378.4 %all-reduce.4.cloned.1.call-start = ((), (), s32[]{:S(2)}) async-start(), calls=%async_computation.5 | async-start | bytes 4210688 | tf_op jit(solution)/shard_map/psum | solution.py:309
  275.5 38.4 %copy-start.6 = (f32[12288]{0:T(1024)}, f32[12288]{0:T(1024)S(1)}, u32[]{:S(2)}) copy-start(f32[12288]{0:T(1024)S(1)} %rsqrt.12) | copy-start | bytes 147460
  284.2 29.7 %copy-start.11 = (bf16[1024,256]{1,0:T(8,128)(2,1)S(1)}, bf16[1024,256]{1,0:T(8,128)(2,1)}, u32[]{:S(2)}) copy-start(bf16[1024,256]{1,0:T(8,128)(2,1)} %param.22) | copy-start | bytes 1572868
  313.9 33.4 %copy-start.7 = (f32[12288]{0:T(1024)S(1)}, f32[12288]{0:T(1024)}, u32[]{:S(2)}) copy-start(f32[12288]{0:T(1024)} %copy-done.6) | copy-start | bytes 147460
  313.9 33.4 %copy-start.9 = (f32[256]{0:T(256)S(1)}, f32[256]{0:T(256)}, u32[]{:S(2)}) copy-start(f32[256]{0:T(256)} %copy-done.8) | copy-start | bytes 3076
  366.0 14.3 %copy-start.10 = (bf16[3,64,64,256]{3,2,1,0:T(8,128)(2,1)S(1)}, bf16[3,64,64,256]{3,2,1,0:T(8,128)(2,1)}, u32[]{:S(2)}) copy-start(bf16[3,64,64,256]{3,2,1,0:T(8,128)(2,1)} %param.23) | copy-start | bytes 18874372
  531.0 4.3 collective-permute-start.4
  535.3 4.7 collective-permute-start.5
  540.0 5.2 collective-permute-start.6
  545.3 1.3 collective-permute-start.7
  546.6 14.8 %copy-start.5 = (f32[1025,256]{1,0:T(8,128)S(1)}, f32[1025,256]{1,0:T(8,128)}, u32[]{:S(2)}) copy-start(f32[1025,256]{1,0:T(8,128)} %get-tuple-element.57) | copy-start | bytes 3148804
  546.6 17.0 %copy-start.4 = (f32[256,1024]{1,0:T(8,128)S(1)}, f32[256,1024]{1,0:T(8,128)}, u32[]{:S(2)}) copy-start(f32[256,1024]{1,0:T(8,128)} %get-tuple-element.153) | copy-start | bytes 3145732
  546.6 16.4 %collective-permute-start.8 = (f32[64,256]{1,0:T(8,128)S(1)}, f32[64,256]{1,0:T(8,128)S(1)}, u32[]{:S(2)}, u32[]{:S(2)}) collective-permute-start(f32[64,256]{1,0:T(8,128)S(1)} %add.315), channel_id=1, source_target_pairs={{0,2},{1,3},{2,0},{3,1},{4,6},{5,7},{6,4},{7,5},{8,10},{9,11},{10,... | collective-permute-start | bytes 196616 | tf_op jit(solution)/shard_map/ppermute | solution.py:338
Sparse Core Ops, SparseCore 0:
  39.5 62.7 all-gather.2
  393.4 137.5 all-reduce.3

commit v6 on v5

--- a/solution.py
+++ b/solution.py
@@ -303,27 +303,24 @@
     w_in_grad = lax.dot_general(
         hidden_in, pre_grad, contract_rows, preferred_element_type=jnp.float32
     )
+    w_in_grad, w_out_grad, pre_grad = lax.optimization_barrier((w_in_grad, w_out_grad, pre_grad))
     hidden_grad = lax.dot_general(pre_grad, w_in, contract_cols, preferred_element_type=jnp.float32)
     gain_grad = jnp.sum(hidden_grad * normalized, axis=0)
-    out_rows = w_out_grad.shape[0]
-    w_in_grad, out_and_gain = lax.psum(
-        (w_in_grad, jnp.concatenate([w_out_grad, gain_grad[None, :]], axis=0)),
-        ("face", "row", "col"),
-    )
-    w_out_grad = out_and_gain[:out_rows]
-    gain_grad = out_and_gain[out_rows]
+    w_in_grad, w_out_grad = lax.psum((w_in_grad, w_out_grad), ("face", "row", "col"))
     scaled_grad = hidden_grad * gain_float
     aggregated_grad = inverse_rms * (
         scaled_grad - normalized * jnp.mean(scaled_grad * normalized, axis=-1, keepdims=True)
     )
     aggregated_grad = aggregated_grad.reshape(local_count, rows_dev, cols_dev, channels)
     stencil_grad = stencil_backward(offsets, extended, aggregated_grad)
-    stencil_grad, w_in_grad, out_and_gain = lax.optimization_barrier(
-        (stencil_grad, w_in_grad, out_and_gain)
-    )
-    w_out_grad = out_and_gain[:out_rows]
-    gain_grad = out_and_gain[out_rows]
-    stencil_grad = butterfly_sum(stencil_grad, ("face", "row", "col"))
+    tap_count = stencil_grad.shape[0]
+    small_grads = jnp.concatenate([stencil_grad, gain_grad[None, :]], axis=0)
+    small_grads, w_in_grad, w_out_grad, increment = lax.optimization_barrier(
+        (small_grads, w_in_grad, w_out_grad, increment)
+    )
+    small_grads = butterfly_sum(small_grads, ("face", "row", "col"))
+    stencil_grad = small_grads[:tap_count]
+    gain_grad = small_grads[tap_count]
     return (increment.reshape(state.shape), stencil_grad, gain_grad, w_in_grad, w_out_grad)
 
 

time: 580 us -> 573 us (0.988)
  waiting for transfers between devices: 64.9 us -> 54.4 us
    psum x1, waiting for transfers between devices: 38.3 us -> 23.8 us  [shards(): lax.psum((w_in_grad, w_out_grad), ('face', 'row', 'col'))]
    unnamed x29 -> x26, local copies, waits for them, and re-layouts: 11.8 us -> 15.4 us
  transfers between devices with their start and end apart: 15 -> 15, of which waited for: 8 -> 9; matrix products, arithmetic and copies ran while one was open for 15% -> 15% of each run, Pallas kernels for 14% -> 14%
where the time goes in v6:
time: 573 us; the launch traced here: 565 us
  Pallas kernels  176 us (31%)
  matrix products  123 us (21%)
  between operations  68.4 us (12%)
  other arithmetic  63.5 us (11%)
  waiting for transfers between devices  54.4 us (9%)
  local copies, waits for them, and re-layouts  49 us (9%)
  starting transfers between devices  30 us (5%)
    pallas_call x1, Pallas kernels, stencil_forward(): pl.pallas_call(_fwd_kernel, grid=(faces,), in_specs=[pl.BlockSpec((1, ext...  94.5 us
    pallas_call x1, Pallas kernels, stencil_backward(): pl.pallas_call(_bwd_kernel, grid_spec=pltpu.PrefetchScalarGridSpec(num_sc...  81.7 us
    dot_general x1, matrix products, shards(): lax.dot_general(target_rows, w_out, contract_cols, preferred_element_type...  33.4 us
    dot_general x1, matrix products, shards(): pre_act = jnp.dot(hidden_in, w_in, preferred_element_type=jnp.float32)  29.7 us
    psum x1, waiting for transfers between devices, shards(): lax.psum((w_in_grad, w_out_grad), ('face', 'row', 'col'))  23.8 us
    dot_general x1, matrix products, shards(): lax.dot_general(pre_grad, w_in, contract_cols, preferred_element_type=jnp...  19 us
    mul x1, other arithmetic, shards(): inverse_rms * (scaled_grad - normalized * jnp.mean(scaled_grad * normaliz...  16.6 us
    unnamed x26, local copies, waits for them, and re-layouts  15.4 us
  transfers between devices with their start and end apart: 15, of which 9 were waited for; matrix products, arithmetic and copies ran while one was open for 15% of the time, Pallas kernels for 14%

profile of v6, /device:TPU:0, one launch (start us, length us, event | category | flops | bytes accessed | tf_op | source)
XLA Modules:
  0.0 564.8 jit_solution(16096042702710066516)
XLA Ops:
  9.9 4.2 all-to-all-start.1
  17.1 4.5 all-to-all-done.1
  21.5 5.5 all-to-all-start
  27.1 11.5 %all-to-all-done = bf16[3,4,4,16,256]{4,3,1,0,2:T(8,128)(2,1)S(1)} async-done(((bf16[3,4,4,16,256]{4,3,1,0,2:T(8,128)(2,1)}), bf16[3,4,4,16,256]{4,3,1,0,2:T(8,128)(2,1)S(1)}, u32[]{:S(2)}, u32[]{:S(2)}) %all-to-all-start) | async-done | bytes 393248 | tf_op jit(solution)/shard_map/all_to_all | solution.py:178
  102.5 3.4 constant_dynamic-update-slice_fusion.1
  105.9 2.9 copy-done.2
  113.4 3.6 copy.58
  118.7 2.6 fusion.3
  121.4 2.8 copy-done.1
  130.2 3.6 all-to-all-start.3
  135.1 2.5 rev.54
  137.7 2.5 rev.55
  140.2 2.5 rev.56
  142.7 2.5 rev.57
  151.1 3.6 all-to-all-start.2
  154.9 8.8 %pad_maximum_fusion = bf16[3,72,72,256]{3,2,1,0:T(8,128)(2,1)} fusion(bf16[3,72,4,256]{3,2,1,0:T(4,128)(2,1)} %collective-permute-done.3, bf16[3,72,64,256]{3,2,1,0:T(8,128)(2,1)} %copy-done.2, bf16[3,72,4,256]{3,2,1,0:T(4,128)(2,1)} %collective-permute-done.2), kind=kLoop, calls=%fused_computation.15 | loop fusion | flops 23887872 | bytes 15925248 | tf_op jit(solution)/shard_map/concatenate | solution.py:135
  176.7 94.5 %shard_map.119 = f32[3,64,64,256]{3,2,1,0:T(8,128)} custom-call(bf16[3,72,72,256]{3,2,1,0:T(8,128)(2,1)} %fusion.4.ext_ref, f32[81,256]{1,0:T(8,128)S(1)} %fusion.8.w_ref), custom_call_target="tpu_custom_call" | custom-call | tf_op jit(solution)/shard_map/pallas_call | solution.py:47
  271.1 6.3 %multiply_reduce_fusion.2 = f32[3,64,64]{2,1,0:T(8,128)S(1)} fusion(f32[3,64,64,256]{3,2,1,0:T(8,128)} %shard_map.119), kind=kLoop, calls=%fused_computation.12 | loop fusion | flops 6279168 | bytes 12632064 | tf_op jit(solution)/shard_map/reduce_sum | solution.py:284
  277.5 8.6 %multiply_convert_fusion.2 = bf16[12288,256]{1,0:T(8,128)(2,1)} fusion(f32[3,64,64,256]{3,2,1,0:T(8,128)} %shard_map.119, f32[256]{0:T(256)S(1)} %convert_element_type.12, f32[12288]{0:T(1024)S(1)} %rsqrt.12), kind=kLoop, calls=%fused_computation.11 | loop fusion | flops 9437184 | bytes 18924544 | tf_op jit(solution)/shard_map/convert_element_type | solution.py:288
  286.2 29.7 %multiply_convert_fusion = (bf16[12288,1024]{1,0:T(8,128)(2,1)}, f32[12288,1024]{1,0:T(8,128)}) fusion(bf16[12288,256]{1,0:T(8,128)(2,1)} %multiply_convert_fusion.2, bf16[256,1024]{1,0:T(8,128)(2,1)S(1)} %copy-done), kind=kOutput, calls=%fused_computation | convolution fusion | flops 6505365504 | bytes 82313216 | tf_op jit(solution)/shard_map/dot_general | solution.py:289
  315.9 33.4 %multiply_convert_fusion.1 = bf16[12288,1024]{1,0:T(8,128)(2,1)} fusion(f32[12288,1024]{1,0:T(8,128)} %get-tuple-element.138, bf16[12288,256]{1,0:T(8,128)(2,1)} %bitcast.177, bf16[1024,256]{1,0:T(8,128)(2,1)S(1)} %copy-done.9), kind=kOutput, calls=%fused_computation.1 | convolution fusion | flops 6555697152 | bytes 82313216 | tf_op jit(solution)/shard_map/dot_general | solution.py:299
  349.2 14.3 %fusion.14 = f32[256,1024]{1,0:T(8,128)} fusion(bf16[12288,256]{1,0:T(8,128)(2,1)} %multiply_convert_fusion.2, bf16[12288,1024]{1,0:T(8,128)(2,1)} %multiply_convert_fusion.1), kind=kOutput, calls=%fused_computation.106 | convolution fusion | flops 6442450944 | bytes 32505856 | tf_op jit(solution)/shard_map/dot_general | solution.py:303
  363.6 12.7 %fusion.15 = f32[1024,256]{1,0:T(8,128)} fusion(bf16[12288,1024]{1,0:T(8,128)(2,1)} %get-tuple-element.137, bf16[12288,256]{1,0:T(8,128)(2,1)S(1)} %bitcast.178), kind=kOutput, calls=%fused_computation.107 | convolution fusion | flops 6442450944 | bytes 32505856 | tf_op jit(solution)/shard_map/dot_general | solution.py:296
  376.3 19.0 %multiply_reduce_fusion.1 = (f32[12288]{0:T(1024)S(1)}, f32[256]{0:T(256)S(1)}, f32[12288,256]{1,0:T(8,128)}) fusion(f32[3,64,64,256]{3,2,1,0:T(8,128)} %shard_map.119, f32[256]{0:T(256)S(1)} %copy-done.7, f32[12288]{0:T(1024)S(1)} %copy-done.5, bf16[12288,1024]{1,0:T(8,128)(2,1)} %multiply_convert_fusion.1, bf16[256,1024]{1,0:T(8,128)(2,1)S(1)} %copy-done), kind=kOutput, calls=%fused_computation.10 | convolution fusion | flops 6461313024 | bytes 50956288 | tf_op jit(solution)/shard_map/dot_general | solution.py:307
  395.3 16.6 %subtract_multiply_fusion = f32[12288,256]{1,0:T(8,128)} fusion(f32[12288,256]{1,0:T(8,128)} %get-tuple-element.139, f32[3,64,64,256]{3,2,1,0:T(8,128)} %shard_map.119, f32[12288]{0:T(1024)S(1)} %broadcast_multiply_fusion, f32[256]{0:T(256)S(1)} %copy-done.7, f32[12288]{0:T(1024)S(1)} %copy-done.5), kind=kLoop, calls=%fused_computation.9 | loop fusion | flops 15728640 | bytes 37848064 | tf_op jit(solution)/shard_map/mul | solution.py:311
  411.9 81.7 %shard_map.120 = f32[64,8,256]{2,1,0:T(8,128)} custom-call(s32[128]{0:T(128)} %reshape.412.off_ref, bf16[3,72,72,256]{3,2,1,0:T(8,128)(2,1)} %fusion.4.ext_ref, f32[3,64,64,256]{3,2,1,0:T(8,128)} %bitcast.165), custom_call_target="tpu_custom_call" | custom-call | tf_op jit(solution)/shard_map/pallas_call | solution.py:109
  494.8 13.3 %convolution_convert_fusion = bf16[12288,256]{1,0:T(8,128)(2,1)} fusion(bf16[12288,1024]{1,0:T(8,128)(2,1)} %get-tuple-element.137, bf16[1024,256]{1,0:T(8,128)(2,1)S(1)} %copy-done.9), kind=kOutput, calls=%fused_computation.5 | convolution fusion | flops 6445596672 | bytes 31981568 | tf_op jit(solution)/shard_map/dot_general | solution.py:292
  508.0 23.8 %all-reduce.4.cloned.1.call-done = (f32[256,1024]{1,0:T(8,128)}, f32[1024,256]{1,0:T(8,128)}) async-done(((f32[256,1024]{1,0:T(8,128)}, f32[1024,256]{1,0:T(8,128)}), (f32[256,1024]{1,0:T(8,128)}, f32[1024,256]{1,0:T(8,128)})) %all-reduce.4.cloned.1.call-update) | async-done | bytes 2097168 | tf_op jit(solution)/shard_map/psum | solution.py:309
  533.3 2.9 collective-permute-done.4
  537.7 2.9 collective-permute-done.5
  542.8 3.1 collective-permute-done.6
  548.9 2.9 collective-permute-done.8
  (108 shorter events, 63.9 us)
Async XLA Ops:
  7.2 279.0 %copy-start = (bf16[256,1024]{1,0:T(8,128)(2,1)S(1)}, bf16[256,1024]{1,0:T(8,128)(2,1)}, u32[]{:S(2)}) copy-start(bf16[256,1024]{1,0:T(8,128)(2,1)} %param.21) | copy-start | bytes 1572868
  9.9 11.7 %all-to-all-start.1 = ((bf16[3,4,4,16,256]{4,3,1,0,2:T(8,128)(2,1)}), bf16[3,4,4,16,256]{4,3,1,0,2:T(8,128)(2,1)S(1)}, u32[]{:S(2)}, u32[]{:S(2)}) async-start(bf16[3,4,4,16,256]{4,3,1,0,2:T(8,128)(2,1)} %copy.57), calls=%async_computation.1 | async-start | bytes 786432 | tf_op jit(solution)/shard_map/all_to_all | solution.py:185
  21.5 17.0 %all-to-all-start = ((bf16[3,4,4,16,256]{4,3,1,0,2:T(8,128)(2,1)}), bf16[3,4,4,16,256]{4,3,1,0,2:T(8,128)(2,1)S(1)}, u32[]{:S(2)}, u32[]{:S(2)}) async-start(bf16[3,4,4,16,256]{4,3,1,0,2:T(8,128)(2,1)} %copy.54), calls=%async_computation | async-start | bytes 786432 | tf_op jit(solution)/shard_map/all_to_all | solution.py:178
  27.1 86.3 %all-gather.3.cloned.1.call-start = ((), (), s32[]{:S(2)}) async-start(), calls=%async_computation.4 | async-start | bytes 6684672 | tf_op jit(solution)/shard_map/all_gather | solution.py:195
  39.4 63.1 %collective-permute-start = (bf16[3,4,64,256]{3,2,1,0:T(8,128)(2,1)S(1)}, bf16[3,4,64,256]{3,2,1,0:T(8,128)(2,1)S(1)}, u32[]{:S(2)}, u32[]{:S(2)}) collective-permute-start(bf16[3,4,64,256]{3,2,1,0:T(8,128)(2,1)S(1)} %slice.346), channel_id=1, source_target_pairs={{0,4},{4,8},{8,12},{1,5},{5,9},{9,13},{2,6},{6,10},{10,14},{3,7},{... | collective-permute-start | bytes 1179656 | tf_op jit(solution)/shard_map/ppermute | solution.py:137
  40.9 65.0 %collective-permute-start.1 = (bf16[3,4,64,256]{3,2,1,0:T(8,128)(2,1)S(1)}, bf16[3,4,64,256]{3,2,1,0:T(8,128)(2,1)S(1)}, u32[]{:S(2)}, u32[]{:S(2)}) collective-permute-start(bf16[3,4,64,256]{3,2,1,0:T(8,128)(2,1)S(1)} %get-tuple-element.88), channel_id=1, source_target_pairs={{4,0},{8,4},{12,8},{5,1},{9,5},{13,9},{6,2},{10,6},{14,10},{7,3},{... | collective-permute-start | bytes 1179656 | tf_op jit(solution)/shard_map/ppermute | solution.py:139
  91.8 185.8 %copy-start.6 = (f32[256]{0:T(256)}, f32[256]{0:T(256)S(1)}, u32[]{:S(2)}) copy-start(f32[256]{0:T(256)S(1)} %convert_element_type.12) | copy-start | bytes 3076
  105.9 2.9 copy-start.2
  110.0 44.8 %collective-permute-start.2 = (bf16[3,72,4,256]{3,2,1,0:T(4,128)(2,1)}, bf16[3,72,4,256]{3,2,1,0:T(4,128)(2,1)}, u32[]{:S(2)}, u32[]{:S(2)}) collective-permute-start(bf16[3,72,4,256]{3,2,1,0:T(4,128)(2,1)} %get-tuple-element.71), channel_id=1, source_target_pairs={{0,1},{1,2},{2,3},{4,5},{5,6},{6,7},{8,9},{9,10},{10,11},{12,13},{... | collective-permute-start | bytes 1327112 | tf_op jit(solution)/shard_map/ppermute | solution.py:137
  112.1 42.8 %collective-permute-start.3 = (bf16[3,72,4,256]{3,2,1,0:T(4,128)(2,1)}, bf16[3,72,4,256]{3,2,1,0:T(4,128)(2,1)}, u32[]{:S(2)}, u32[]{:S(2)}) collective-permute-start(bf16[3,72,4,256]{3,2,1,0:T(4,128)(2,1)} %get-tuple-element.72), channel_id=1, source_target_pairs={{1,0},{2,1},{3,2},{5,4},{6,5},{7,6},{9,8},{10,9},{11,10},{13,12},{... | collective-permute-start | bytes 1327112 | tf_op jit(solution)/shard_map/ppermute | solution.py:139
  121.4 2.8 copy-start.1
  130.2 20.9 %all-to-all-start.3 = ((bf16[6,4,72,256]{3,2,1,0:T(8,128)(2,1)}), bf16[6,4,72,256]{3,2,1,0:T(8,128)(2,1)S(1)}, u32[]{:S(2)}, u32[]{:S(2)}) async-start(bf16[6,4,72,256]{3,2,1,0:T(8,128)(2,1)} %bitcast_dynamic-update-slice_fusion), calls=%async_computation.3 | async-start | bytes 1769472 | tf_op jit(solution)/shard_map/all_to_all | solution.py:257
  150.2 0.9 copy-start.3
  151.1 16.6 %all-to-all-start.2 = ((bf16[6,4,72,256]{3,2,1,0:T(8,128)(2,1)}), bf16[6,4,72,256]{3,2,1,0:T(8,128)(2,1)S(1)}, u32[]{:S(2)}, u32[]{:S(2)}) async-start(bf16[6,4,72,256]{3,2,1,0:T(8,128)(2,1)} %copy-done.3), calls=%async_computation.2 | async-start | bytes 1769472 | tf_op jit(solution)/shard_map/all_to_all | solution.py:256
  154.7 377.2 %all-reduce.4.cloned.1.call-start = ((), (), s32[]{:S(2)}) async-start(), calls=%async_computation.5 | async-start | bytes 4194304 | tf_op jit(solution)/shard_map/psum | solution.py:309
  277.5 38.4 %copy-start.4 = (f32[12288]{0:T(1024)}, f32[12288]{0:T(1024)S(1)}, u32[]{:S(2)}) copy-start(f32[12288]{0:T(1024)S(1)} %rsqrt.12) | copy-start | bytes 147460
  286.2 29.7 %copy-start.9 = (bf16[1024,256]{1,0:T(8,128)(2,1)S(1)}, bf16[1024,256]{1,0:T(8,128)(2,1)}, u32[]{:S(2)}) copy-start(bf16[1024,256]{1,0:T(8,128)(2,1)} %param.22) | copy-start | bytes 1572868
  349.2 14.3 %copy-start.8 = (bf16[3,64,64,256]{3,2,1,0:T(8,128)(2,1)S(1)}, bf16[3,64,64,256]{3,2,1,0:T(8,128)(2,1)}, u32[]{:S(2)}) copy-start(bf16[3,64,64,256]{3,2,1,0:T(8,128)(2,1)} %param.23) | copy-start | bytes 18874372
  363.5 12.7 %copy-start.5 = (f32[12288]{0:T(1024)S(1)}, f32[12288]{0:T(1024)}, u32[]{:S(2)}) copy-start(f32[12288]{0:T(1024)} %copy-done.4) | copy-start | bytes 147460
  363.5 12.7 %copy-start.7 = (f32[256]{0:T(256)S(1)}, f32[256]{0:T(256)}, u32[]{:S(2)}) copy-start(f32[256]{0:T(256)} %copy-done.6) | copy-start | bytes 3076
  531.8 4.4 collective-permute-start.4
  536.2 4.4 collective-permute-start.5
  540.6 5.3 collective-permute-start.6
  546.0 1.3 collective-permute-start.7
  547.3 4.4 collective-permute-start.8
Sparse Core Ops, SparseCore 0:
  39.5 62.6 all-gather.2
  395.4 136.3 all-reduce.3

commit v7 on v6

--- a/solution.py
+++ b/solution.py
@@ -315,9 +315,7 @@
     stencil_grad = stencil_backward(offsets, extended, aggregated_grad)
     tap_count = stencil_grad.shape[0]
     small_grads = jnp.concatenate([stencil_grad, gain_grad[None, :]], axis=0)
-    small_grads, w_in_grad, w_out_grad, increment = lax.optimization_barrier(
-        (small_grads, w_in_grad, w_out_grad, increment)
-    )
+    small_grads, increment = lax.optimization_barrier((small_grads, increment))
     small_grads = butterfly_sum(small_grads, ("face", "row", "col"))
     stencil_grad = small_grads[:tap_count]
     gain_grad = small_grads[tap_count]

time: 573 us -> 555 us (0.969)
  waiting for transfers between devices: 54.4 us -> 33.5 us
    psum x1, waiting for transfers between devices: 23.8 us -> 0.01 us  [shards(): lax.psum((w_in_grad, w_out_grad), ('face', 'row', 'col'))]
  transfers between devices with their start and end apart: 15 -> 15, of which waited for: 9 -> 8; matrix products, arithmetic and copies ran while one was open for 15% -> 16% of each run, Pallas kernels for 14% -> 15%
where the time goes in v7:
time: 555 us; the launch traced here: 548 us
  Pallas kernels  176 us (32%)
  matrix products  124 us (22%)
  between operations  68.4 us (12%)
  other arithmetic  62.5 us (11%)
  local copies, waits for them, and re-layouts  49 us (9%)
  starting transfers between devices  34.3 us (6%)
  waiting for transfers between devices  33.5 us (6%)
    pallas_call x1, Pallas kernels, stencil_forward(): pl.pallas_call(_fwd_kernel, grid=(faces,), in_specs=[pl.BlockSpec((1, ext...  94.5 us
    pallas_call x1, Pallas kernels, stencil_backward(): pl.pallas_call(_bwd_kernel, grid_spec=pltpu.PrefetchScalarGridSpec(num_sc...  81.7 us
    dot_general x1, matrix products, shards(): lax.dot_general(target_rows, w_out, contract_cols, preferred_element_type...  33.3 us
    dot_general x1, matrix products, shards(): pre_act = jnp.dot(hidden_in, w_in, preferred_element_type=jnp.float32)  29.7 us
    dot_general x1, matrix products, shards(): lax.dot_general(pre_grad, w_in, contract_cols, preferred_element_type=jnp...  19 us
    mul x1, other arithmetic, shards(): inverse_rms * (scaled_grad - normalized * jnp.mean(scaled_grad * normaliz...  16.5 us
    ppermute x5, waiting for transfers between devices, butterfly_sum(): lax.ppermute(value, axis, [(i, i ^ step) for i in range(count)])  15.9 us
    unnamed x26, local copies, waits for them, and re-layouts  15.4 us
  transfers between devices with their start and end apart: 15, of which 8 were waited for; matrix products, arithmetic and copies ran while one was open for 16% of the time, Pallas kernels for 15%

profile of v7, /device:TPU:0, one launch (start us, length us, event | category | flops | bytes accessed | tf_op | source)
XLA Modules:
  0.0 547.5 jit_solution(17703519227480003892)
XLA Ops:
  9.9 4.2 all-to-all-start.1
  17.1 4.5 all-to-all-done.1
  21.5 5.5 %all-to-all-start = ((bf16[3,4,4,16,256]{4,3,1,0,2:T(8,128)(2,1)}), bf16[3,4,4,16,256]{4,3,1,0,2:T(8,128)(2,1)S(1)}, u32[]{:S(2)}, u32[]{:S(2)}) async-start(bf16[3,4,4,16,256]{4,3,1,0,2:T(8,128)(2,1)} %copy.54), calls=%async_computation | async-start | bytes 786432 | tf_op jit(solution)/shard_map/all_to_all | solution.py:178
  27.1 11.5 %all-to-all-done = bf16[3,4,4,16,256]{4,3,1,0,2:T(8,128)(2,1)S(1)} async-done(((bf16[3,4,4,16,256]{4,3,1,0,2:T(8,128)(2,1)}), bf16[3,4,4,16,256]{4,3,1,0,2:T(8,128)(2,1)S(1)}, u32[]{:S(2)}, u32[]{:S(2)}) %all-to-all-start) | async-done | bytes 393248 | tf_op jit(solution)/shard_map/all_to_all | solution.py:178
  102.5 3.4 constant_dynamic-update-slice_fusion.1
  105.9 2.9 copy-done.2
  113.4 3.6 copy.58
  118.7 2.6 fusion.3
  121.4 2.8 copy-done.1
  130.2 3.6 all-to-all-start.3
  135.1 2.5 rev.54
  140.2 2.5 rev.56
  142.7 2.5 rev.57
  150.2 3.6 all-to-all-start.2
  154.0 8.8 %pad_maximum_fusion = bf16[3,72,72,256]{3,2,1,0:T(8,128)(2,1)} fusion(bf16[3,72,4,256]{3,2,1,0:T(4,128)(2,1)} %collective-permute-done.3, bf16[3,72,64,256]{3,2,1,0:T(8,128)(2,1)} %copy-done.2, bf16[3,72,4,256]{3,2,1,0:T(4,128)(2,1)} %collective-permute-done.2), kind=kLoop, calls=%fused_computation.15 | loop fusion | flops 23887872 | bytes 15925248 | tf_op jit(solution)/shard_map/concatenate | solution.py:135
  175.7 94.5 %shard_map.119 = f32[3,64,64,256]{3,2,1,0:T(8,128)} custom-call(bf16[3,72,72,256]{3,2,1,0:T(8,128)(2,1)} %fusion.4.ext_ref, f32[81,256]{1,0:T(8,128)S(1)} %fusion.8.w_ref), custom_call_target="tpu_custom_call" | custom-call | tf_op jit(solution)/shard_map/pallas_call | solution.py:47
  270.2 6.3 %multiply_reduce_fusion.2 = f32[3,64,64]{2,1,0:T(8,128)S(1)} fusion(f32[3,64,64,256]{3,2,1,0:T(8,128)} %shard_map.119), kind=kLoop, calls=%fused_computation.12 | loop fusion | flops 6279168 | bytes 12632064 | tf_op jit(solution)/shard_map/reduce_sum | solution.py:284
  276.6 8.6 %multiply_convert_fusion.2 = bf16[12288,256]{1,0:T(8,128)(2,1)} fusion(f32[3,64,64,256]{3,2,1,0:T(8,128)} %shard_map.119, f32[256]{0:T(256)S(1)} %convert_element_type.12, f32[12288]{0:T(1024)S(1)} %rsqrt.12), kind=kLoop, calls=%fused_computation.11 | loop fusion | flops 9437184 | bytes 18924544 | tf_op jit(solution)/shard_map/convert_element_type | solution.py:288
  285.3 29.7 %multiply_convert_fusion = (bf16[12288,1024]{1,0:T(8,128)(2,1)}, f32[12288,1024]{1,0:T(8,128)}) fusion(bf16[12288,256]{1,0:T(8,128)(2,1)} %multiply_convert_fusion.2, bf16[256,1024]{1,0:T(8,128)(2,1)S(1)} %copy-done), kind=kOutput, calls=%fused_computation | convolution fusion | flops 6505365504 | bytes 82313216 | tf_op jit(solution)/shard_map/dot_general | solution.py:289
  315.0 33.3 %multiply_convert_fusion.1 = bf16[12288,1024]{1,0:T(8,128)(2,1)} fusion(f32[12288,1024]{1,0:T(8,128)} %get-tuple-element.134, bf16[12288,256]{1,0:T(8,128)(2,1)} %bitcast.177, bf16[1024,256]{1,0:T(8,128)(2,1)S(1)} %copy-done.9), kind=kOutput, calls=%fused_computation.1 | convolution fusion | flops 6555697152 | bytes 82313216 | tf_op jit(solution)/shard_map/dot_general | solution.py:299
  348.3 14.3 %fusion.14 = f32[256,1024]{1,0:T(8,128)} fusion(bf16[12288,256]{1,0:T(8,128)(2,1)} %multiply_convert_fusion.2, bf16[12288,1024]{1,0:T(8,128)(2,1)} %multiply_convert_fusion.1), kind=kOutput, calls=%fused_computation.106 | convolution fusion | flops 6442450944 | bytes 32505856 | tf_op jit(solution)/shard_map/dot_general | solution.py:303
  362.6 12.7 %fusion.15 = f32[1024,256]{1,0:T(8,128)} fusion(bf16[12288,1024]{1,0:T(8,128)(2,1)} %get-tuple-element.133, bf16[12288,256]{1,0:T(8,128)(2,1)S(1)} %bitcast.178), kind=kOutput, calls=%fused_computation.107 | convolution fusion | flops 6442450944 | bytes 32505856 | tf_op jit(solution)/shard_map/dot_general | solution.py:296
  375.3 19.0 %multiply_reduce_fusion.1 = (f32[12288]{0:T(1024)S(1)}, f32[256]{0:T(256)S(1)}, f32[12288,256]{1,0:T(8,128)}) fusion(f32[3,64,64,256]{3,2,1,0:T(8,128)} %shard_map.119, f32[256]{0:T(256)S(1)} %copy-done.7, f32[12288]{0:T(1024)S(1)} %copy-done.5, bf16[12288,1024]{1,0:T(8,128)(2,1)} %multiply_convert_fusion.1, bf16[256,1024]{1,0:T(8,128)(2,1)S(1)} %copy-done), kind=kOutput, calls=%fused_computation.10 | convolution fusion | flops 6461313024 | bytes 50956288 | tf_op jit(solution)/shard_map/dot_general | solution.py:307
  394.4 16.5 %subtract_multiply_fusion = f32[12288,256]{1,0:T(8,128)} fusion(f32[12288,256]{1,0:T(8,128)} %get-tuple-element.135, f32[3,64,64,256]{3,2,1,0:T(8,128)} %shard_map.119, f32[12288]{0:T(1024)S(1)} %broadcast_multiply_fusion, f32[256]{0:T(256)S(1)} %copy-done.7, f32[12288]{0:T(1024)S(1)} %copy-done.5), kind=kLoop, calls=%fused_computation.9 | loop fusion | flops 15728640 | bytes 37848064 | tf_op jit(solution)/shard_map/mul | solution.py:311
  410.9 13.5 %convolution_convert_fusion = bf16[12288,256]{1,0:T(8,128)(2,1)} fusion(bf16[12288,1024]{1,0:T(8,128)(2,1)} %get-tuple-element.133, bf16[1024,256]{1,0:T(8,128)(2,1)S(1)} %copy-done.9), kind=kOutput, calls=%fused_computation.5 | convolution fusion | flops 6445596672 | bytes 31981568 | tf_op jit(solution)/shard_map/dot_general | solution.py:292
  424.4 81.7 %shard_map.120 = f32[64,8,256]{2,1,0:T(8,128)} custom-call(s32[128]{0:T(128)} %reshape.412.off_ref, bf16[3,72,72,256]{3,2,1,0:T(8,128)(2,1)} %fusion.4.ext_ref, f32[3,64,64,256]{3,2,1,0:T(8,128)} %bitcast.165), custom_call_target="tpu_custom_call" | custom-call | tf_op jit(solution)/shard_map/pallas_call | solution.py:109
  507.8 4.7 collective-permute-done.4
  512.5 5.8 %collective-permute-start.5 = (f32[65,256]{1,0:T(8,128)S(1)}, f32[65,256]{1,0:T(8,128)S(1)}, u32[]{:S(2)}, u32[]{:S(2)}) collective-permute-start(f32[65,256]{1,0:T(8,128)S(1)} %add.312), channel_id=1, source_target_pairs={{0,4},{4,0},{8,12},{12,8},{1,5},{5,1},{9,13},{13,9},{2,6},{6,2},{1... | collective-permute-start | bytes 199688 | tf_op jit(solution)/shard_map/ppermute | solution.py:333
  518.3 2.9 collective-permute-done.5
  521.2 2.9 collective-permute-start.6
  524.1 4.4 collective-permute-done.6
  531.9 2.6 collective-permute-done.8
  (108 shorter events, 61.2 us)
Async XLA Ops:
  7.2 278.1 %copy-start = (bf16[256,1024]{1,0:T(8,128)(2,1)S(1)}, bf16[256,1024]{1,0:T(8,128)(2,1)}, u32[]{:S(2)}) copy-start(bf16[256,1024]{1,0:T(8,128)(2,1)} %param.21) | copy-start | bytes 1572868
  9.9 11.7 %all-to-all-start.1 = ((bf16[3,4,4,16,256]{4,3,1,0,2:T(8,128)(2,1)}), bf16[3,4,4,16,256]{4,3,1,0,2:T(8,128)(2,1)S(1)}, u32[]{:S(2)}, u32[]{:S(2)}) async-start(bf16[3,4,4,16,256]{4,3,1,0,2:T(8,128)(2,1)} %copy.57), calls=%async_computation.1 | async-start | bytes 786432 | tf_op jit(solution)/shard_map/all_to_all | solution.py:185
  21.5 17.0 %all-to-all-start = ((bf16[3,4,4,16,256]{4,3,1,0,2:T(8,128)(2,1)}), bf16[3,4,4,16,256]{4,3,1,0,2:T(8,128)(2,1)S(1)}, u32[]{:S(2)}, u32[]{:S(2)}) async-start(bf16[3,4,4,16,256]{4,3,1,0,2:T(8,128)(2,1)} %copy.54), calls=%async_computation | async-start | bytes 786432 | tf_op jit(solution)/shard_map/all_to_all | solution.py:178
  27.1 86.3 %all-gather.3.cloned.1.call-start = ((), (), s32[]{:S(2)}) async-start(), calls=%async_computation.4 | async-start | bytes 6684672 | tf_op jit(solution)/shard_map/all_gather | solution.py:195
  39.4 63.1 %collective-permute-start = (bf16[3,4,64,256]{3,2,1,0:T(8,128)(2,1)S(1)}, bf16[3,4,64,256]{3,2,1,0:T(8,128)(2,1)S(1)}, u32[]{:S(2)}, u32[]{:S(2)}) collective-permute-start(bf16[3,4,64,256]{3,2,1,0:T(8,128)(2,1)S(1)} %slice.346), channel_id=1, source_target_pairs={{0,4},{4,8},{8,12},{1,5},{5,9},{9,13},{2,6},{6,10},{10,14},{3,7},{... | collective-permute-start | bytes 1179656 | tf_op jit(solution)/shard_map/ppermute | solution.py:137
  40.9 65.0 %collective-permute-start.1 = (bf16[3,4,64,256]{3,2,1,0:T(8,128)(2,1)S(1)}, bf16[3,4,64,256]{3,2,1,0:T(8,128)(2,1)S(1)}, u32[]{:S(2)}, u32[]{:S(2)}) collective-permute-start(bf16[3,4,64,256]{3,2,1,0:T(8,128)(2,1)S(1)} %get-tuple-element.84), channel_id=1, source_target_pairs={{4,0},{8,4},{12,8},{5,1},{9,5},{13,9},{6,2},{10,6},{14,10},{7,3},{... | collective-permute-start | bytes 1179656 | tf_op jit(solution)/shard_map/ppermute | solution.py:139
  91.8 184.8 %copy-start.6 = (f32[256]{0:T(256)}, f32[256]{0:T(256)S(1)}, u32[]{:S(2)}) copy-start(f32[256]{0:T(256)S(1)} %convert_element_type.12) | copy-start | bytes 3076
  105.9 2.9 copy-start.2
  110.0 43.9 %collective-permute-start.2 = (bf16[3,72,4,256]{3,2,1,0:T(4,128)(2,1)}, bf16[3,72,4,256]{3,2,1,0:T(4,128)(2,1)}, u32[]{:S(2)}, u32[]{:S(2)}) collective-permute-start(bf16[3,72,4,256]{3,2,1,0:T(4,128)(2,1)} %get-tuple-element.67), channel_id=1, source_target_pairs={{0,1},{1,2},{2,3},{4,5},{5,6},{6,7},{8,9},{9,10},{10,11},{12,13},{... | collective-permute-start | bytes 1327112 | tf_op jit(solution)/shard_map/ppermute | solution.py:137
  112.1 41.9 %collective-permute-start.3 = (bf16[3,72,4,256]{3,2,1,0:T(4,128)(2,1)}, bf16[3,72,4,256]{3,2,1,0:T(4,128)(2,1)}, u32[]{:S(2)}, u32[]{:S(2)}) collective-permute-start(bf16[3,72,4,256]{3,2,1,0:T(4,128)(2,1)} %get-tuple-element.68), channel_id=1, source_target_pairs={{1,0},{2,1},{3,2},{5,4},{6,5},{7,6},{9,8},{10,9},{11,10},{13,12},{... | collective-permute-start | bytes 1327112 | tf_op jit(solution)/shard_map/ppermute | solution.py:139
  121.4 2.8 copy-start.1
  130.2 20.0 %all-to-all-start.3 = ((bf16[6,4,72,256]{3,2,1,0:T(8,128)(2,1)}), bf16[6,4,72,256]{3,2,1,0:T(8,128)(2,1)S(1)}, u32[]{:S(2)}, u32[]{:S(2)}) async-start(bf16[6,4,72,256]{3,2,1,0:T(8,128)(2,1)} %bitcast_dynamic-update-slice_fusion), calls=%async_computation.3 | async-start | bytes 1769472 | tf_op jit(solution)/shard_map/all_to_all | solution.py:257
  149.3 0.9 copy-start.3
  150.2 16.6 %all-to-all-start.2 = ((bf16[6,4,72,256]{3,2,1,0:T(8,128)(2,1)}), bf16[6,4,72,256]{3,2,1,0:T(8,128)(2,1)S(1)}, u32[]{:S(2)}, u32[]{:S(2)}) async-start(bf16[6,4,72,256]{3,2,1,0:T(8,128)(2,1)} %copy-done.3), calls=%async_computation.2 | async-start | bytes 1769472 | tf_op jit(solution)/shard_map/all_to_all | solution.py:256
  153.7 381.9 %all-reduce.4.cloned.1.call-start = ((), (), s32[]{:S(2)}) async-start(), calls=%async_computation.5 | async-start | bytes 4194304 | tf_op jit(solution)/shard_map/psum | solution.py:309
  276.6 38.4 %copy-start.4 = (f32[12288]{0:T(1024)}, f32[12288]{0:T(1024)S(1)}, u32[]{:S(2)}) copy-start(f32[12288]{0:T(1024)S(1)} %rsqrt.12) | copy-start | bytes 147460
  285.2 29.7 %copy-start.9 = (bf16[1024,256]{1,0:T(8,128)(2,1)S(1)}, bf16[1024,256]{1,0:T(8,128)(2,1)}, u32[]{:S(2)}) copy-start(bf16[1024,256]{1,0:T(8,128)(2,1)} %param.22) | copy-start | bytes 1572868
  348.3 14.3 %copy-start.8 = (bf16[3,64,64,256]{3,2,1,0:T(8,128)(2,1)S(1)}, bf16[3,64,64,256]{3,2,1,0:T(8,128)(2,1)}, u32[]{:S(2)}) copy-start(bf16[3,64,64,256]{3,2,1,0:T(8,128)(2,1)} %param.23) | copy-start | bytes 18874372
  362.6 12.7 %copy-start.5 = (f32[12288]{0:T(1024)S(1)}, f32[12288]{0:T(1024)}, u32[]{:S(2)}) copy-start(f32[12288]{0:T(1024)} %copy-done.4) | copy-start | bytes 147460
  362.6 12.7 %copy-start.7 = (f32[256]{0:T(256)S(1)}, f32[256]{0:T(256)}, u32[]{:S(2)}) copy-start(f32[256]{0:T(256)} %copy-done.6) | copy-start | bytes 3076
  507.3 5.2 collective-permute-start.4
  512.5 8.7 %collective-permute-start.5 = (f32[65,256]{1,0:T(8,128)S(1)}, f32[65,256]{1,0:T(8,128)S(1)}, u32[]{:S(2)}, u32[]{:S(2)}) collective-permute-start(f32[65,256]{1,0:T(8,128)S(1)} %add.312), channel_id=1, source_target_pairs={{0,4},{4,0},{8,12},{12,8},{1,5},{5,1},{9,13},{13,9},{2,6},{6,2},{1... | collective-permute-start | bytes 199688 | tf_op jit(solution)/shard_map/ppermute | solution.py:333
  521.2 7.3 %collective-permute-start.6 = (f32[65,256]{1,0:T(8,128)S(1)}, f32[65,256]{1,0:T(8,128)S(1)}, u32[]{:S(2)}, u32[]{:S(2)}) collective-permute-start(f32[65,256]{1,0:T(8,128)S(1)} %add.313), channel_id=1, source_target_pairs={{0,8},{4,12},{8,0},{12,4},{1,9},{5,13},{9,1},{13,5},{2,10},{6,14},... | collective-permute-start | bytes 199688 | tf_op jit(solution)/shard_map/ppermute | solution.py:333
  528.6 1.3 collective-permute-start.7
  529.9 4.6 collective-permute-start.8
Sparse Core Ops, SparseCore 0:
  39.5 62.6 all-gather.2
  394.5 139.7 all-reduce.3
